TPU v7x, 128 devices: a whole 4x4x4 slice. The times are simulated.
128 devices in a mesh: page: 8 (over z, core), tensor: 16 (over x, y).
Axes of the slice: x: 4, y: 4, z: 4, core: 2. Of those that a mesh axis runs over, the one named last changes fastest.
Arguments:
- hidden_in: bfloat16 [1, 32, 8192], P(None, 'tensor', 'page'), may hold values from -6 to 6
- w_query: bfloat16 [8192, 8192], P('page', 'tensor'), may hold values from -0.0625 to 0.0625
- w_keyval: bfloat16 [8192, 2048], P('page', 'tensor'), may hold values from -0.0625 to 0.0625
- w_output: bfloat16 [8192, 8192], P('tensor', 'page'), may hold values from -0.0625 to 0.0625
- kv_pool: bfloat16 [8192, 64, 2048], P(('page', 'tensor'))
- page_table: int32 [8192], replicated, may hold values from 0 to 8191, each once
- selected: int32 [1, 32, 8, 32], replicated, may hold values from 0 to 255, as said below
Outputs:
- attn_out: bfloat16 [1, 32, 8192], P(None, 'tensor', 'page')
- new_kv: bfloat16 [1, 32, 2048], P(None, 'page', 'tensor')
Inputs may be any that keep to these rules, and one draw needn't show every extreme that they name: `page_table`: each pool slot holds exactly one page: entry s * 256 + l is the slot of page l of sequence s. `selected`: the 32 pages of one row are different.
All inputs are finite; a program needn't handle non-finite values.
Results may differ from a plain program's by a relative error of at most 0.018.
The roundings to bfloat16 on the way count: a program that leaves them out, or rounds other values in their place, can miss the bound.
Values may be sent and summed in bfloat16 or wider, within the bound.
No kernel may reach another device: no remote copies, remote signals or barrier semaphores. Data moves between devices by JAX's collectives and lax.ppermute only.
A program may use at most 192 MiB of HBM per device.

v0:
```python
import math

import jax
import jax.numpy as jnp
from jax import lax
from jax.sharding import PartitionSpec as P

H = 64
KVH = 8
HD = 128
PAGE_TOK = 64
PAGES = 256


NEG_BIG = -1e30


def frequencies(head_dim):
    half_dim = head_dim // 2
    index = jnp.arange(half_dim, dtype=jnp.float32)
    base_freq = jnp.exp(-(2.0 * index / head_dim) * math.log(500000.0))
    wavelen = 2.0 * math.pi / base_freq
    smooth = (8192.0 / wavelen - 1.0) / 3.0
    middle = (1.0 - smooth) * base_freq / 8.0 + smooth * base_freq
    scaled = jnp.where(wavelen > 8192.0, base_freq / 8.0, base_freq)
    is_middle = jnp.logical_and(wavelen >= 2048.0, wavelen <= 8192.0)
    return jnp.where(is_middle, middle, scaled)


def rotate(vectors, position):
    half_dim = vectors.shape[-1] // 2
    angles = position * frequencies(vectors.shape[-1])
    cosine = jnp.cos(angles)
    sine_v = jnp.sin(angles)
    first_half = vectors[..., :half_dim]
    second_half = vectors[..., half_dim:]
    return jnp.concatenate(
        [first_half * cosine - second_half * sine_v, first_half * sine_v + second_half * cosine],
        axis=-1,
    )


def finish(summed, position, query_cols, kind_ids):
    n_rows = summed.shape[0]
    query = rotate(summed[:, :query_cols].reshape(n_rows, query_cols // HD, HD), position)
    query = query.reshape(n_rows, query_cols).astype(jnp.bfloat16)
    keyval = summed[:, query_cols:].reshape(n_rows, -1, HD)
    rotated = rotate(keyval, position)
    keyval = jnp.where(kind_ids[None, :, None] == 0, rotated, keyval)
    return (query, keyval.reshape(n_rows, -1).astype(jnp.bfloat16))


def per_device(hidden_in, w_query, w_keyval, w_output, kv_pool, page_table, selected):
    n_page = lax.axis_size("page")
    n_tensor = lax.axis_size("tensor")
    my_page = lax.axis_index("page")
    my_tensor = lax.axis_index("tensor")
    seqs = selected.shape[1]
    groups = H // KVH
    local_heads = H // n_tensor
    scale = 1.0 / math.sqrt(HD)
    slots = kv_pool.shape[0]
    pool_size = page_table.shape[0]
    device = my_page * n_tensor + my_tensor
    logical = (
        jnp.zeros((pool_size,), jnp.int32)
        .at[page_table]
        .set(jnp.arange(pool_size, dtype=jnp.int32))
    )
    my_logical = lax.dynamic_slice_in_dim(logical, device * slots, slots)
    seq_of = my_logical // PAGES
    page_of = my_logical % PAGES
    owner_rows = jnp.arange(seqs, dtype=jnp.int32)[:, None] == seq_of[None, :]
    owner_hot = owner_rows.astype(jnp.float32)
    w_joined = jnp.concatenate([w_query, w_keyval], axis=1)
    query_cols = w_query.shape[1]
    sub_heads = w_keyval.shape[1] // HD
    kind_ids = (my_tensor * sub_heads + jnp.arange(sub_heads, dtype=jnp.int32)) % 2
    pool_five = kv_pool.reshape(slots, PAGE_TOK, KVH, 2, HD)
    key_rows = pool_five[:, :, :, 0]
    val_rows = pool_five[:, :, :, 1]
    seq_share = seqs // n_page
    position = float(PAGES * PAGE_TOK)
    tok_rows = hidden_in[0]
    partial_value = jnp.dot(
        lax.all_gather(tok_rows, "tensor", axis=0, tiled=True),
        w_joined,
        preferred_element_type=jnp.float32,
    )
    summed = lax.psum(partial_value, "page")
    query, new_local = finish(summed, position, query_cols, kind_ids)
    new_rows = [lax.dynamic_slice_in_dim(new_local, my_page * seq_share, seq_share, 0)]
    query_full = lax.all_gather(query, "tensor", axis=1, tiled=True)
    sel_rows = selected[0][seq_of]
    picked = jnp.any(sel_rows == page_of[:, None, None], axis=2)
    slot_query = query_full[seq_of].reshape(slots, KVH, groups, HD)
    scores = (
        jnp.einsum("sghd,stgd->sght", slot_query, key_rows, preferred_element_type=jnp.float32)
        * scale
    )
    page_max = jnp.max(scores, axis=-1)
    weights = jnp.exp(scores - page_max[..., None]).astype(jnp.bfloat16)
    pick_mask = picked.astype(jnp.float32)[:, :, None]
    page_total = jnp.sum(weights.astype(jnp.float32), axis=-1) * pick_mask
    weighted = (
        jnp.einsum("sght,stgd->sghd", weights, val_rows, preferred_element_type=jnp.float32)
        * pick_mask[..., None]
    )
    page_max = jnp.where(picked[:, :, None], page_max, NEG_BIG)
    seq_max = jnp.max(jnp.where(owner_rows[:, :, None, None], page_max[None], NEG_BIG), axis=1)
    factor = jnp.exp(page_max - seq_max[seq_of])
    seq_total = jnp.dot(
        owner_hot, (page_total * factor).reshape(slots, H), precision=lax.Precision.HIGHEST
    )
    seq_acc = jnp.dot(
        owner_hot,
        (weighted * factor[..., None]).reshape(slots, H * HD),
        precision=lax.Precision.HIGHEST,
    ).reshape(seqs, H, HD)
    seq_max = seq_max.reshape(seqs, H)
    top_max = lax.pmax(seq_max, ("page", "tensor"))
    rescale = jnp.exp(seq_max - top_max)
    full_total, full_acc = lax.psum(
        (seq_total * rescale, seq_acc * rescale[..., None]), ("page", "tensor")
    )
    head_start = my_tensor * local_heads
    mine_total = lax.dynamic_slice_in_dim(full_total, head_start, local_heads, 1)
    mine_acc = lax.dynamic_slice_in_dim(full_acc, head_start, local_heads, 1)
    heads = (mine_acc / mine_total[..., None]).astype(jnp.bfloat16).reshape(seqs, local_heads * HD)
    outputs = [
        lax.psum_scatter(
            jnp.dot(heads, w_output, preferred_element_type=jnp.float32),
            "tensor",
            scatter_dimension=0,
            tiled=True,
        ).astype(jnp.bfloat16)
    ]
    return (jnp.stack(outputs), jnp.stack(new_rows))


def solution(mesh):
    return jax.shard_map(
        per_device,
        mesh=mesh,
        in_specs=(
            P(None, "tensor", "page"),
            P("page", "tensor"),
            P("page", "tensor"),
            P("tensor", "page"),
            P(("page", "tensor"), None, None),
            P(),
            P(),
        ),
        out_specs=(P(None, "tensor", "page"), P(None, "page", "tensor")),
        check_vma=False,
    )
```

profile of v0, /device:TPU:0, one launch (start us, length us, event | category | flops | bytes accessed | tf_op | source)
XLA Modules:
  0.0 482.4 jit_solution(10256855988019674995)
XLA Ops:
  7.2 0.0 copy-start
  7.2 0.0 copy-start.4
  7.2 0.0 all-reduce.5.cloned.1.call-start
  7.2 0.8 copy.29
  8.0 24.1 %all-gather = bf16[1,32,1024]{2,0,1:T(2,128)(2,1)S(1)} all-gather(bf16[1,2,1024]{2,0,1:T(2,128)(2,1)S(1)} %copy.29), channel_id=2, replica_groups=mesh['page'=8,'tensor'=16] {'tensor'}, dimensions={1}, use_global_device_ids=true | all-gather | bytes 69632 | tf_op jit(solution)/shard_map/all_gather | solution.py:86
  32.1 2.3 fusion.12
  34.4 0.0 all-reduce.5.cloned.1.call-update
  34.4 0.0 all-reduce.7.cloned.1.call-start
  34.5 0.0 copy-done.4
  34.5 30.5 %scatter_custom_fusion = s32[8192]{0:T(1024)S(1)} fusion(s32[8192]{0:T(1024)S(1)} %compare_select_fusion, s32[8192]{0:T(1024)S(1)} %iota.30, s32[]{:T(128)} %constant.80.clone.1), kind=kCustom, calls=%fused_computation.46 | custom fusion | bytes 32772 | tf_op jit(solution)/shard_map/scatter | solution.py:68
  65.0 0.1 and_select_fusion
  65.1 0.1 compare_select_fusion.1
  65.2 0.0 copy-start.5
  65.2 27.4 %reshape.97 = bf16[64,64,8,2,128]{4,3,2,1,0:T(2,128)(2,1)} reshape(bf16[64,64,2048]{2,1,0:T(8,128)(2,1)} %param.11) | data formatting | bytes 33554432 | tf_op jit(solution)/shard_map/reshape | solution.py:79
  92.6 33.7 %fusion.37 = (bf16[64,64,8,1,128]{4,3,2,1,0:T(2,128)(2,1)}, bf16[64,64,8,1,128]{4,3,2,1,0:T(2,128)(2,1)}) fusion(bf16[64,64,8,2,128]{4,3,2,1,0:T(2,128)(2,1)} %reshape.97), kind=kLoop, calls=%fused_computation.74 | loop fusion | bytes 33554432 | tf_op jit(solution)/shard_map/slice | solution.py:81
  126.2 0.0 copy-done.1
  126.3 0.6 gather_fusion.1
  126.9 1.3 compare_reduce_fusion
  128.1 0.1 fusion.33
  128.2 0.0 copy-start.6
  128.2 0.0 copy-start.8
  128.3 0.6 convert_element_type.33
  128.9 0.0 copy-done.10
  128.9 0.6 dynamic-slice
  130.1 0.0 all-reduce.5.cloned.1.call-done
  130.1 0.8 slice.38
  131.0 0.1 subtract_convert_fusion
  131.1 0.1 pad_maximum_fusion
  131.2 23.4 %all_gather.7 = bf16[32,8192]{1,0:T(8,128)(2,1)S(1)} all-gather(bf16[32,512]{1,0:T(8,128)(2,1)S(1)} %bitcast.76), channel_id=1, replica_groups=mesh['page'=8,'tensor'=16] {'tensor'}, dimensions={1}, use_global_device_ids=true | all-gather | bytes 557056 | tf_op jit(solution)/shard_map/all_gather | solution.py:93
  154.6 0.0 copy-done.5
  154.6 1.2 gather_fusion
  155.8 0.0 copy-done.6
  155.8 0.0 copy-done.8
  155.9 0.3 copy.43
  156.1 10.3 %multiply_reduce_fusion = (f32[64,8,8]{2,1,0:T(8,128)S(1)}, f32[64,8,8,64]{3,2,1,0:T(8,128)S(1)}) fusion(bf16[64,8,8,128]{3,2,1,0:T(8,128)(2,1)S(1)} %bitcast.70, bf16[64,64,8,1,128]{4,3,2,1,0:T(2,128)(2,1)} %get-tuple-element.9), kind=kOutput, calls=%fused_computation.15 | convolution fusion | flops 67629056 | bytes 10502144 | tf_op jit(solution)/shard_map/sghd,stgd->sght/dot_general | solution.py:98
  166.4 0.8 broadcast_select_fusion
  167.3 1.7 copy.32
  168.9 1.1 select_reduce_fusion
  170.0 0.7 copy.34
  170.8 1.4 gather_fusion.2
  172.2 2.0 convert_reduce_fusion
  174.2 0.0 copy-done.2
  174.2 64.2 %pmax.7 = f32[32,64]{0,1:T(8,128)S(1)} all-reduce(f32[32,64]{0,1:T(8,128)S(1)} %bitcast.74), channel_id=1, replica_groups=mesh['page'=8,'tensor'=16] {'page','tensor'}, use_global_device_ids=true, to_apply=%region_5.6 | all-reduce | flops 2048 | bytes 16384 | tf_op jit(solution)/shard_map/pmax | solution.py:121
  238.4 0.0 copy-done.3
  238.4 2.0 multiply_multiply_fusion.1
  240.4 1.1 copy.35
  241.5 9.7 %multiply_multiply_fusion = f32[64,8,8,128]{3,2,1,0:T(8,128)S(1)} fusion(bf16[64,64,8,1,128]{4,3,2,1,0:T(2,128)(2,1)} %get-tuple-element.8, f32[64,8,8]{2,1,0:T(8,128)} %get-tuple-element.3, f32[64,8]{1,0:T(8,128)S(1)} %copy-done.3, f32[64,8,8,64]{3,2,1,0:T(8,128)S(1)} %get-tuple-element.15, f32[64,8,8]{2,1,0:T(8,128)S(1)} %get-tuple-element.14), kind=kOutput, calls=%fused_computation.13 | convolution fusion | flops 68943872 | bytes 11569152 | tf_op jit(solution)/shard_map/sght,stgd->sghd/dot_general | solution.py:106
  251.2 0.1 convolution_multiply_fusion
  251.4 0.0 copy-start.7
  251.4 0.0 copy-start.9
  251.4 3.2 fusion.5
  254.6 0.0 all-reduce.7.cloned.1.call-update
  254.6 0.7 slice_bitcast_fusion
  255.3 0.7 slice.43
  256.0 65.0 %psum.23 = f32[32,64]{0,1:T(8,128)S(1)} all-reduce(f32[32,64]{0,1:T(8,128)S(1)} %convolution_multiply_fusion), channel_id=1, replica_groups=mesh['page'=8,'tensor'=16] {'page','tensor'}, use_global_device_ids=true, to_apply=%region_8.9 | all-reduce | flops 2048 | bytes 16384 | tf_op jit(solution)/shard_map/psum | solution.py:123
  321.0 0.0 copy-done.7
  321.0 0.0 copy-done.9
  321.1 0.1 subtract_bitcast_fusion
  321.1 0.6 fusion.31
  321.8 78.1 %all-reduce.7.cloned.1.call-done = f32[32,64,128]{2,0,1:T(8,128)} async-done(((f32[32,64,128]{2,0,1:T(8,128)}), f32[32,64,128]{2,0,1:T(8,128)}) %all-reduce.7.cloned.1.call-update) | async-done | bytes 1048592 | tf_op jit(solution)/shard_map/psum | solution.py:123
  399.9 0.0 copy-done
  399.9 1.2 fusion.17
  401.0 73.9 %all-reduce.8 = bf16[32,1024]{1,0:T(8,128)(2,1)S(1)} all-reduce(f32[32,1024]{1,0:T(8,128)S(1)} %fusion.17), channel_id=3, replica_groups=mesh['page'=8,'tensor'=16] {'tensor'}, use_global_device_ids=true, to_apply=%region_9.10.clone | all-reduce | flops 32768 | bytes 196608
  475.0 0.6 fusion.27
  (12 shorter events, 0.1 us)
Async XLA Ops:
  7.2 392.7 %copy-start = (bf16[512,1024]{1,0:T(8,128)(2,1)S(1)}, bf16[512,1024]{1,0:T(8,128)(2,1)}, u32[]{:S(2)}) copy-start(bf16[512,1024]{1,0:T(8,128)(2,1)} %param.10) | copy-start | bytes 3145732
  7.2 27.3 %copy-start.4 = (s32[8192]{0:T(1024)S(1)}, s32[8192]{0:T(1024)}, u32[]{:S(2)}) copy-start(s32[8192]{0:T(1024)} %param.12) | copy-start | bytes 98308
  7.2 122.9 %all-reduce.5.cloned.1.call-start = ((), (), s32[]{:S(2)}) async-start(), calls=%async_computation | async-start | bytes 163840 | tf_op jit(solution)/shard_map/psum | solution.py:90
  34.4 365.4 %all-reduce.7.cloned.1.call-start = ((), (), s32[]{:S(2)}) async-start(), calls=%async_computation.1 | async-start | bytes 2097152 | tf_op jit(solution)/shard_map/psum | solution.py:123
  65.2 89.4 %copy-start.5 = (s32[1024]{0:T(1024)}, s32[1024]{0:T(1024)S(1)}, u32[]{:S(2)}) copy-start(s32[1024]{0:T(1024)S(1)} %pad_clamp_fusion) | copy-start | bytes 12292
  92.6 33.7 %copy-start.1 = (s32[1,32,8,32]{3,2,1,0:T(8,128)S(1)}, s32[1,32,8,32]{3,2,1,0:T(8,128)}, u32[]{:S(2)}) copy-start(s32[1,32,8,32]{3,2,1,0:T(8,128)} %param.13) | copy-start | bytes 98308
  92.6 36.3 %copy-start.10 = (u32[128]{0:T(128)S(1)}, u32[128]{0:T(128)}, u32[]{:S(2)}) copy-start(u32[128]{0:T(128)} %constant.117) | copy-start | bytes 1540
  128.2 27.6 %copy-start.6 = (f32[64]{0:T(128)}, f32[64]{0:T(128)S(1)}, u32[]{:S(2)}) copy-start(f32[64]{0:T(128)S(1)} %get-tuple-element.16) | copy-start | bytes 772
  128.2 27.6 %copy-start.8 = (f32[64]{0:T(128)}, f32[64]{0:T(128)S(1)}, u32[]{:S(2)}) copy-start(f32[64]{0:T(128)S(1)} %get-tuple-element.17) | copy-start | bytes 772
  172.2 2.0 copy-start.2
  172.2 66.2 %copy-start.3 = (f32[64,8]{1,0:T(8,128)S(1)}, f32[64,8]{1,0:T(8,128)}, u32[]{:S(2)}) copy-start(f32[64,8]{1,0:T(8,128)} %convert_element_type.33) | copy-start | bytes 6148
  251.4 69.6 %copy-start.7 = (f32[64]{0:T(128)S(1)}, f32[64]{0:T(128)}, u32[]{:S(2)}) copy-start(f32[64]{0:T(128)} %copy-done.6) | copy-start | bytes 772
  251.4 69.6 %copy-start.9 = (f32[64]{0:T(128)S(1)}, f32[64]{0:T(128)}, u32[]{:S(2)}) copy-start(f32[64]{0:T(128)} %copy-done.8) | copy-start | bytes 772
Sparse Core Ops, SparseCore 0:
  34.5 55.7 all-reduce.4
  254.7 145.0 all-reduce.6
where the time goes:
time: 484 us; the launch traced here: 482 us
  blocking collectives  251 us (52%)
  local copies, waits for them, and re-layouts  103 us (21%)
  waiting for transfers between devices  78.1 us (16%)
  matrix products  26.8 us (6%)
  between operations  15 us (3%)
  other arithmetic  9.03 us (2%)
    psum x1, waiting for transfers between devices, per_device(): lax.psum((seq_total * rescale, seq_acc * rescale[..., None]), ('page', 't...  78.1 us
    unnamed x1, blocking collectives  73.9 us
    psum x1, blocking collectives, per_device(): lax.psum((seq_total * rescale, seq_acc * rescale[..., None]), ('page', 't...  65 us
    pmax x1, blocking collectives, per_device(): top_max = lax.pmax(seq_max, ('page', 'tensor'))  64.2 us
    slice x1, local copies, waits for them, and re-layouts, per_device(): val_rows = pool_five[:, :, :, 1]  33.7 us
    scatter x1, local copies, waits for them, and re-layouts, per_device(): logical = jnp.zeros((pool_size,), jnp.int32).at[page_table].set(jnp.arang...  30.5 us
    reshape x1, local copies, waits for them, and re-layouts, per_device(): pool_five = kv_pool.reshape(slots, PAGE_TOK, KVH, 2, HD)  27.4 us
    all_gather x1, blocking collectives, per_device(): lax.all_gather(tok_rows, 'tensor', axis=0, tiled=True)  24.1 us
  transfers between devices with their start and end apart: 2, of which 1 were waited for; matrix products, arithmetic and copies ran while one was open for 20% of the time, Pallas kernels for 0%

commit v1 on v0

v1 whole, which is shorter than its diff:
```python
import math

import jax
import jax.numpy as jnp
from jax import lax
from jax.sharding import PartitionSpec as P

H = 64
KVH = 8
HD = 128
PAGE_TOK = 64
PAGES = 256


NEG_BIG = -1e30


def frequencies(head_dim):
    half_dim = head_dim // 2
    index = jnp.arange(half_dim, dtype=jnp.float32)
    base_freq = jnp.exp(-(2.0 * index / head_dim) * math.log(500000.0))
    wavelen = 2.0 * math.pi / base_freq
    smooth = (8192.0 / wavelen - 1.0) / 3.0
    middle = (1.0 - smooth) * base_freq / 8.0 + smooth * base_freq
    scaled = jnp.where(wavelen > 8192.0, base_freq / 8.0, base_freq)
    is_middle = jnp.logical_and(wavelen >= 2048.0, wavelen <= 8192.0)
    return jnp.where(is_middle, middle, scaled)


def rotate(vectors, position):
    half_dim = vectors.shape[-1] // 2
    angles = position * frequencies(vectors.shape[-1])
    cosine = jnp.cos(angles)
    sine_v = jnp.sin(angles)
    first_half = vectors[..., :half_dim]
    second_half = vectors[..., half_dim:]
    return jnp.concatenate(
        [first_half * cosine - second_half * sine_v, first_half * sine_v + second_half * cosine],
        axis=-1,
    )


def gather_blocks(x, axis, n):
    return lax.all_to_all(jnp.broadcast_to(x[None], (n,) + x.shape), axis, 0, 0, tiled=True)


def butterfly_sum(x, axis, n):
    d = 1
    while d < n:
        x = x + lax.ppermute(x, axis, [(i, i ^ d) for i in range(n)])
        d *= 2
    return x


def per_device(hidden_in, w_query, w_keyval, w_output, kv_pool, page_table, selected):
    n_page = lax.axis_size("page")
    n_tensor = lax.axis_size("tensor")
    my_page = lax.axis_index("page")
    my_tensor = lax.axis_index("tensor")
    seqs = selected.shape[1]
    groups = H // KVH
    local_heads = H // n_tensor
    scale = 1.0 / math.sqrt(HD)
    slots = kv_pool.shape[0]
    pool_size = page_table.shape[0]
    device = my_page * n_tensor + my_tensor
    position = float(PAGES * PAGE_TOK)
    seq_share = seqs // n_page
    query_cols = w_query.shape[1]
    sub_heads = w_keyval.shape[1] // HD

    my_slots = device * slots + jnp.arange(slots, dtype=jnp.int32)
    match = page_table[None, :] == my_slots[:, None]
    my_logical = jnp.sum(
        jnp.where(match, jnp.arange(pool_size, dtype=jnp.int32)[None, :], 0), axis=1
    )
    seq_of = my_logical // PAGES
    page_of = my_logical % PAGES
    sel_rows = selected[0][seq_of]
    picked = jnp.any(sel_rows == page_of[:, None, None], axis=2)

    tok_all = gather_blocks(hidden_in[0], "tensor", n_tensor).reshape(seqs, -1)
    part_q = jnp.dot(tok_all, w_query, preferred_element_type=jnp.float32)
    part_kv = jnp.dot(tok_all, w_keyval, preferred_element_type=jnp.float32)
    summed = butterfly_sum(jnp.concatenate([part_q, part_kv], axis=1), "page", n_page)
    query = rotate(summed[:, :query_cols].reshape(seqs, local_heads, HD), position)
    query = query.astype(jnp.bfloat16).reshape(seqs, query_cols)
    keyval = summed[:, query_cols:].reshape(seqs, sub_heads, HD)
    kind_ids = (my_tensor * sub_heads + jnp.arange(sub_heads, dtype=jnp.int32)) % 2
    keyval = jnp.where(kind_ids[None, :, None] == 0, rotate(keyval, position), keyval)
    keyval = keyval.reshape(seqs, -1).astype(jnp.bfloat16)
    new_rows = lax.dynamic_slice_in_dim(keyval, my_page * seq_share, seq_share, 0)

    q_all = gather_blocks(query, "tensor", n_tensor)
    q_all = q_all.reshape(KVH, n_tensor // KVH, seqs, local_heads, HD)
    q_all = q_all.transpose(2, 0, 1, 3, 4).reshape(seqs, KVH, groups, HD)
    slot_query = q_all[seq_of]

    maxes, totals, accs = [], [], []
    for g in range(KVH):
        base = g * 2 * HD
        key_g = kv_pool[:, :, base:base + HD]
        val_g = kv_pool[:, :, base + HD:base + 2 * HD]
        sc = jnp.einsum(
            "shd,std->sht", slot_query[:, g], key_g, preferred_element_type=jnp.float32
        ) * scale
        pm = jnp.max(sc, axis=-1)
        wt = jnp.exp(sc - pm[..., None]).astype(jnp.bfloat16)
        pt = jnp.sum(wt.astype(jnp.float32), axis=-1)
        pa = jnp.einsum("sht,std->shd", wt, val_g, preferred_element_type=jnp.float32)
        maxes.append(pm)
        totals.append(pt)
        accs.append(pa)
    page_max = jnp.stack(maxes, axis=1)
    page_total = jnp.stack(totals, axis=1)
    page_acc = jnp.stack(accs, axis=1)
    pick = picked[:, :, None]
    page_max = jnp.where(pick, page_max, NEG_BIG).reshape(slots, H)
    page_total = jnp.where(pick, page_total, 0.0).reshape(slots, H)
    page_acc = jnp.where(pick[..., None], page_acc, 0.0).reshape(slots, H, HD)

    owner_rows = jnp.arange(seqs, dtype=jnp.int32)[:, None] == seq_of[None, :]
    owner_hot = owner_rows.astype(jnp.float32)
    loc_max = jnp.max(jnp.where(owner_rows[:, :, None], page_max[None], NEG_BIG), axis=1)
    factor = jnp.exp(page_max - loc_max[seq_of])
    loc_total = jnp.dot(owner_hot, page_total * factor, precision=lax.Precision.HIGHEST)
    loc_acc = jnp.dot(
        owner_hot,
        (page_acc * factor[..., None]).reshape(slots, H * HD),
        precision=lax.Precision.HIGHEST,
    ).reshape(seqs, H, HD)

    packed = jnp.concatenate([loc_acc, loc_total[..., None], loc_max[..., None]], axis=-1)
    width = HD + 2
    packed = packed.reshape(n_page, seq_share, n_tensor, local_heads, width)
    packed = packed.transpose(0, 2, 1, 3, 4).reshape(n_page * n_tensor, -1)
    got = lax.all_to_all(packed, ("page", "tensor"), 0, 0, tiled=True)
    got = got.reshape(n_page * n_tensor, seq_share, local_heads, width)
    src_max = got[..., HD + 1]
    top_max = jnp.max(src_max, axis=0)
    rescale = jnp.exp(src_max - top_max[None])
    full_total = jnp.sum(got[..., HD] * rescale, axis=0)
    full_acc = jnp.sum(got[..., :HD] * rescale[..., None], axis=0)
    heads = (full_acc / full_total[..., None]).astype(jnp.bfloat16)

    heads_all = gather_blocks(heads.reshape(seq_share, local_heads * HD), "page", n_page)
    heads_all = heads_all.reshape(seqs, local_heads * HD)
    part_out = jnp.dot(heads_all, w_output, preferred_element_type=jnp.float32)
    part_out = part_out.reshape(n_tensor, seqs // n_tensor, -1)
    out = jnp.sum(lax.all_to_all(part_out, "tensor", 0, 0, tiled=True), axis=0)
    return (out.astype(jnp.bfloat16)[None], new_rows[None])


def solution(mesh):
    return jax.shard_map(
        per_device,
        mesh=mesh,
        in_specs=(
            P(None, "tensor", "page"),
            P("page", "tensor"),
            P("page", "tensor"),
            P("tensor", "page"),
            P(("page", "tensor"), None, None),
            P(),
            P(),
        ),
        out_specs=(P(None, "tensor", "page"), P(None, "page", "tensor")),
        check_vma=False,
    )
```

time: 484 us -> 178 us (0.37)
  blocking collectives: 251 us -> 0 us
  local copies, waits for them, and re-layouts: 103 us -> 33 us
  starting transfers between devices: 0.08 us -> 30.5 us
  waiting for transfers between devices: 78.1 us -> 51.5 us
  matrix products: 26.8 us -> 44.2 us
  between operations: 15 us -> 1.37 us
  other arithmetic: 9.03 us -> 16.1 us
    psum x2 -> x0, waiting for transfers between devices: 78.1 us -> none  [the longest x1 78.1 us: per_device(): lax.psum((seq_total * rescale, seq_acc * rescale[..., None]), ('page', 't...]
    unnamed x1 -> x0, blocking collectives: 73.9 us -> none
    psum x1 -> x0, blocking collectives: 65 us -> none  [per_device(): lax.psum((seq_total * rescale, seq_acc * rescale[..., None]), ('page', 't...]
    pmax x1 -> x0, blocking collectives: 64.2 us -> none  [per_device(): top_max = lax.pmax(seq_max, ('page', 'tensor'))]
    all_gather x2 -> x0, blocking collectives: 47.5 us -> none  [the longest x1 24.1 us: per_device(): lax.all_gather(tok_rows, 'tensor', axis=0, tiled=True)]
    all_to_all x0 -> x5, waiting for transfers between devices: none -> 47.1 us  [the longest x3 21.1 us: gather_blocks(): lax.all_to_all(jnp.broadcast_to(x[None], (n,) + x.shape), axis, 0, 0, til...]
    slice x3 -> x2, local copies, waits for them, and re-layouts: 35.2 us -> 0.73 us  [the longest x1 0.72 us: per_device(): keyval = summed[:, query_cols:].reshape(seqs, sub_heads, HD)]
    scatter x1 -> x0, local copies, waits for them, and re-layouts: 30.5 us -> none  [per_device(): logical = jnp.zeros((pool_size,), jnp.int32).at[page_table].set(jnp.arang...]
  transfers between devices with their start and end apart: 2 -> 8, of which waited for: 1 -> 8; matrix products, arithmetic and copies ran while one was open for 20% -> 3% of each run, Pallas kernels for 0% -> 0%
where the time goes in v1:
time: 178 us; the launch traced here: 177 us
  waiting for transfers between devices  51.5 us (29%)
  matrix products  44.2 us (25%)
  local copies, waits for them, and re-layouts  33 us (19%)
  starting transfers between devices  30.5 us (17%)
  other arithmetic  16.1 us (9%)
    all_to_all x3, waiting for transfers between devices, gather_blocks(): lax.all_to_all(jnp.broadcast_to(x[None], (n,) + x.shape), axis, 0, 0, til...  21.1 us
    all_to_all x1, waiting for transfers between devices, per_device(): got = lax.all_to_all(packed, ('page', 'tensor'), 0, 0, tiled=True)  19.7 us
    dot_general x8, matrix products, per_device(): jnp.einsum('sht,std->shd', wt, val_g, preferred_element_type=jnp.float32)  19.1 us
    dot_general x8, matrix products, per_device(): jnp.einsum('shd,std->sht', slot_query[:, g], key_g, preferred_element_typ...  18.7 us
    all_to_all x3, starting transfers between devices, gather_blocks(): lax.all_to_all(jnp.broadcast_to(x[None], (n,) + x.shape), axis, 0, 0, til...  14.2 us
    all_to_all x1, starting transfers between devices, per_device(): got = lax.all_to_all(packed, ('page', 'tensor'), 0, 0, tiled=True)  6.86 us
    all_to_all x1, waiting for transfers between devices, per_device(): out = jnp.sum(lax.all_to_all(part_out, 'tensor', 0, 0, tiled=True), axis=0)  6.32 us
    ppermute x3, starting transfers between devices, butterfly_sum(): x = x + lax.ppermute(x, axis, [(i, i ^ d) for i in range(n)])  5.86 us
  transfers between devices with their start and end apart: 8, of which 8 were waited for; matrix products, arithmetic and copies ran while one was open for 3% of the time, Pallas kernels for 0%

profile of v1, /device:TPU:0, one launch (start us, length us, event | category | flops | bytes accessed | tf_op | source)
XLA Modules:
  0.0 176.6 jit_solution(8891138392290862596)
XLA Ops:
  0.7 1.5 broadcast_in_dim.138
  2.1 7.1 %all-to-all-start = ((bf16[16,2,1024]{2,1,0:T(2,128)(2,1)}), bf16[16,2,1024]{2,1,0:T(2,128)(2,1)S(1)}, u32[]{:S(2)}, u32[]{:S(2)}) async-start(bf16[16,2,1024]{2,1,0:T(2,128)(2,1)} %broadcast_in_dim.138), calls=%async_computation | async-start | bytes 131072 | tf_op jit(solution)/shard_map/all_to_all | solution.py:44
  9.3 1.1 select_reduce_fusion
  10.5 6.5 %all-to-all-done = bf16[16,2,1024]{2,1,0:T(2,128)(2,1)S(1)} async-done(((bf16[16,2,1024]{2,1,0:T(2,128)(2,1)}), bf16[16,2,1024]{2,1,0:T(2,128)(2,1)S(1)}, u32[]{:S(2)}, u32[]{:S(2)}) %all-to-all-start) | async-done | bytes 65568 | tf_op jit(solution)/shard_map/all_to_all | solution.py:44
  17.0 1.5 fusion.57
  18.5 1.1 fusion.58
  19.7 0.6 gather_fusion
  21.0 2.0 %collective-permute-start.1 = (f32[32,640]{1,0:T(8,128)S(1)}, f32[32,640]{1,0:T(8,128)S(1)}, u32[]{:S(2)}, u32[]{:S(2)}) collective-permute-start(f32[32,640]{1,0:T(8,128)S(1)} %fusion.47), channel_id=1, source_target_pairs={{0,32},{16,48},{32,0},{48,16},{64,96},{80,112},{96,64},{112,80},{1... | collective-permute-start | bytes 245768 | tf_op jit(solution)/shard_map/ppermute | solution.py:50
  23.0 1.3 compare_reduce_fusion
  24.3 1.4 collective-permute-done.1
  25.8 3.8 %collective-permute-start.2 = (f32[32,640]{1,0:T(8,128)S(1)}, f32[32,640]{1,0:T(8,128)S(1)}, u32[]{:S(2)}, u32[]{:S(2)}) collective-permute-start(f32[32,640]{1,0:T(8,128)S(1)} %add.112), channel_id=1, source_target_pairs={{0,64},{16,80},{32,96},{48,112},{64,0},{80,16},{96,32},{112,48},{1... | collective-permute-start | bytes 245768 | tf_op jit(solution)/shard_map/ppermute | solution.py:50
  29.6 2.3 %collective-permute-done.2 = f32[32,640]{1,0:T(8,128)S(1)} collective-permute-done((f32[32,640]{1,0:T(8,128)S(1)}, f32[32,640]{1,0:T(8,128)S(1)}, u32[]{:S(2)}, u32[]{:S(2)}) %collective-permute-start.2) | collective-permute-done | bytes 81952 | tf_op jit(solution)/shard_map/ppermute | solution.py:50
  32.9 0.8 broadcast_in_dim.139
  33.7 3.8 %all-to-all-start.1 = ((bf16[16,32,512]{2,1,0:T(8,128)(2,1)}), bf16[16,32,512]{2,1,0:T(8,128)(2,1)S(1)}, u32[]{:S(2)}, u32[]{:S(2)}) async-start(bf16[16,32,512]{2,1,0:T(8,128)(2,1)} %broadcast_in_dim.139), calls=%async_computation.1 | async-start | bytes 1048576 | tf_op jit(solution)/shard_map/all_to_all | solution.py:44
  37.6 10.0 %all-to-all-done.1 = bf16[16,32,512]{2,1,0:T(8,128)(2,1)S(1)} async-done(((bf16[16,32,512]{2,1,0:T(8,128)(2,1)}), bf16[16,32,512]{2,1,0:T(8,128)(2,1)S(1)}, u32[]{:S(2)}, u32[]{:S(2)}) %all-to-all-start.1) | async-done | bytes 524320 | tf_op jit(solution)/shard_map/all_to_all | solution.py:44
  48.5 0.7 gather_fusion.1
  49.2 1.9 %fusion.49 = (f32[64,8]{1,0:T(8,128)S(1)}, f32[64,8,64]{2,1,0:T(8,128)S(1)}) fusion(bf16[64,64,2048]{2,1,0:T(8,128)(2,1)} %param.11, bf16[64,8,8,128]{3,2,1,0:T(8,128)(2,1)S(1)} %gather_fusion.1), kind=kOutput, calls=%fused_computation.155 | convolution fusion | flops 8453632 | bytes 1312768 | tf_op jit(solution)/shard_map/shd,std->sht/dot_general | solution.py:104
  51.2 3.2 %fusion.50 = (f32[64,8]{1,0:T(8,128)}, f32[64,8,64]{2,1,0:T(8,128)}) fusion(bf16[64,64,2048]{2,1,0:T(8,128)(2,1)} %param.11, bf16[64,8,8,128]{3,2,1,0:T(8,128)(2,1)S(1)} %gather_fusion.1), kind=kOutput, calls=%fused_computation.156 | convolution fusion | flops 8453632 | bytes 1312768 | tf_op jit(solution)/shard_map/shd,std->sht/dot_general | solution.py:104
  54.4 3.2 %fusion.51 = (f32[64,8]{1,0:T(8,128)}, f32[64,8,64]{2,1,0:T(8,128)}) fusion(bf16[64,64,2048]{2,1,0:T(8,128)(2,1)} %param.11, bf16[64,8,8,128]{3,2,1,0:T(8,128)(2,1)S(1)} %gather_fusion.1), kind=kOutput, calls=%fused_computation.157 | convolution fusion | flops 8453632 | bytes 1312768 | tf_op jit(solution)/shard_map/shd,std->sht/dot_general | solution.py:104
  57.6 2.6 %fusion.52 = (f32[64,8]{1,0:T(8,128)}, f32[64,8,64]{2,1,0:T(8,128)S(1)}) fusion(bf16[64,64,2048]{2,1,0:T(8,128)(2,1)} %param.11, bf16[64,8,8,128]{3,2,1,0:T(8,128)(2,1)S(1)} %gather_fusion.1), kind=kOutput, calls=%fused_computation.158 | convolution fusion | flops 8453632 | bytes 1312768 | tf_op jit(solution)/shard_map/shd,std->sht/dot_general | solution.py:104
  60.1 1.9 %fusion.53 = (f32[64,8]{1,0:T(8,128)S(1)}, f32[64,8,64]{2,1,0:T(8,128)S(1)}) fusion(bf16[64,64,2048]{2,1,0:T(8,128)(2,1)} %param.11, bf16[64,8,8,128]{3,2,1,0:T(8,128)(2,1)S(1)} %gather_fusion.1), kind=kOutput, calls=%fused_computation.159 | convolution fusion | flops 8453632 | bytes 1312768 | tf_op jit(solution)/shard_map/shd,std->sht/dot_general | solution.py:104
  62.1 2.0 %fusion.54 = (f32[64,8]{1,0:T(8,128)S(1)}, f32[64,8,64]{2,1,0:T(8,128)S(1)}) fusion(bf16[64,64,2048]{2,1,0:T(8,128)(2,1)} %param.11, bf16[64,8,8,128]{3,2,1,0:T(8,128)(2,1)S(1)} %gather_fusion.1), kind=kOutput, calls=%fused_computation.160 | convolution fusion | flops 8453632 | bytes 1312768 | tf_op jit(solution)/shard_map/shd,std->sht/dot_general | solution.py:104
  64.1 2.0 %fusion.55 = (f32[64,8]{1,0:T(8,128)S(1)}, f32[64,8,64]{2,1,0:T(8,128)S(1)}) fusion(bf16[64,64,2048]{2,1,0:T(8,128)(2,1)} %param.11, bf16[64,8,8,128]{3,2,1,0:T(8,128)(2,1)S(1)} %gather_fusion.1), kind=kOutput, calls=%fused_computation.161 | convolution fusion | flops 8453632 | bytes 1312768 | tf_op jit(solution)/shard_map/shd,std->sht/dot_general | solution.py:104
  66.0 2.0 %fusion.56 = (f32[64,8]{1,0:T(8,128)S(1)}, f32[64,8,64]{2,1,0:T(8,128)S(1)}) fusion(bf16[64,64,2048]{2,1,0:T(8,128)(2,1)} %param.11, bf16[64,8,8,128]{3,2,1,0:T(8,128)(2,1)S(1)} %gather_fusion.1), kind=kOutput, calls=%fused_computation.162 | convolution fusion | flops 8453632 | bytes 1312768 | tf_op jit(solution)/shard_map/shd,std->sht/dot_general | solution.py:104
  68.0 2.4 %fusion.11 = f32[64,8,8,128]{3,2,0,1:T(8,128)} fusion(bf16[64,64,2048]{2,1,0:T(8,128)(2,1)} %param.11, f32[64,8,64]{2,1,0:T(8,128)S(1)} %get-tuple-element.14, f32[64,8]{1,0:T(8,128)S(1)} %get-tuple-element.13), kind=kOutput, calls=%fused_computation.26 | convolution fusion | flops 8454143 | bytes 1443840 | tf_op jit(solution)/shard_map/sht,std->shd/dot_general | solution.py:110
  70.4 0.8 convert_reduce_fusion.7
  71.2 0.8 copy.161
  72.1 0.8 copy.162
  72.9 0.8 copy.163
  73.7 0.8 copy.164
  75.6 1.3 gather_fusion.2
  76.9 0.9 concatenate.23
  77.8 0.8 convert_reduce_fusion.6
  78.6 2.4 %fusion.10 = f32[64,8,8,128]{3,2,0,1:T(8,128)} fusion(f32[64,8,8,128]{3,2,0,1:T(8,128)} %fusion.11, bf16[64,64,2048]{2,1,0:T(8,128)(2,1)} %param.11, f32[64,8,64]{2,1,0:T(8,128)S(1)} %copy-done.3, f32[64,8]{1,0:T(8,128)S(1)} %copy-done.7), kind=kOutput, calls=%fused_computation.24 | convolution fusion | flops 8454144 | bytes 1443840 | tf_op jit(solution)/shard_map/sht,std->shd/dot_general | solution.py:110
  81.0 0.8 convert_reduce_fusion.5
  81.8 2.4 %fusion.9 = f32[64,8,8,128]{3,2,0,1:T(8,128)} fusion(f32[64,8,8,128]{3,2,0,1:T(8,128)} %fusion.10, bf16[64,64,2048]{2,1,0:T(8,128)(2,1)} %param.11, f32[64,8,64]{2,1,0:T(8,128)S(1)} %copy-done.2, f32[64,8]{1,0:T(8,128)S(1)} %copy-done.6), kind=kOutput, calls=%fused_computation.22 | convolution fusion | flops 8454144 | bytes 1443840 | tf_op jit(solution)/shard_map/sht,std->shd/dot_general | solution.py:110
  84.2 0.8 convert_reduce_fusion.4
  85.0 2.4 %fusion.8 = f32[64,8,8,128]{3,2,0,1:T(8,128)} fusion(f32[64,8,8,128]{3,2,0,1:T(8,128)} %fusion.9, bf16[64,64,2048]{2,1,0:T(8,128)(2,1)} %param.11, f32[64,8,64]{2,1,0:T(8,128)S(1)} %get-tuple-element.20, f32[64,8]{1,0:T(8,128)S(1)} %copy-done.5), kind=kOutput, calls=%fused_computation.20 | convolution fusion | flops 8454144 | bytes 1443840 | tf_op jit(solution)/shard_map/sht,std->shd/dot_general | solution.py:110
  87.6 2.4 %fusion.7 = f32[64,8,8,128]{3,2,0,1:T(8,128)} fusion(f32[64,8,8,128]{3,2,0,1:T(8,128)} %fusion.8, bf16[64,64,2048]{2,1,0:T(8,128)(2,1)} %param.11, f32[64,8,64]{2,1,0:T(8,128)S(1)} %get-tuple-element.22, f32[64,8]{1,0:T(8,128)S(1)} %get-tuple-element.21), kind=kOutput, calls=%fused_computation.18 | convolution fusion | flops 8454144 | bytes 1443840 | tf_op jit(solution)/shard_map/sht,std->shd/dot_general | solution.py:110
  90.3 2.4 %fusion.6 = f32[64,8,8,128]{3,2,0,1:T(8,128)} fusion(f32[64,8,8,128]{3,2,0,1:T(8,128)} %fusion.7, bf16[64,64,2048]{2,1,0:T(8,128)(2,1)} %param.11, f32[64,8,64]{2,1,0:T(8,128)S(1)} %get-tuple-element.24, f32[64,8]{1,0:T(8,128)S(1)} %get-tuple-element.23), kind=kOutput, calls=%fused_computation.16 | convolution fusion | flops 8454144 | bytes 1443840 | tf_op jit(solution)/shard_map/sht,std->shd/dot_general | solution.py:110
  92.9 2.4 %fusion.5 = f32[64,8,8,128]{3,2,0,1:T(8,128)} fusion(f32[64,8,8,128]{3,2,0,1:T(8,128)} %fusion.6, bf16[64,64,2048]{2,1,0:T(8,128)(2,1)} %param.11, f32[64,8,64]{2,1,0:T(8,128)S(1)} %get-tuple-element.26, f32[64,8]{1,0:T(8,128)S(1)} %get-tuple-element.25), kind=kOutput, calls=%fused_computation.14 | convolution fusion | flops 8454144 | bytes 1443840 | tf_op jit(solution)/shard_map/sht,std->shd/dot_general | solution.py:110
  95.5 2.4 %fusion.4 = f32[64,8,8,128]{3,2,0,1:T(8,128)} fusion(f32[64,8,8,128]{3,2,0,1:T(8,128)} %fusion.5, bf16[64,64,2048]{2,1,0:T(8,128)(2,1)} %param.11, f32[64,8,64]{2,1,0:T(8,128)S(1)} %get-tuple-element.28, f32[64,8]{1,0:T(8,128)S(1)} %get-tuple-element.27), kind=kOutput, calls=%fused_computation.12 | convolution fusion | flops 8454144 | bytes 1443840 | tf_op jit(solution)/shard_map/sht,std->shd/dot_general | solution.py:110
  97.9 1.9 %copy.160 = f32[64,8,8,128]{3,2,1,0:T(8,128)S(1)} copy(f32[64,8,8,128]{3,2,0,1:T(8,128)} %fusion.4) | data formatting | bytes 4194304 | tf_op jit(solution)/shard_map/stack | solution.py:116
  101.2 0.9 broadcast_in_dim.135
  102.1 4.9 %fusion = f32[8192,64]{0,1:T(8,128)} fusion(f32[8,8,64,128]{3,2,1,0:T(8,128)S(1)} %bitcast.200, f32[8,8,64,128]{3,2,1,0:T(8,128)S(1)} %bitcast.199, pred[8,8,64,128]{3,2,1,0:T(8,128)(4,1)S(1)} %bitcast.203), kind=kLoop, calls=%fused_computation.4 | loop fusion | flops 1048576 | bytes 6815744 | tf_op jit(solution)/shard_map/dot_general | solution.py:127
  107.1 2.7 %dot_general.92 = f32[16,4,128,64]{2,1,0,3:T(4,128)S(1)} reshape(f32[8192,64]{0,1:T(8,128)} %fusion) | data formatting | bytes 4194304 | tf_op jit(solution)/shard_map/dot_general | solution.py:127
  109.8 3.1 %fusion.1 = f32[8,4,16,4,128]{4,0,3,2,1:T(8,128)} fusion(f32[16,4,128,64]{2,1,0,3:T(4,128)S(1)} %dot_general.92, s32[64]{0:T(128)S(1)} %copy-done.20, s32[8,4]{0,1:T(4,128)S(1)} %multiply_add_fusion), kind=kOutput, calls=%fused_computation.7 | convolution fusion | flops 201328640 | bytes 3146112 | tf_op jit(solution)/shard_map/dot_general | solution.py:127
  113.2 2.0 %copy.184 = f32[8,4,16,4,1]{4,0,3,2,1:T(8,128)} copy(f32[8,4,16,4,1]{2,0,4,3,1:T(8,128)S(1)} %convolution_bitcast_fusion.8) | data formatting | bytes 16384 | tf_op jit(solution)/shard_map/dot_general | solution.py:126
  115.2 3.3 %copy.185 = f32[8,4,16,4,1]{4,0,3,2,1:T(8,128)S(1)} copy(f32[8,4,16,4,1]{3,2,1,0,4:T(8,128)S(1)} %copy-done.4) | data formatting | bytes 16384 | tf_op jit(solution)/shard_map/concatenate | solution.py:133
  118.4 1.6 maximum_bitcast_fusion
  120.1 0.8 copy.186
  120.9 4.4 %all_to_all.24 = f32[128,1,2080]{2,1,0:T(1,128)} reshape(f32[8,16,4,4,130]{4,3,2,1,0:T(4,128)S(1)} %copy.186) | data formatting | bytes 2129920 | tf_op jit(solution)/shard_map/all_to_all | solution.py:137
  125.3 6.9 %all-to-all-start.2 = ((f32[128,1,2080]{2,1,0:T(1,128)}), f32[128,1,2080]{2,1,0:T(1,128)S(1)}, u32[]{:S(2)}, u32[]{:S(2)}) async-start(f32[128,1,2080]{2,1,0:T(1,128)} %all_to_all.24), calls=%async_computation.2 | async-start | bytes 2228224 | tf_op jit(solution)/shard_map/all_to_all | solution.py:137
  132.2 19.7 %all-to-all-done.2 = f32[128,1,2080]{2,1,0:T(1,128)S(1)} async-done(((f32[128,1,2080]{2,1,0:T(1,128)}), f32[128,1,2080]{2,1,0:T(1,128)S(1)}, u32[]{:S(2)}, u32[]{:S(2)}) %all-to-all-start.2) | async-done | bytes 1064992 | tf_op jit(solution)/shard_map/all_to_all | solution.py:137
  151.8 1.5 copy.188
  154.9 3.3 %all-to-all-start.3 = ((bf16[8,4,512]{2,1,0:T(4,128)(2,1)}), bf16[8,4,512]{2,1,0:T(4,128)(2,1)S(1)}, u32[]{:S(2)}, u32[]{:S(2)}) async-start(bf16[8,4,512]{2,1,0:T(4,128)(2,1)} %broadcast_in_dim.146), calls=%async_computation.3 | async-start | bytes 65536 | tf_op jit(solution)/shard_map/all_to_all | solution.py:44
  158.2 0.7 slice_bitcast_fusion.16
  158.9 4.6 %all-to-all-done.3 = bf16[8,4,512]{2,1,0:T(4,128)(2,1)S(1)} async-done(((bf16[8,4,512]{2,1,0:T(4,128)(2,1)}), bf16[8,4,512]{2,1,0:T(4,128)(2,1)S(1)}, u32[]{:S(2)}, u32[]{:S(2)}) %all-to-all-start.3) | async-done | bytes 32800 | tf_op jit(solution)/shard_map/all_to_all | solution.py:44
  163.9 0.7 copy.190
  164.6 3.5 %all-to-all-start.4 = ((f32[16,2,1024]{2,1,0:T(2,128)}), f32[16,2,1024]{2,1,0:T(2,128)S(1)}, u32[]{:S(2)}, u32[]{:S(2)}) async-start(f32[16,2,1024]{2,1,0:T(2,128)} %copy.190), calls=%async_computation.4 | async-start | bytes 262144 | tf_op jit(solution)/shard_map/all_to_all | solution.py:150
  168.2 0.7 slice.152
  169.0 0.6 fusion.42
  169.6 6.3 %all-to-all-done.4 = f32[16,2,1024]{2,1,0:T(2,128)S(1)} async-done(((f32[16,2,1024]{2,1,0:T(2,128)}), f32[16,2,1024]{2,1,0:T(2,128)S(1)}, u32[]{:S(2)}, u32[]{:S(2)}) %all-to-all-start.4) | async-done | bytes 131104 | tf_op jit(solution)/shard_map/all_to_all | solution.py:150
  175.9 0.6 reduce_sum.122
  (126 shorter events, 8.1 us)
Async XLA Ops:
  0.6 163.0 %copy-start = (bf16[512,1024]{1,0:T(8,128)(2,1)S(1)}, bf16[512,1024]{1,0:T(8,128)(2,1)}, u32[]{:S(2)}) copy-start(bf16[512,1024]{1,0:T(8,128)(2,1)} %param.10) | copy-start | bytes 3145732
  0.6 19.1 %copy-start.9 = (s32[1,32,8,32]{3,2,1,0:T(8,128)S(1)}, s32[1,32,8,32]{3,2,1,0:T(8,128)}, u32[]{:S(2)}) copy-start(s32[1,32,8,32]{3,2,1,0:T(8,128)} %param.13) | copy-start | bytes 98308
  2.1 14.8 %all-to-all-start = ((bf16[16,2,1024]{2,1,0:T(2,128)(2,1)}), bf16[16,2,1024]{2,1,0:T(2,128)(2,1)S(1)}, u32[]{:S(2)}, u32[]{:S(2)}) async-start(bf16[16,2,1024]{2,1,0:T(2,128)(2,1)} %broadcast_in_dim.138), calls=%async_computation | async-start | bytes 131072 | tf_op jit(solution)/shard_map/all_to_all | solution.py:44
  10.4 27.1 %copy-start.19 = (s32[64]{0:T(128)}, s32[64]{0:T(128)S(1)}, u32[]{:S(2)}) copy-start(s32[64]{0:T(128)S(1)} %get-tuple-element.11) | copy-start | bytes 772
  19.6 1.4 collective-permute-start
  19.7 28.7 %copy-start.18 = (s32[1024]{0:T(1024)}, s32[1024]{0:T(1024)S(1)}, u32[]{:S(2)}) copy-start(s32[1024]{0:T(1024)S(1)} %pad_clamp_fusion) | copy-start | bytes 12292
  21.0 4.8 %collective-permute-start.1 = (f32[32,640]{1,0:T(8,128)S(1)}, f32[32,640]{1,0:T(8,128)S(1)}, u32[]{:S(2)}, u32[]{:S(2)}) collective-permute-start(f32[32,640]{1,0:T(8,128)S(1)} %fusion.47), channel_id=1, source_target_pairs={{0,32},{16,48},{32,0},{48,16},{64,96},{80,112},{96,64},{112,80},{1... | collective-permute-start | bytes 245768 | tf_op jit(solution)/shard_map/ppermute | solution.py:50
  25.8 6.2 %collective-permute-start.2 = (f32[32,640]{1,0:T(8,128)S(1)}, f32[32,640]{1,0:T(8,128)S(1)}, u32[]{:S(2)}, u32[]{:S(2)}) collective-permute-start(f32[32,640]{1,0:T(8,128)S(1)} %add.112), channel_id=1, source_target_pairs={{0,64},{16,80},{32,96},{48,112},{64,0},{80,16},{96,32},{112,48},{1... | collective-permute-start | bytes 245768 | tf_op jit(solution)/shard_map/ppermute | solution.py:50
  29.6 4.1 %copy-start.21 = (f32[64]{0:T(128)}, f32[64]{0:T(128)S(1)}, u32[]{:S(2)}) copy-start(f32[64]{0:T(128)S(1)} %get-tuple-element.29) | copy-start | bytes 772
  29.6 4.1 %copy-start.23 = (f32[64]{0:T(128)}, f32[64]{0:T(128)S(1)}, u32[]{:S(2)}) copy-start(f32[64]{0:T(128)S(1)} %get-tuple-element.30) | copy-start | bytes 772
  32.0 0.6 copy-start.10
  33.7 13.9 %all-to-all-start.1 = ((bf16[16,32,512]{2,1,0:T(8,128)(2,1)}), bf16[16,32,512]{2,1,0:T(8,128)(2,1)S(1)}, u32[]{:S(2)}, u32[]{:S(2)}) async-start(bf16[16,32,512]{2,1,0:T(8,128)(2,1)} %broadcast_in_dim.139), calls=%async_computation.1 | async-start | bytes 1048576 | tf_op jit(solution)/shard_map/all_to_all | solution.py:44
  51.2 19.2 %copy-start.8 = (f32[64,8]{1,0:T(8,128)}, f32[64,8]{1,0:T(8,128)S(1)}, u32[]{:S(2)}) copy-start(f32[64,8]{1,0:T(8,128)S(1)} %get-tuple-element.13) | copy-start | bytes 6148
  68.0 9.8 %copy-start.3 = (f32[64,8,64]{2,1,0:T(8,128)S(1)}, f32[64,8,64]{2,1,0:T(8,128)}, u32[]{:S(2)}) copy-start(f32[64,8,64]{2,1,0:T(8,128)} %get-tuple-element.16) | copy-start | bytes 393220
  68.0 9.8 %copy-start.7 = (f32[64,8]{1,0:T(8,128)S(1)}, f32[64,8]{1,0:T(8,128)}, u32[]{:S(2)}) copy-start(f32[64,8]{1,0:T(8,128)} %get-tuple-element.15) | copy-start | bytes 6148
  70.4 10.6 %copy-start.2 = (f32[64,8,64]{2,1,0:T(8,128)S(1)}, f32[64,8,64]{2,1,0:T(8,128)}, u32[]{:S(2)}) copy-start(f32[64,8,64]{2,1,0:T(8,128)} %get-tuple-element.18) | copy-start | bytes 393220
  70.4 10.6 %copy-start.6 = (f32[64,8]{1,0:T(8,128)S(1)}, f32[64,8]{1,0:T(8,128)}, u32[]{:S(2)}) copy-start(f32[64,8]{1,0:T(8,128)} %get-tuple-element.17) | copy-start | bytes 6148
  75.0 0.6 copy-start.11
  76.9 7.3 %copy-start.5 = (f32[64,8]{1,0:T(8,128)S(1)}, f32[64,8]{1,0:T(8,128)}, u32[]{:S(2)}) copy-start(f32[64,8]{1,0:T(8,128)} %get-tuple-element.19) | copy-start | bytes 6148
  97.9 1.9 %copy-start.14 = (f32[64,8]{1,0:T(8,128)S(1)}, f32[64,8]{1,0:T(8,128)}, u32[]{:S(2)}) copy-start(f32[64,8]{1,0:T(8,128)} %convert_reduce_fusion.6) | copy-start | bytes 6148
  97.9 2.0 %copy-start.13 = (f32[64,8]{1,0:T(8,128)S(1)}, f32[64,8]{1,0:T(8,128)}, u32[]{:S(2)}) copy-start(f32[64,8]{1,0:T(8,128)} %convert_reduce_fusion.7) | copy-start | bytes 6148
  97.9 2.1 %copy-start.15 = (f32[64,8]{1,0:T(8,128)S(1)}, f32[64,8]{1,0:T(8,128)}, u32[]{:S(2)}) copy-start(f32[64,8]{1,0:T(8,128)} %convert_reduce_fusion.5) | copy-start | bytes 6148
  97.9 2.2 %copy-start.16 = (f32[64,8]{1,0:T(8,128)S(1)}, f32[64,8]{1,0:T(8,128)}, u32[]{:S(2)}) copy-start(f32[64,8]{1,0:T(8,128)} %convert_reduce_fusion.4) | copy-start | bytes 6148
  97.9 2.6 %copy-start.12 = (f32[64,64]{1,0:T(8,128)S(1)}, f32[64,64]{1,0:T(8,128)}, u32[]{:S(2)}) copy-start(f32[64,64]{1,0:T(8,128)} %copy-done.11) | copy-start | bytes 49156
  97.9 2.6 %copy-start.17 = (f32[64,64]{1,0:T(8,128)S(1)}, f32[64,64]{1,0:T(8,128)}, u32[]{:S(2)}) copy-start(f32[64,64]{1,0:T(8,128)} %gather_fusion.2) | copy-start | bytes 49156
  107.0 2.8 %copy-start.20 = (s32[64]{0:T(128)S(1)}, s32[64]{0:T(128)}, u32[]{:S(2)}) copy-start(s32[64]{0:T(128)} %copy-done.19) | copy-start | bytes 772
  109.8 5.4 %copy-start.4 = (f32[8,4,16,4,1]{3,2,1,0,4:T(8,128)S(1)}, f32[8,4,16,4,1]{3,2,1,0,4:T(8,128)}, u32[]{:S(2)}) copy-start(f32[8,4,16,4,1]{3,2,1,0,4:T(8,128)} %concatenate.23) | copy-start | bytes 24580
  113.0 5.5 %copy-start.1 = (f32[8,4,16,4,128]{4,0,3,2,1:T(8,128)S(1)}, f32[8,4,16,4,128]{4,0,3,2,1:T(8,128)}, u32[]{:S(2)}) copy-start(f32[8,4,16,4,128]{4,0,3,2,1:T(8,128)} %fusion.1) | copy-start | bytes 3145732
  125.3 26.6 %all-to-all-start.2 = ((f32[128,1,2080]{2,1,0:T(1,128)}), f32[128,1,2080]{2,1,0:T(1,128)S(1)}, u32[]{:S(2)}, u32[]{:S(2)}) async-start(f32[128,1,2080]{2,1,0:T(1,128)} %all_to_all.24), calls=%async_computation.2 | async-start | bytes 2228224 | tf_op jit(solution)/shard_map/all_to_all | solution.py:137
  153.4 14.8 %copy-start.22 = (f32[64]{0:T(128)S(1)}, f32[64]{0:T(128)}, u32[]{:S(2)}) copy-start(f32[64]{0:T(128)} %copy-done.21) | copy-start | bytes 772
  153.4 14.8 %copy-start.24 = (f32[64]{0:T(128)S(1)}, f32[64]{0:T(128)}, u32[]{:S(2)}) copy-start(f32[64]{0:T(128)} %copy-done.23) | copy-start | bytes 772
  154.9 8.7 %all-to-all-start.3 = ((bf16[8,4,512]{2,1,0:T(4,128)(2,1)}), bf16[8,4,512]{2,1,0:T(4,128)(2,1)S(1)}, u32[]{:S(2)}, u32[]{:S(2)}) async-start(bf16[8,4,512]{2,1,0:T(4,128)(2,1)} %broadcast_in_dim.146), calls=%async_computation.3 | async-start | bytes 65536 | tf_op jit(solution)/shard_map/all_to_all | solution.py:44
  164.6 11.3 %all-to-all-start.4 = ((f32[16,2,1024]{2,1,0:T(2,128)}), f32[16,2,1024]{2,1,0:T(2,128)S(1)}, u32[]{:S(2)}, u32[]{:S(2)}) async-start(f32[16,2,1024]{2,1,0:T(2,128)} %copy.190), calls=%async_computation.4 | async-start | bytes 262144 | tf_op jit(solution)/shard_map/all_to_all | solution.py:150

commit v2 on v1

--- a/solution.py
+++ b/solution.py
@@ -3,6 +3,7 @@
 import jax
 import jax.numpy as jnp
 from jax import lax
+from jax.experimental import pallas as pl
 from jax.sharding import PartitionSpec as P
 
 H = 64
@@ -50,6 +51,56 @@
         x = x + lax.ppermute(x, axis, [(i, i ^ d) for i in range(n)])
         d *= 2
     return x
+
+
+def attn_kernel(q_ref, kv_ref, acc_ref, m_ref, t_ref):
+    tok = kv_ref.shape[1]
+    rows = lax.broadcasted_iota(jnp.int32, (H, KVH * tok), 0) // (H // KVH)
+    cols = lax.broadcasted_iota(jnp.int32, (H, KVH * tok), 1) // tok
+    same_group = rows == cols
+    scale = 1.0 / math.sqrt(HD)
+
+    def body(j, carry):
+        keys = jnp.concatenate(
+            [kv_ref[j, :, pl.ds(g * 2 * HD, HD)] for g in range(KVH)], axis=0
+        )
+        vals = jnp.concatenate(
+            [kv_ref[j, :, pl.ds(g * 2 * HD + HD, HD)] for g in range(KVH)], axis=0
+        )
+        sc = lax.dot_general(
+            q_ref[j], keys, (((1,), (1,)), ((), ())), preferred_element_type=jnp.float32
+        ) * scale
+        sc = jnp.where(same_group, sc, -jnp.inf)
+        pm = jnp.max(sc, axis=1, keepdims=True)
+        wt = jnp.exp(sc - pm).astype(jnp.bfloat16)
+        acc_ref[j] = jnp.dot(wt, vals, preferred_element_type=jnp.float32)
+        m_ref[j] = pm
+        t_ref[j] = jnp.sum(wt.astype(jnp.float32), axis=1, keepdims=True)
+        return carry
+
+    lax.fori_loop(0, q_ref.shape[0], body, 0)
+
+
+def attend(slot_query, kv_pool, block=8):
+    slots, tok, width = kv_pool.shape
+    return pl.pallas_call(
+        attn_kernel,
+        grid=(slots // block,),
+        in_specs=[
+            pl.BlockSpec((block, H, HD), lambda i: (i, 0, 0)),
+            pl.BlockSpec((block, tok, width), lambda i: (i, 0, 0)),
+        ],
+        out_specs=[
+            pl.BlockSpec((block, H, HD), lambda i: (i, 0, 0)),
+            pl.BlockSpec((block, H, 1), lambda i: (i, 0, 0)),
+            pl.BlockSpec((block, H, 1), lambda i: (i, 0, 0)),
+        ],
+        out_shape=[
+            jax.ShapeDtypeStruct((slots, H, HD), jnp.float32),
+            jax.ShapeDtypeStruct((slots, H, 1), jnp.float32),
+            jax.ShapeDtypeStruct((slots, H, 1), jnp.float32),
+        ],
+    )(slot_query, kv_pool)
 
 
 def per_device(hidden_in, w_query, w_keyval, w_output, kv_pool, page_table, selected):
@@ -96,24 +147,10 @@
     q_all = q_all.transpose(2, 0, 1, 3, 4).reshape(seqs, KVH, groups, HD)
     slot_query = q_all[seq_of]
 
-    maxes, totals, accs = [], [], []
-    for g in range(KVH):
-        base = g * 2 * HD
-        key_g = kv_pool[:, :, base:base + HD]
-        val_g = kv_pool[:, :, base + HD:base + 2 * HD]
-        sc = jnp.einsum(
-            "shd,std->sht", slot_query[:, g], key_g, preferred_element_type=jnp.float32
-        ) * scale
-        pm = jnp.max(sc, axis=-1)
-        wt = jnp.exp(sc - pm[..., None]).astype(jnp.bfloat16)
-        pt = jnp.sum(wt.astype(jnp.float32), axis=-1)
-        pa = jnp.einsum("sht,std->shd", wt, val_g, preferred_element_type=jnp.float32)
-        maxes.append(pm)
-        totals.append(pt)
-        accs.append(pa)
-    page_max = jnp.stack(maxes, axis=1)
-    page_total = jnp.stack(totals, axis=1)
-    page_acc = jnp.stack(accs, axis=1)
+    page_acc, page_max, page_total = attend(slot_query.reshape(slots, H, HD), kv_pool)
+    page_max = page_max.reshape(slots, KVH, groups)
+    page_total = page_total.reshape(slots, KVH, groups)
+    page_acc = page_acc.reshape(slots, KVH, groups, HD)
     pick = picked[:, :, None]
     page_max = jnp.where(pick, page_max, NEG_BIG).reshape(slots, H)
     page_total = jnp.where(pick, page_total, 0.0).reshape(slots, H)

time: 178 us -> 162 us (0.910)
  matrix products: 44.2 us -> 6 us
  Pallas kernels: 0 us -> 27.9 us
  other arithmetic: 16.1 us -> 13.9 us
    dot_general x16 -> x0, matrix products: 37.9 us -> none  [the longest x8 19.1 us: per_device(): jnp.einsum('sht,std->shd', wt, val_g, preferred_element_type=jnp.float32)]
    pallas_call x0 -> x1, Pallas kernels: none -> 27.9 us  [attend(): pl.pallas_call(attn_kernel, grid=(slots // block,), in_specs=[pl.BlockSpe...]
    another operation x21 -> x0, local copies, waits for them, and re-layouts: 6.08 us -> none  [the longest x10 3.6 us: per_device(): page_max = jnp.stack(maxes, axis=1)]
    dot_general x1 -> x0, other arithmetic: 4.94 us -> none  [per_device(): jnp.dot(owner_hot, (page_acc * factor[..., None]).reshape(slots, H * HD),...]
    reduce_sum x8 -> x0, other arithmetic: 4.2 us -> none  [per_device(): pt = jnp.sum(wt.astype(jnp.float32), axis=-1)]
    pallas_call x0 -> x2, other arithmetic: none -> 3.58 us  [attend(): pl.pallas_call(attn_kernel, grid=(slots // block,), in_specs=[pl.BlockSpe...]
    broadcast_in_dim x0 -> x2, local copies, waits for them, and re-layouts: none -> 2.71 us  [per_device(): page_max = jnp.where(pick, page_max, NEG_BIG).reshape(slots, H)]
    exp x0 -> x1, other arithmetic: none -> 2.45 us  [per_device(): factor = jnp.exp(page_max - loc_max[seq_of])]
  transfers between devices with their start and end apart: 8 -> 8, of which waited for: 8 -> 8; matrix products, arithmetic and copies ran while one was open for 3% -> 4% of each run, Pallas kernels for 0% -> 0%
where the time goes in v2:
time: 162 us
  waiting for transfers between devices  50.2 us (31%)
  local copies, waits for them, and re-layouts  32.1 us (20%)
  starting transfers between devices  30.5 us (19%)
  Pallas kernels  27.9 us (17%)
  other arithmetic  13.9 us (9%)
  matrix products  6 us (4%)
    pallas_call x1, Pallas kernels, attend(): pl.pallas_call(attn_kernel, grid=(slots // block,), in_specs=[pl.BlockSpe...  27.9 us
    all_to_all x1, waiting for transfers between devices, per_device(): got = lax.all_to_all(packed, ('page', 'tensor'), 0, 0, tiled=True)  19.7 us
    all_to_all x3, waiting for transfers between devices, gather_blocks(): lax.all_to_all(jnp.broadcast_to(x[None], (n,) + x.shape), axis, 0, 0, til...  19.1 us
    all_to_all x3, starting transfers between devices, gather_blocks(): lax.all_to_all(jnp.broadcast_to(x[None], (n,) + x.shape), axis, 0, 0, til...  14.2 us
    all_to_all x1, waiting for transfers between devices, per_device(): out = jnp.sum(lax.all_to_all(part_out, 'tensor', 0, 0, tiled=True), axis=0)  7.03 us
    all_to_all x1, starting transfers between devices, per_device(): got = lax.all_to_all(packed, ('page', 'tensor'), 0, 0, tiled=True)  6.86 us
    ppermute x3, starting transfers between devices, butterfly_sum(): x = x + lax.ppermute(x, axis, [(i, i ^ d) for i in range(n)])  5.86 us
    all_to_all x2, local copies, waits for them, and re-layouts, per_device(): got = lax.all_to_all(packed, ('page', 'tensor'), 0, 0, tiled=True)  5.83 us
  transfers between devices with their start and end apart: 8, of which 8 were waited for; matrix products, arithmetic and copies ran while one was open for 4% of the time, Pallas kernels for 0%

profile of v2, /device:TPU:0, one launch (start us, length us, event | category | flops | bytes accessed | tf_op | source)
XLA Modules:
  0.0 161.7 jit_solution(8549034432666987721)
XLA Ops:
  0.7 1.4 broadcast_in_dim.131
  2.1 7.1 %all-to-all-start = ((bf16[16,2,1024]{2,1,0:T(2,128)(2,1)}), bf16[16,2,1024]{2,1,0:T(2,128)(2,1)S(1)}, u32[]{:S(2)}, u32[]{:S(2)}) async-start(bf16[16,2,1024]{2,1,0:T(2,128)(2,1)} %broadcast_in_dim.131), calls=%async_computation | async-start | bytes 131072 | tf_op jit(solution)/shard_map/all_to_all | solution.py:45
  9.3 1.1 select_reduce_fusion
  10.5 6.5 %all-to-all-done = bf16[16,2,1024]{2,1,0:T(2,128)(2,1)S(1)} async-done(((bf16[16,2,1024]{2,1,0:T(2,128)(2,1)}), bf16[16,2,1024]{2,1,0:T(2,128)(2,1)S(1)}, u32[]{:S(2)}, u32[]{:S(2)}) %all-to-all-start) | async-done | bytes 65568 | tf_op jit(solution)/shard_map/all_to_all | solution.py:45
  17.0 1.1 fusion.25
  18.1 1.5 fusion.24
  19.6 0.1 collective-permute-start
  19.7 0.6 gather_fusion
  20.4 0.6 collective-permute-done
  21.0 2.0 %collective-permute-start.1 = (f32[32,640]{1,0:T(8,128)S(1)}, f32[32,640]{1,0:T(8,128)S(1)}, u32[]{:S(2)}, u32[]{:S(2)}) collective-permute-start(f32[32,640]{1,0:T(8,128)S(1)} %fusion.22), channel_id=1, source_target_pairs={{0,32},{16,48},{32,0},{48,16},{64,96},{80,112},{96,64},{112,80},{1... | collective-permute-start | bytes 245768 | tf_op jit(solution)/shard_map/ppermute | solution.py:51
  23.0 1.3 compare_reduce_fusion
  24.3 1.4 collective-permute-done.1
  25.7 3.8 %collective-permute-start.2 = (f32[32,640]{1,0:T(8,128)S(1)}, f32[32,640]{1,0:T(8,128)S(1)}, u32[]{:S(2)}, u32[]{:S(2)}) collective-permute-start(f32[32,640]{1,0:T(8,128)S(1)} %add.112), channel_id=1, source_target_pairs={{0,64},{16,80},{32,96},{48,112},{64,0},{80,16},{96,32},{112,48},{1... | collective-permute-start | bytes 245768 | tf_op jit(solution)/shard_map/ppermute | solution.py:51
  29.6 2.3 %collective-permute-done.2 = f32[32,640]{1,0:T(8,128)S(1)} collective-permute-done((f32[32,640]{1,0:T(8,128)S(1)}, f32[32,640]{1,0:T(8,128)S(1)}, u32[]{:S(2)}, u32[]{:S(2)}) %collective-permute-start.2) | collective-permute-done | bytes 81952 | tf_op jit(solution)/shard_map/ppermute | solution.py:51
  32.0 0.1 subtract_convert_fusion
  32.1 0.1 pad_maximum_fusion.1
  32.2 0.8 broadcast_in_dim.132
  33.1 3.8 %all-to-all-start.1 = ((bf16[16,32,512]{2,1,0:T(8,128)(2,1)}), bf16[16,32,512]{2,1,0:T(8,128)(2,1)S(1)}, u32[]{:S(2)}, u32[]{:S(2)}) async-start(bf16[16,32,512]{2,1,0:T(8,128)(2,1)} %broadcast_in_dim.132), calls=%async_computation.1 | async-start | bytes 1048576 | tf_op jit(solution)/shard_map/all_to_all | solution.py:45
  36.9 0.1 copy.60
  37.0 2.7 %copy.63 = pred[64,64,1]{2,1,0:T(8,128)(4,1)} copy(pred[64,64,1]{0,1,2:T(8,128)(4,1)S(1)} %get-tuple-element.15) | data formatting | bytes 8192 | tf_op jit(solution)/shard_map/jit(_where)/broadcast_in_dim | solution.py:155
  39.7 7.3 %all-to-all-done.1 = bf16[16,32,512]{2,1,0:T(8,128)(2,1)S(1)} async-done(((bf16[16,32,512]{2,1,0:T(8,128)(2,1)}), bf16[16,32,512]{2,1,0:T(8,128)(2,1)S(1)}, u32[]{:S(2)}, u32[]{:S(2)}) %all-to-all-start.1) | async-done | bytes 524320 | tf_op jit(solution)/shard_map/all_to_all | solution.py:45
  47.0 0.1 reshape.270
  47.1 0.6 copy.61
  47.7 0.7 gather_fusion.1
  48.5 1.3 copy.97
  49.8 27.9 %shard_map.86 = (f32[64,64,128]{2,1,0:T(8,128)}, f32[64,64,1]{2,1,0:T(8,128)}, f32[64,64,1]{2,1,0:T(8,128)}) custom-call(bf16[64,64,128]{2,1,0:T(8,128)(2,1)} %bitcast.93, bf16[64,64,2048]{2,1,0:T(8,128)(2,1)} %kv_ref.1), custom_call_target="tpu_custom_call" | custom-call | tf_op jit(solution)/shard_map/pallas_call | solution.py:86
  77.7 2.4 %reduce.1 = f32[64,64]{1,0:T(8,128)S(1)} reduce(f32[64,64,1]{2,1,0:T(8,128)} %get-tuple-element.6, f32[]{:T(128)} %constant.111), dimensions={2}, to_apply=%get-tuple-element.6.reduce_sub_computation | reduce | bytes 32772 | tf_op jit(solution)/shard_map/pallas_call | solution.py:86
  80.0 0.4 select_reduce_fusion.1
  80.4 0.2 copy-done.7
  80.6 0.6 gather_fusion.2
  81.2 0.2 concatenate.23
  81.4 1.2 reduce.3
  82.6 0.8 multiply_bitcast_fusion
  83.4 0.7 copy.68
  84.1 4.2 %copy.71 = f32[8,4,16,4,1]{4,0,3,2,1:T(8,128)} copy(f32[8,4,16,4,1]{3,2,1,0,4:T(8,128)S(1)} %concatenate.23) | data formatting | bytes 16384 | tf_op jit(solution)/shard_map/concatenate | solution.py:170
  88.3 1.0 convolution_bitcast_fusion
  89.4 1.9 %copy.70 = f32[8,4,16,4,1]{4,0,3,2,1:T(8,128)} copy(f32[8,4,16,4,1]{2,0,4,3,1:T(8,128)S(1)} %convolution_bitcast_fusion) | data formatting | bytes 16384 | tf_op jit(solution)/shard_map/dot_general | solution.py:163
  91.3 2.0 %copy.65 = f32[64,64,1]{2,1,0:T(8,128)} copy(f32[64,64,1]{1,0,2:T(8,128)S(1)} %bitcast.96) | data formatting | bytes 32768 | tf_op jit(solution)/shard_map/gather | solution.py:162
  93.3 2.4 %exponential_reduce_fusion = f32[64,64]{1,0:T(8,128)S(1)} fusion(f32[64,64,1]{2,1,0:T(8,128)} %copy.65, pred[64,64,1]{2,1,0:T(8,128)(4,1)} %copy.63, f32[64,64,1]{2,1,0:T(8,128)S(1)} %copy-done.1), kind=kLoop, calls=%fused_computation.8 | loop fusion | flops 8192 | bytes 53248 | tf_op jit(solution)/shard_map/exp | solution.py:162
  95.8 1.4 select_multiply_fusion
  97.2 2.5 %copy.96 = f32[8,8,64,128]{3,1,2,0:T(8,128)} copy(f32[8,8,64,128]{3,2,1,0:T(8,128)S(1)} %bitcast.90) | data formatting | bytes 4194304
  99.7 2.9 %dot_general.28 = f32[16,4,128,64]{2,1,0,3:T(4,128)S(1)} reshape(f32[8192,64]{0,1:T(8,128)} %bitcast.91) | data formatting | bytes 4194304 | tf_op jit(solution)/shard_map/dot_general | solution.py:164
  102.6 2.1 %fusion = f32[8,4,16,4,128]{4,0,3,2,1:T(8,128)S(1)} fusion(f32[16,4,128,64]{2,1,0,3:T(4,128)S(1)} %dot_general.28, s32[64]{0:T(128)S(1)} %get-tuple-element.17, s32[8,4]{0,1:T(4,128)S(1)} %multiply_add_fusion), kind=kOutput, calls=%fused_computation.5 | convolution fusion | flops 201328640 | bytes 3146112 | tf_op jit(solution)/shard_map/dot_general | solution.py:164
  104.8 0.4 maximum_bitcast_fusion
  105.2 0.8 copy.72
  106.0 4.4 %all_to_all.24 = f32[128,1,2080]{2,1,0:T(1,128)} reshape(f32[8,16,4,4,130]{4,3,2,1,0:T(4,128)S(1)} %copy.72) | data formatting | bytes 2129920 | tf_op jit(solution)/shard_map/all_to_all | solution.py:174
  110.3 6.9 %all-to-all-start.2 = ((f32[128,1,2080]{2,1,0:T(1,128)}), f32[128,1,2080]{2,1,0:T(1,128)S(1)}, u32[]{:S(2)}, u32[]{:S(2)}) async-start(f32[128,1,2080]{2,1,0:T(1,128)} %all_to_all.24), calls=%async_computation.2 | async-start | bytes 2228224 | tf_op jit(solution)/shard_map/all_to_all | solution.py:174
  117.2 19.7 %all-to-all-done.2 = f32[128,1,2080]{2,1,0:T(1,128)S(1)} async-done(((f32[128,1,2080]{2,1,0:T(1,128)}), f32[128,1,2080]{2,1,0:T(1,128)S(1)}, u32[]{:S(2)}, u32[]{:S(2)}) %all-to-all-start.2) | async-done | bytes 1064992 | tf_op jit(solution)/shard_map/all_to_all | solution.py:174
  136.9 1.5 copy.74
  138.5 0.1 fusion.23
  138.6 0.1 subtract_exponential_fusion
  138.7 0.4 fusion.3
  139.1 0.2 multiply_reduce_fusion
  139.2 0.1 fusion.13
  139.3 0.6 broadcast_in_dim.141
  139.9 3.3 %all-to-all-start.3 = ((bf16[8,4,512]{2,1,0:T(4,128)(2,1)}), bf16[8,4,512]{2,1,0:T(4,128)(2,1)S(1)}, u32[]{:S(2)}, u32[]{:S(2)}) async-start(bf16[8,4,512]{2,1,0:T(4,128)(2,1)} %broadcast_in_dim.141), calls=%async_computation.3 | async-start | bytes 65536 | tf_op jit(solution)/shard_map/all_to_all | solution.py:45
  143.3 5.4 %all-to-all-done.3 = bf16[8,4,512]{2,1,0:T(4,128)(2,1)S(1)} async-done(((bf16[8,4,512]{2,1,0:T(4,128)(2,1)}), bf16[8,4,512]{2,1,0:T(4,128)(2,1)S(1)}, u32[]{:S(2)}, u32[]{:S(2)}) %all-to-all-start.3) | async-done | bytes 32800 | tf_op jit(solution)/shard_map/all_to_all | solution.py:45
  148.7 0.3 fusion.4
  149.0 0.8 copy.76
  149.7 3.5 %all-to-all-start.4 = ((f32[16,2,1024]{2,1,0:T(2,128)}), f32[16,2,1024]{2,1,0:T(2,128)S(1)}, u32[]{:S(2)}, u32[]{:S(2)}) async-start(f32[16,2,1024]{2,1,0:T(2,128)} %copy.76), calls=%async_computation.4 | async-start | bytes 262144 | tf_op jit(solution)/shard_map/all_to_all | solution.py:187
  153.3 0.1 subtract_bitcast_fusion
  153.3 0.6 fusion.17
  154.0 7.0 %all-to-all-done.4 = f32[16,2,1024]{2,1,0:T(2,128)S(1)} async-done(((f32[16,2,1024]{2,1,0:T(2,128)}), f32[16,2,1024]{2,1,0:T(2,128)S(1)}, u32[]{:S(2)}, u32[]{:S(2)}) %all-to-all-start.4) | async-done | bytes 131104 | tf_op jit(solution)/shard_map/all_to_all | solution.py:187
  161.0 0.6 reduce_sum.42
  (46 shorter events, 0.5 us)
Async XLA Ops:
  0.6 148.0 %copy-start = (bf16[512,1024]{1,0:T(8,128)(2,1)S(1)}, bf16[512,1024]{1,0:T(8,128)(2,1)}, u32[]{:S(2)}) copy-start(bf16[512,1024]{1,0:T(8,128)(2,1)} %param.10) | copy-start | bytes 3145732
  0.6 19.1 %copy-start.6 = (s32[1,32,8,32]{3,2,1,0:T(8,128)S(1)}, s32[1,32,8,32]{3,2,1,0:T(8,128)}, u32[]{:S(2)}) copy-start(s32[1,32,8,32]{3,2,1,0:T(8,128)} %param.13) | copy-start | bytes 98308
  2.1 14.8 %all-to-all-start = ((bf16[16,2,1024]{2,1,0:T(2,128)(2,1)}), bf16[16,2,1024]{2,1,0:T(2,128)(2,1)S(1)}, u32[]{:S(2)}, u32[]{:S(2)}) async-start(bf16[16,2,1024]{2,1,0:T(2,128)(2,1)} %broadcast_in_dim.131), calls=%async_computation | async-start | bytes 131072 | tf_op jit(solution)/shard_map/all_to_all | solution.py:45
  19.6 1.4 collective-permute-start
  21.0 4.8 %collective-permute-start.1 = (f32[32,640]{1,0:T(8,128)S(1)}, f32[32,640]{1,0:T(8,128)S(1)}, u32[]{:S(2)}, u32[]{:S(2)}) collective-permute-start(f32[32,640]{1,0:T(8,128)S(1)} %fusion.22), channel_id=1, source_target_pairs={{0,32},{16,48},{32,0},{48,16},{64,96},{80,112},{96,64},{112,80},{1... | collective-permute-start | bytes 245768 | tf_op jit(solution)/shard_map/ppermute | solution.py:51
  25.7 6.2 %collective-permute-start.2 = (f32[32,640]{1,0:T(8,128)S(1)}, f32[32,640]{1,0:T(8,128)S(1)}, u32[]{:S(2)}, u32[]{:S(2)}) collective-permute-start(f32[32,640]{1,0:T(8,128)S(1)} %add.112), channel_id=1, source_target_pairs={{0,64},{16,80},{32,96},{48,112},{64,0},{80,16},{96,32},{112,48},{1... | collective-permute-start | bytes 245768 | tf_op jit(solution)/shard_map/ppermute | solution.py:51
  29.6 3.5 %copy-start.8 = (f32[64]{0:T(128)}, f32[64]{0:T(128)S(1)}, u32[]{:S(2)}) copy-start(f32[64]{0:T(128)S(1)} %get-tuple-element.19) | copy-start | bytes 772
  29.6 3.5 %copy-start.10 = (f32[64]{0:T(128)}, f32[64]{0:T(128)S(1)}, u32[]{:S(2)}) copy-start(f32[64]{0:T(128)S(1)} %get-tuple-element.20) | copy-start | bytes 772
  33.1 13.9 %all-to-all-start.1 = ((bf16[16,32,512]{2,1,0:T(8,128)(2,1)}), bf16[16,32,512]{2,1,0:T(8,128)(2,1)S(1)}, u32[]{:S(2)}, u32[]{:S(2)}) async-start(bf16[16,32,512]{2,1,0:T(8,128)(2,1)} %broadcast_in_dim.132), calls=%async_computation.1 | async-start | bytes 1048576 | tf_op jit(solution)/shard_map/all_to_all | solution.py:45
  77.7 3.7 %copy-start.4 = (f32[64,64,1]{2,1,0:T(8,128)S(1)}, f32[64,64,1]{2,1,0:T(8,128)}, u32[]{:S(2)}) copy-start(f32[64,64,1]{2,1,0:T(8,128)} %get-tuple-element.7) | copy-start | bytes 49156
  80.0 0.6 copy-start.7
  84.1 9.2 %copy-start.1 = (f32[64,64,1]{2,1,0:T(8,128)S(1)}, f32[64,64,1]{2,1,0:T(8,128)}, u32[]{:S(2)}) copy-start(f32[64,64,1]{2,1,0:T(8,128)} %get-tuple-element.6) | copy-start | bytes 49156
  93.3 2.5 %copy-start.5 = (f32[64,64,128]{2,1,0:T(8,128)S(1)}, f32[64,64,128]{2,1,0:T(8,128)}, u32[]{:S(2)}) copy-start(f32[64,64,128]{2,1,0:T(8,128)} %get-tuple-element.5) | copy-start | bytes 6291460
  102.6 2.1 %copy-start.2 = (f32[8,4,16,4,1]{4,0,3,2,1:T(8,128)S(1)}, f32[8,4,16,4,1]{4,0,3,2,1:T(8,128)}, u32[]{:S(2)}) copy-start(f32[8,4,16,4,1]{4,0,3,2,1:T(8,128)} %copy.71) | copy-start | bytes 24580
  102.6 2.1 %copy-start.3 = (f32[8,4,16,4,1]{4,0,3,2,1:T(8,128)S(1)}, f32[8,4,16,4,1]{4,0,3,2,1:T(8,128)}, u32[]{:S(2)}) copy-start(f32[8,4,16,4,1]{4,0,3,2,1:T(8,128)} %copy.70) | copy-start | bytes 24580
  110.3 26.6 %all-to-all-start.2 = ((f32[128,1,2080]{2,1,0:T(1,128)}), f32[128,1,2080]{2,1,0:T(1,128)S(1)}, u32[]{:S(2)}, u32[]{:S(2)}) async-start(f32[128,1,2080]{2,1,0:T(1,128)} %all_to_all.24), calls=%async_computation.2 | async-start | bytes 2228224 | tf_op jit(solution)/shard_map/all_to_all | solution.py:174
  138.5 14.8 %copy-start.9 = (f32[64]{0:T(128)S(1)}, f32[64]{0:T(128)}, u32[]{:S(2)}) copy-start(f32[64]{0:T(128)} %copy-done.8) | copy-start | bytes 772
  138.5 14.8 %copy-start.11 = (f32[64]{0:T(128)S(1)}, f32[64]{0:T(128)}, u32[]{:S(2)}) copy-start(f32[64]{0:T(128)} %copy-done.10) | copy-start | bytes 772
  139.9 8.7 %all-to-all-start.3 = ((bf16[8,4,512]{2,1,0:T(4,128)(2,1)}), bf16[8,4,512]{2,1,0:T(4,128)(2,1)S(1)}, u32[]{:S(2)}, u32[]{:S(2)}) async-start(bf16[8,4,512]{2,1,0:T(4,128)(2,1)} %broadcast_in_dim.141), calls=%async_computation.3 | async-start | bytes 65536 | tf_op jit(solution)/shard_map/all_to_all | solution.py:45
  149.7 11.3 %all-to-all-start.4 = ((f32[16,2,1024]{2,1,0:T(2,128)}), f32[16,2,1024]{2,1,0:T(2,128)S(1)}, u32[]{:S(2)}, u32[]{:S(2)}) async-start(f32[16,2,1024]{2,1,0:T(2,128)} %copy.76), calls=%async_computation.4 | async-start | bytes 262144 | tf_op jit(solution)/shard_map/all_to_all | solution.py:187

commit v3 on v1

--- a/solution.py
+++ b/solution.py
@@ -3,6 +3,8 @@
 import jax
 import jax.numpy as jnp
 from jax import lax
+from jax.experimental import pallas as pl
+from jax.experimental.pallas import tpu as pltpu
 from jax.sharding import PartitionSpec as P
 
 H = 64
@@ -52,6 +54,59 @@
     return x
 
 
+def merge_kernel(seq_ref, pick_ref, q_ref, kv_ref, acc_ref, tot_ref, max_ref):
+    block = kv_ref.shape[0]
+    step = pl.program_id(0)
+    scale = 1.0 / math.sqrt(HD)
+
+    @pl.when(step == 0)
+    def _init():
+        acc_ref[...] = jnp.zeros(acc_ref.shape, jnp.float32)
+        tot_ref[...] = jnp.zeros(tot_ref.shape, jnp.float32)
+        max_ref[...] = jnp.full(max_ref.shape, NEG_BIG, jnp.float32)
+
+    def body(j, carry):
+        slot = step * block + j
+        seq = seq_ref[slot]
+        for g in range(KVH):
+            @pl.when(pick_ref[slot * KVH + g] != 0)
+            def _page():
+                keys = kv_ref[j, :, pl.ds(g * 2 * HD, HD)]
+                vals = kv_ref[j, :, pl.ds(g * 2 * HD + HD, HD)]
+                sc = lax.dot_general(q_ref[seq, g], keys, (((1,), (1,)), ((), ())),
+                                     preferred_element_type=jnp.float32) * scale
+                pm = jnp.max(sc, axis=1, keepdims=True)
+                wt = jnp.exp(sc - pm).astype(jnp.bfloat16)
+                pt = jnp.sum(wt.astype(jnp.float32), axis=1, keepdims=True)
+                pa = jnp.dot(wt, vals, preferred_element_type=jnp.float32)
+                m_old = max_ref[seq, g]
+                m_new = jnp.maximum(m_old, pm)
+                alpha = jnp.exp(m_old - m_new)
+                beta = jnp.exp(pm - m_new)
+                acc_ref[seq, g] = acc_ref[seq, g] * alpha + pa * beta
+                tot_ref[seq, g] = tot_ref[seq, g] * alpha + pt * beta
+                max_ref[seq, g] = m_new
+        return carry
+
+    lax.fori_loop(0, block, body, 0)
+
+def merge_pages(seq_of, picked, q_all, kv, block=8):
+    slots, tok, width = kv.shape
+    seqs = q_all.shape[0]
+    full = (seqs, KVH, H // KVH, HD)
+    grid_spec = pltpu.PrefetchScalarGridSpec(
+        num_scalar_prefetch=2,
+        grid=(slots // block,),
+        in_specs=[pl.BlockSpec(full, lambda i, s, p: (0, 0, 0, 0)),
+                  pl.BlockSpec((block, tok, width), lambda i, s, p: (i, 0, 0))],
+        out_specs=[pl.BlockSpec(full, lambda i, s, p: (0, 0, 0, 0))] * 3,
+    )
+    return pl.pallas_call(
+        merge_kernel, grid_spec=grid_spec,
+        out_shape=[jax.ShapeDtypeStruct(full, jnp.float32)] * 3,
+    )(seq_of, picked.reshape(-1).astype(jnp.int32), q_all, kv)
+
+
 def per_device(hidden_in, w_query, w_keyval, w_output, kv_pool, page_table, selected):
     n_page = lax.axis_size("page")
     n_tensor = lax.axis_size("tensor")
@@ -94,41 +149,11 @@
     q_all = gather_blocks(query, "tensor", n_tensor)
     q_all = q_all.reshape(KVH, n_tensor // KVH, seqs, local_heads, HD)
     q_all = q_all.transpose(2, 0, 1, 3, 4).reshape(seqs, KVH, groups, HD)
-    slot_query = q_all[seq_of]
 
-    maxes, totals, accs = [], [], []
-    for g in range(KVH):
-        base = g * 2 * HD
-        key_g = kv_pool[:, :, base:base + HD]
-        val_g = kv_pool[:, :, base + HD:base + 2 * HD]
-        sc = jnp.einsum(
-            "shd,std->sht", slot_query[:, g], key_g, preferred_element_type=jnp.float32
-        ) * scale
-        pm = jnp.max(sc, axis=-1)
-        wt = jnp.exp(sc - pm[..., None]).astype(jnp.bfloat16)
-        pt = jnp.sum(wt.astype(jnp.float32), axis=-1)
-        pa = jnp.einsum("sht,std->shd", wt, val_g, preferred_element_type=jnp.float32)
-        maxes.append(pm)
-        totals.append(pt)
-        accs.append(pa)
-    page_max = jnp.stack(maxes, axis=1)
-    page_total = jnp.stack(totals, axis=1)
-    page_acc = jnp.stack(accs, axis=1)
-    pick = picked[:, :, None]
-    page_max = jnp.where(pick, page_max, NEG_BIG).reshape(slots, H)
-    page_total = jnp.where(pick, page_total, 0.0).reshape(slots, H)
-    page_acc = jnp.where(pick[..., None], page_acc, 0.0).reshape(slots, H, HD)
-
-    owner_rows = jnp.arange(seqs, dtype=jnp.int32)[:, None] == seq_of[None, :]
-    owner_hot = owner_rows.astype(jnp.float32)
-    loc_max = jnp.max(jnp.where(owner_rows[:, :, None], page_max[None], NEG_BIG), axis=1)
-    factor = jnp.exp(page_max - loc_max[seq_of])
-    loc_total = jnp.dot(owner_hot, page_total * factor, precision=lax.Precision.HIGHEST)
-    loc_acc = jnp.dot(
-        owner_hot,
-        (page_acc * factor[..., None]).reshape(slots, H * HD),
-        precision=lax.Precision.HIGHEST,
-    ).reshape(seqs, H, HD)
+    loc_acc, loc_total, loc_max = merge_pages(seq_of, picked, q_all, kv_pool)
+    loc_acc = loc_acc.reshape(seqs, H, HD)
+    loc_total = loc_total[..., 0].reshape(seqs, H)
+    loc_max = loc_max[..., 0].reshape(seqs, H)
 
     packed = jnp.concatenate([loc_acc, loc_total[..., None], loc_max[..., None]], axis=-1)
     width = HD + 2

time: 178 us -> 150 us (0.84)
  matrix products: 44.2 us -> 2.92 us
  Pallas kernels: 0 us -> 28 us
  local copies, waits for them, and re-layouts: 33 us -> 22.6 us
  other arithmetic: 16.1 us -> 7.44 us
  starting transfers between devices: 30.5 us -> 35.4 us
    dot_general x18 -> x0, matrix products: 41.3 us -> none  [the longest x8 19.1 us: per_device(): jnp.einsum('sht,std->shd', wt, val_g, preferred_element_type=jnp.float32)]
    pallas_call x0 -> x1, Pallas kernels: none -> 28 us  [merge_pages(): pl.pallas_call(merge_kernel, grid_spec=grid_spec, out_shape=[jax.ShapeDty...]
    another operation x21 -> x0, local copies, waits for them, and re-layouts: 6.08 us -> none  [the longest x10 3.6 us: per_device(): page_max = jnp.stack(maxes, axis=1)]
    all_to_all x1, starting transfers between devices: 6.86 us -> 12 us  [per_device(): got = lax.all_to_all(packed, ('page', 'tensor'), 0, 0, tiled=True)]
    dot_general x2 -> x0, other arithmetic: 4.96 us -> none  [the longest x1 4.94 us: per_device(): jnp.dot(owner_hot, (page_acc * factor[..., None]).reshape(slots, H * HD),...]
    dot_general x3 -> x0, local copies, waits for them, and re-layouts: 4.71 us -> none  [the longest x1 2.67 us: per_device(): jnp.dot(owner_hot, (page_acc * factor[..., None]).reshape(slots, H * HD),...]
    concatenate x2 -> x4, local copies, waits for them, and re-layouts: 4.14 us -> 8.43 us  [per_device(): jnp.concatenate([loc_acc, loc_total[..., None], loc_max[..., None]], axis...]
    reduce_sum x8 -> x0, other arithmetic: 4.2 us -> none  [per_device(): pt = jnp.sum(wt.astype(jnp.float32), axis=-1)]
where the time goes in v3:
time: 150 us
  waiting for transfers between devices  52.8 us (35%)
  starting transfers between devices  35.4 us (24%)
  Pallas kernels  28 us (19%)
  local copies, waits for them, and re-layouts  22.6 us (15%)
  other arithmetic  7.44 us (5%)
  matrix products  2.92 us (2%)
    pallas_call x1, Pallas kernels, merge_pages(): pl.pallas_call(merge_kernel, grid_spec=grid_spec, out_shape=[jax.ShapeDty...  28 us
    all_to_all x3, waiting for transfers between devices, gather_blocks(): lax.all_to_all(jnp.broadcast_to(x[None], (n,) + x.shape), axis, 0, 0, til...  20.2 us
    all_to_all x1, waiting for transfers between devices, per_device(): got = lax.all_to_all(packed, ('page', 'tensor'), 0, 0, tiled=True)  19.7 us
    all_to_all x3, starting transfers between devices, gather_blocks(): lax.all_to_all(jnp.broadcast_to(x[None], (n,) + x.shape), axis, 0, 0, til...  14.1 us
    all_to_all x1, starting transfers between devices, per_device(): got = lax.all_to_all(packed, ('page', 'tensor'), 0, 0, tiled=True)  12 us
    concatenate x4, local copies, waits for them, and re-layouts, per_device(): jnp.concatenate([loc_acc, loc_total[..., None], loc_max[..., None]], axis...  8.43 us
    all_to_all x1, waiting for transfers between devices, per_device(): out = jnp.sum(lax.all_to_all(part_out, 'tensor', 0, 0, tiled=True), axis=0)  7.05 us
    ppermute x3, waiting for transfers between devices, butterfly_sum(): x = x + lax.ppermute(x, axis, [(i, i ^ d) for i in range(n)])  5.92 us
  transfers between devices with their start and end apart: 8, of which 8 were waited for; matrix products, arithmetic and copies ran while one was open for 3% of the time, Pallas kernels for 0%

profile of v3, /device:TPU:0, one launch (start us, length us, event | category | flops | bytes accessed | tf_op | source)
XLA Modules:
  0.0 150.2 jit_solution(4570379352488796650)
XLA Ops:
  0.6 0.0 copy-start
  0.6 0.0 copy-start.3
  0.7 1.4 broadcast_in_dim.35
  2.1 7.1 %all-to-all-start = ((bf16[16,2,1024]{2,1,0:T(2,128)(2,1)}), bf16[16,2,1024]{2,1,0:T(2,128)(2,1)S(1)}, u32[]{:S(2)}, u32[]{:S(2)}) async-start(bf16[16,2,1024]{2,1,0:T(2,128)(2,1)} %broadcast_in_dim.35), calls=%async_computation | async-start | bytes 131072 | tf_op jit(solution)/shard_map/all_to_all | solution.py:46
  9.3 7.7 %all-to-all-done = bf16[16,2,1024]{2,1,0:T(2,128)(2,1)S(1)} async-done(((bf16[16,2,1024]{2,1,0:T(2,128)(2,1)}), bf16[16,2,1024]{2,1,0:T(2,128)(2,1)S(1)}, u32[]{:S(2)}, u32[]{:S(2)}) %all-to-all-start) | async-done | bytes 65568 | tf_op jit(solution)/shard_map/all_to_all | solution.py:46
  16.9 1.1 fusion.16
  18.0 0.0 copy-start.2
  18.1 1.5 %fusion.15 = f32[32,512]{1,0:T(8,128)S(1)} fusion(bf16[32,1024]{1,0:T(8,128)(2,1)S(1)} %reshape.164, bf16[1024,512]{1,0:T(8,128)(2,1)} %param.8), kind=kOutput, calls=%fused_computation.53 | convolution fusion | flops 33554432 | bytes 1179648 | tf_op jit(solution)/shard_map/dot_general | solution.py:138
  19.6 0.1 collective-permute-start
  19.7 1.3 collective-permute-done
  21.0 2.0 %collective-permute-start.1 = (f32[32,640]{1,0:T(8,128)S(1)}, f32[32,640]{1,0:T(8,128)S(1)}, u32[]{:S(2)}, u32[]{:S(2)}) collective-permute-start(f32[32,640]{1,0:T(8,128)S(1)} %fusion.13), channel_id=1, source_target_pairs={{0,32},{16,48},{32,0},{48,16},{64,96},{80,112},{96,64},{112,80},{1... | collective-permute-start | bytes 245768 | tf_op jit(solution)/shard_map/ppermute | solution.py:52
  23.0 0.0 copy-done.3
  23.0 0.4 select_reduce_fusion
  23.4 2.3 %collective-permute-done.1 = f32[32,640]{1,0:T(8,128)S(1)} collective-permute-done((f32[32,640]{1,0:T(8,128)S(1)}, f32[32,640]{1,0:T(8,128)S(1)}, u32[]{:S(2)}, u32[]{:S(2)}) %collective-permute-start.1) | collective-permute-done | bytes 81952 | tf_op jit(solution)/shard_map/ppermute | solution.py:52
  25.8 3.8 %collective-permute-start.2 = (f32[32,640]{1,0:T(8,128)S(1)}, f32[32,640]{1,0:T(8,128)S(1)}, u32[]{:S(2)}, u32[]{:S(2)}) collective-permute-start(f32[32,640]{1,0:T(8,128)S(1)} %add.105), channel_id=1, source_target_pairs={{0,64},{16,80},{32,96},{48,112},{64,0},{80,16},{96,32},{112,48},{1... | collective-permute-start | bytes 245768 | tf_op jit(solution)/shard_map/ppermute | solution.py:52
  29.6 0.1 fusion.11
  29.6 2.4 %collective-permute-done.2 = f32[32,640]{1,0:T(8,128)S(1)} collective-permute-done((f32[32,640]{1,0:T(8,128)S(1)}, f32[32,640]{1,0:T(8,128)S(1)}, u32[]{:S(2)}, u32[]{:S(2)}) %collective-permute-start.2) | collective-permute-done | bytes 81952 | tf_op jit(solution)/shard_map/ppermute | solution.py:52
  32.0 0.1 subtract_convert_fusion
  32.1 0.1 pad_maximum_fusion.1
  32.3 0.8 broadcast_in_dim.36
  33.1 3.6 %all-to-all-start.1 = ((bf16[16,32,512]{2,1,0:T(8,128)(2,1)}), bf16[16,32,512]{2,1,0:T(8,128)(2,1)S(1)}, u32[]{:S(2)}, u32[]{:S(2)}) async-start(bf16[16,32,512]{2,1,0:T(8,128)(2,1)} %broadcast_in_dim.36), calls=%async_computation.1 | async-start | bytes 1048576 | tf_op jit(solution)/shard_map/all_to_all | solution.py:46
  36.7 0.0 copy-done.2
  36.7 0.6 gather_fusion
  37.4 0.5 and_select_fusion.1
  37.9 1.3 compare_reduce_fusion
  39.2 0.7 reshape.170.pick_ref
  39.8 7.2 %all-to-all-done.1 = bf16[16,32,512]{2,1,0:T(8,128)(2,1)S(1)} async-done(((bf16[16,32,512]{2,1,0:T(8,128)(2,1)}), bf16[16,32,512]{2,1,0:T(8,128)(2,1)S(1)}, u32[]{:S(2)}, u32[]{:S(2)}) %all-to-all-start.1) | async-done | bytes 524320 | tf_op jit(solution)/shard_map/all_to_all | solution.py:46
  47.0 0.1 reshape.166
  47.1 1.1 copy.29
  48.2 28.0 %shard_map.86 = (f32[32,8,8,128]{3,2,1,0:T(8,128)}, f32[32,8,8,128]{3,2,1,0:T(8,128)}, f32[32,8,8,128]{3,2,1,0:T(8,128)}) custom-call(s32[64]{0:T(128)} %get-tuple-element.16.seq_ref, s32[512]{0:T(512)} %reshape.170.pick_ref, bf16[32,8,8,128]{3,2,1,0:T(8,128)(2,1)} %bitcast.54, bf16[64,64,2048]{2,1,0:T(8,128)(2,1)} %kv_ref.1), custom_call_target="tpu_custom_call" | custom-call | tf_op jit(solution)/shard_map/pallas_call | solution.py:104
  76.2 0.0 copy-start.1
  76.2 1.7 %slice_reduce_fusion.1 = f32[32,8,8]{2,1,0:T(8,128)S(1)} fusion(f32[32,8,8,128]{3,2,1,0:T(8,128)} %get-tuple-element.6), kind=kLoop, calls=%fused_computation.8 | loop fusion | bytes 16384 | tf_op jit(solution)/shard_map/slice | solution.py:155
  77.9 0.1 reshape.180
  78.0 0.0 copy-done.1
  78.0 0.3 slice_reduce_fusion
  78.3 0.1 reshape.181
  78.4 4.1 %copy.34 = f32[8,4,16,4,1]{4,3,1,2,0:T(4,128)} copy(f32[8,4,16,4,1]{3,2,1,0,4:T(8,128)S(1)} %reshape.181) | data formatting | bytes 16384 | tf_op jit(solution)/shard_map/concatenate | solution.py:158
  82.6 4.1 %copy.33 = f32[8,4,16,4,1]{4,3,1,2,0:T(4,128)} copy(f32[8,4,16,4,1]{3,2,1,0,4:T(8,128)S(1)} %reshape.180) | data formatting | bytes 16384 | tf_op jit(solution)/shard_map/concatenate | solution.py:158
  86.7 2.7 %maximum_bitcast_fusion = f32[8,16,4,4,130]{4,3,2,1,0:T(4,128)S(1)} fusion(f32[8,4,16,4,1]{4,3,1,2,0:T(4,128)} %copy.34, f32[8,4,16,4,1]{4,3,1,2,0:T(4,128)} %copy.33, f32[8,4,16,4,128]{4,3,2,1,0:T(4,128)} %bitcast.55), kind=kLoop, calls=%fused_computation.1 | loop fusion | flops 532480 | bytes 2129920 | tf_op jit(solution)/shard_map/transpose | solution.py:161
  89.4 4.4 %all_to_all.24 = f32[128,1,2080]{2,1,0:T(1,128)} reshape(f32[8,16,4,4,130]{4,3,2,1,0:T(4,128)S(1)} %maximum_bitcast_fusion) | data formatting | bytes 2129920 | tf_op jit(solution)/shard_map/all_to_all | solution.py:162
  93.7 12.0 %all-to-all-start.2 = ((f32[128,1,2080]{2,1,0:T(1,128)}), f32[128,1,2080]{2,1,0:T(1,128)S(1)}, u32[]{:S(2)}, u32[]{:S(2)}) async-start(f32[128,1,2080]{2,1,0:T(1,128)} %all_to_all.24), calls=%async_computation.2 | async-start | bytes 2228224 | tf_op jit(solution)/shard_map/all_to_all | solution.py:162
  105.8 19.7 %all-to-all-done.2 = f32[128,1,2080]{2,1,0:T(1,128)S(1)} async-done(((f32[128,1,2080]{2,1,0:T(1,128)}), f32[128,1,2080]{2,1,0:T(1,128)S(1)}, u32[]{:S(2)}, u32[]{:S(2)}) %all-to-all-start.2) | async-done | bytes 1064992 | tf_op jit(solution)/shard_map/all_to_all | solution.py:162
  125.4 1.5 copy.36
  126.9 0.1 reshape.168
  127.0 0.1 fusion.14
  127.1 0.1 subtract_exponential_fusion
  127.2 0.4 fusion
  127.6 0.2 multiply_reduce_fusion
  127.7 0.1 fusion.4
  127.8 0.6 broadcast_in_dim.37
  128.4 3.3 %all-to-all-start.3 = ((bf16[8,4,512]{2,1,0:T(4,128)(2,1)}), bf16[8,4,512]{2,1,0:T(4,128)(2,1)S(1)}, u32[]{:S(2)}, u32[]{:S(2)}) async-start(bf16[8,4,512]{2,1,0:T(4,128)(2,1)} %broadcast_in_dim.37), calls=%async_computation.3 | async-start | bytes 65536 | tf_op jit(solution)/shard_map/all_to_all | solution.py:46
  131.8 5.4 %all-to-all-done.3 = bf16[8,4,512]{2,1,0:T(4,128)(2,1)S(1)} async-done(((bf16[8,4,512]{2,1,0:T(4,128)(2,1)}), bf16[8,4,512]{2,1,0:T(4,128)(2,1)S(1)}, u32[]{:S(2)}, u32[]{:S(2)}) %all-to-all-start.3) | async-done | bytes 32800 | tf_op jit(solution)/shard_map/all_to_all | solution.py:46
  137.2 0.0 copy-done
  137.2 0.3 fusion.1
  137.5 0.7 copy.38
  138.2 3.5 %all-to-all-start.4 = ((f32[16,2,1024]{2,1,0:T(2,128)}), f32[16,2,1024]{2,1,0:T(2,128)S(1)}, u32[]{:S(2)}, u32[]{:S(2)}) async-start(f32[16,2,1024]{2,1,0:T(2,128)} %copy.38), calls=%async_computation.4 | async-start | bytes 262144 | tf_op jit(solution)/shard_map/all_to_all | solution.py:175
  141.7 0.1 subtract_bitcast_fusion
  141.8 0.6 fusion.8
  142.5 7.0 %all-to-all-done.4 = f32[16,2,1024]{2,1,0:T(2,128)S(1)} async-done(((f32[16,2,1024]{2,1,0:T(2,128)}), f32[16,2,1024]{2,1,0:T(2,128)S(1)}, u32[]{:S(2)}, u32[]{:S(2)}) %all-to-all-start.4) | async-done | bytes 131104 | tf_op jit(solution)/shard_map/all_to_all | solution.py:175
  149.5 0.6 reduce_sum.42
  (16 shorter events, 0.2 us)
Async XLA Ops:
  0.6 136.5 %copy-start = (bf16[512,1024]{1,0:T(8,128)(2,1)S(1)}, bf16[512,1024]{1,0:T(8,128)(2,1)}, u32[]{:S(2)}) copy-start(bf16[512,1024]{1,0:T(8,128)(2,1)} %param.10) | copy-start | bytes 3145732
  0.6 22.4 %copy-start.3 = (s32[8192]{0:T(1024)S(1)}, s32[8192]{0:T(1024)}, u32[]{:S(2)}) copy-start(s32[8192]{0:T(1024)} %param.12) | copy-start | bytes 98308
  2.1 14.8 %all-to-all-start = ((bf16[16,2,1024]{2,1,0:T(2,128)(2,1)}), bf16[16,2,1024]{2,1,0:T(2,128)(2,1)S(1)}, u32[]{:S(2)}, u32[]{:S(2)}) async-start(bf16[16,2,1024]{2,1,0:T(2,128)(2,1)} %broadcast_in_dim.35), calls=%async_computation | async-start | bytes 131072 | tf_op jit(solution)/shard_map/all_to_all | solution.py:46
  18.0 18.7 %copy-start.2 = (s32[1,32,8,32]{3,2,1,0:T(8,128)S(1)}, s32[1,32,8,32]{3,2,1,0:T(8,128)}, u32[]{:S(2)}) copy-start(s32[1,32,8,32]{3,2,1,0:T(8,128)} %param.13) | copy-start | bytes 98308
  19.6 1.4 collective-permute-start
  21.0 4.8 %collective-permute-start.1 = (f32[32,640]{1,0:T(8,128)S(1)}, f32[32,640]{1,0:T(8,128)S(1)}, u32[]{:S(2)}, u32[]{:S(2)}) collective-permute-start(f32[32,640]{1,0:T(8,128)S(1)} %fusion.13), channel_id=1, source_target_pairs={{0,32},{16,48},{32,0},{48,16},{64,96},{80,112},{96,64},{112,80},{1... | collective-permute-start | bytes 245768 | tf_op jit(solution)/shard_map/ppermute | solution.py:52
  25.8 6.2 %collective-permute-start.2 = (f32[32,640]{1,0:T(8,128)S(1)}, f32[32,640]{1,0:T(8,128)S(1)}, u32[]{:S(2)}, u32[]{:S(2)}) collective-permute-start(f32[32,640]{1,0:T(8,128)S(1)} %add.105), channel_id=1, source_target_pairs={{0,64},{16,80},{32,96},{48,112},{64,0},{80,16},{96,32},{112,48},{1... | collective-permute-start | bytes 245768 | tf_op jit(solution)/shard_map/ppermute | solution.py:52
  33.1 13.9 %all-to-all-start.1 = ((bf16[16,32,512]{2,1,0:T(8,128)(2,1)}), bf16[16,32,512]{2,1,0:T(8,128)(2,1)S(1)}, u32[]{:S(2)}, u32[]{:S(2)}) async-start(bf16[16,32,512]{2,1,0:T(8,128)(2,1)} %broadcast_in_dim.36), calls=%async_computation.1 | async-start | bytes 1048576 | tf_op jit(solution)/shard_map/all_to_all | solution.py:46
  76.2 1.8 %copy-start.1 = (f32[32,8,8,128]{3,2,1,0:T(8,128)S(1)}, f32[32,8,8,128]{3,2,1,0:T(8,128)}, u32[]{:S(2)}) copy-start(f32[32,8,8,128]{3,2,1,0:T(8,128)} %get-tuple-element.7) | copy-start | bytes 3145732
  93.7 31.7 %all-to-all-start.2 = ((f32[128,1,2080]{2,1,0:T(1,128)}), f32[128,1,2080]{2,1,0:T(1,128)S(1)}, u32[]{:S(2)}, u32[]{:S(2)}) async-start(f32[128,1,2080]{2,1,0:T(1,128)} %all_to_all.24), calls=%async_computation.2 | async-start | bytes 2228224 | tf_op jit(solution)/shard_map/all_to_all | solution.py:162
  128.4 8.7 %all-to-all-start.3 = ((bf16[8,4,512]{2,1,0:T(4,128)(2,1)}), bf16[8,4,512]{2,1,0:T(4,128)(2,1)S(1)}, u32[]{:S(2)}, u32[]{:S(2)}) async-start(bf16[8,4,512]{2,1,0:T(4,128)(2,1)} %broadcast_in_dim.37), calls=%async_computation.3 | async-start | bytes 65536 | tf_op jit(solution)/shard_map/all_to_all | solution.py:46
  138.2 11.3 %all-to-all-start.4 = ((f32[16,2,1024]{2,1,0:T(2,128)}), f32[16,2,1024]{2,1,0:T(2,128)S(1)}, u32[]{:S(2)}, u32[]{:S(2)}) async-start(f32[16,2,1024]{2,1,0:T(2,128)} %copy.38), calls=%async_computation.4 | async-start | bytes 262144 | tf_op jit(solution)/shard_map/all_to_all | solution.py:175

commit v4 on v3

--- a/solution.py
+++ b/solution.py
@@ -54,56 +54,82 @@
     return x
 
 
-def merge_kernel(seq_ref, pick_ref, q_ref, kv_ref, acc_ref, tot_ref, max_ref):
-    block = kv_ref.shape[0]
-    step = pl.program_id(0)
+DEPTH = 8
+
+def merge_kernel(seq_ref, pick_ref, q_ref, kv_hbm, acc_ref, tot_ref, max_ref, order_ref, buf, sems):
+    pairs = pick_ref.shape[0]
     scale = 1.0 / math.sqrt(HD)
-
-    @pl.when(step == 0)
-    def _init():
-        acc_ref[...] = jnp.zeros(acc_ref.shape, jnp.float32)
-        tot_ref[...] = jnp.zeros(tot_ref.shape, jnp.float32)
-        max_ref[...] = jnp.full(max_ref.shape, NEG_BIG, jnp.float32)
-
-    def body(j, carry):
-        slot = step * block + j
+    acc_ref[...] = jnp.zeros(acc_ref.shape, jnp.float32)
+    tot_ref[...] = jnp.zeros(tot_ref.shape, jnp.float32)
+    max_ref[...] = jnp.full(max_ref.shape, NEG_BIG, jnp.float32)
+
+    def compact(i, n):
+        order_ref[n] = i
+        return n + pick_ref[i]
+
+    count = lax.fori_loop(0, pairs, compact, 0)
+
+    def copy_of(k):
+        e = order_ref[k]
+        slot = e // KVH
+        g = e % KVH
+        return pltpu.make_async_copy(
+            kv_hbm.at[slot, :, pl.ds(g * 2 * HD, 2 * HD)], buf.at[k % DEPTH], sems.at[k % DEPTH]
+        )
+
+    for k in range(DEPTH):
+        @pl.when(k < count)
+        def _start():
+            copy_of(k).start()
+
+    def body(k, carry):
+        e = order_ref[k]
+        slot = e // KVH
+        g = e % KVH
         seq = seq_ref[slot]
-        for g in range(KVH):
-            @pl.when(pick_ref[slot * KVH + g] != 0)
-            def _page():
-                keys = kv_ref[j, :, pl.ds(g * 2 * HD, HD)]
-                vals = kv_ref[j, :, pl.ds(g * 2 * HD + HD, HD)]
-                sc = lax.dot_general(q_ref[seq, g], keys, (((1,), (1,)), ((), ())),
-                                     preferred_element_type=jnp.float32) * scale
-                pm = jnp.max(sc, axis=1, keepdims=True)
-                wt = jnp.exp(sc - pm).astype(jnp.bfloat16)
-                pt = jnp.sum(wt.astype(jnp.float32), axis=1, keepdims=True)
-                pa = jnp.dot(wt, vals, preferred_element_type=jnp.float32)
-                m_old = max_ref[seq, g]
-                m_new = jnp.maximum(m_old, pm)
-                alpha = jnp.exp(m_old - m_new)
-                beta = jnp.exp(pm - m_new)
-                acc_ref[seq, g] = acc_ref[seq, g] * alpha + pa * beta
-                tot_ref[seq, g] = tot_ref[seq, g] * alpha + pt * beta
-                max_ref[seq, g] = m_new
+        copy_of(k).wait()
+        page = buf[k % DEPTH]
+        keys = page[:, :HD]
+        vals = page[:, HD:]
+        sc = lax.dot_general(q_ref[seq, g], keys, (((1,), (1,)), ((), ())),
+                             preferred_element_type=jnp.float32) * scale
+        pm = jnp.max(sc, axis=1, keepdims=True)
+        wt = jnp.exp(sc - pm).astype(jnp.bfloat16)
+        pt = jnp.sum(wt.astype(jnp.float32), axis=1, keepdims=True)
+        pa = jnp.dot(wt, vals, preferred_element_type=jnp.float32)
+
+        @pl.when(k + DEPTH < count)
+        def _next():
+            copy_of(k + DEPTH).start()
+
+        m_old = max_ref[seq, g]
+        m_new = jnp.maximum(m_old, pm)
+        alpha = jnp.exp(m_old - m_new)
+        beta = jnp.exp(pm - m_new)
+        acc_ref[seq, g] = acc_ref[seq, g] * alpha + pa * beta
+        tot_ref[seq, g] = tot_ref[seq, g] * alpha + pt * beta
+        max_ref[seq, g] = m_new
         return carry
 
-    lax.fori_loop(0, block, body, 0)
-
-def merge_pages(seq_of, picked, q_all, kv, block=8):
+    lax.fori_loop(0, count, body, 0)
+
+
+def merge_pages(seq_of, picked, q_all, kv):
     slots, tok, width = kv.shape
     seqs = q_all.shape[0]
     full = (seqs, KVH, H // KVH, HD)
-    grid_spec = pltpu.PrefetchScalarGridSpec(
-        num_scalar_prefetch=2,
-        grid=(slots // block,),
-        in_specs=[pl.BlockSpec(full, lambda i, s, p: (0, 0, 0, 0)),
-                  pl.BlockSpec((block, tok, width), lambda i, s, p: (i, 0, 0))],
-        out_specs=[pl.BlockSpec(full, lambda i, s, p: (0, 0, 0, 0))] * 3,
-    )
+    vmem = pl.BlockSpec(memory_space=pltpu.VMEM)
+    smem = pl.BlockSpec(memory_space=pltpu.SMEM)
     return pl.pallas_call(
-        merge_kernel, grid_spec=grid_spec,
+        merge_kernel,
+        in_specs=[smem, smem, vmem, pl.BlockSpec(memory_space=pl.ANY)],
+        out_specs=[vmem] * 3,
         out_shape=[jax.ShapeDtypeStruct(full, jnp.float32)] * 3,
+        scratch_shapes=[
+            pltpu.SMEM((slots * KVH,), jnp.int32),
+            pltpu.VMEM((DEPTH, tok, 2 * HD), kv.dtype),
+            pltpu.SemaphoreType.DMA((DEPTH,)),
+        ],
     )(seq_of, picked.reshape(-1).astype(jnp.int32), q_all, kv)
 
 

time: 150 us -> 150 us (level)
  Pallas kernels: 28 us -> 25 us
  starting transfers between devices: 35.4 us -> 37.8 us
    pallas_call x1, Pallas kernels: 28 us -> 25 us  [merge_pages(): pl.pallas_call(merge_kernel, in_specs=[smem, smem, vmem, pl.BlockSpec(mem...]
    all_to_all x1, starting transfers between devices: 12 us -> 14.4 us  [per_device(): got = lax.all_to_all(packed, ('page', 'tensor'), 0, 0, tiled=True)]
where the time goes in v4:
time: 150 us
  waiting for transfers between devices  52.8 us (35%)
  starting transfers between devices  37.8 us (25%)
  Pallas kernels  25 us (17%)
  local copies, waits for them, and re-layouts  22.6 us (15%)
  other arithmetic  7.44 us (5%)
  matrix products  2.92 us (2%)
    pallas_call x1, Pallas kernels, merge_pages(): pl.pallas_call(merge_kernel, in_specs=[smem, smem, vmem, pl.BlockSpec(mem...  25 us
    all_to_all x3, waiting for transfers between devices, gather_blocks(): lax.all_to_all(jnp.broadcast_to(x[None], (n,) + x.shape), axis, 0, 0, til...  20.2 us
    all_to_all x1, waiting for transfers between devices, per_device(): got = lax.all_to_all(packed, ('page', 'tensor'), 0, 0, tiled=True)  19.7 us
    all_to_all x1, starting transfers between devices, per_device(): got = lax.all_to_all(packed, ('page', 'tensor'), 0, 0, tiled=True)  14.4 us
    all_to_all x3, starting transfers between devices, gather_blocks(): lax.all_to_all(jnp.broadcast_to(x[None], (n,) + x.shape), axis, 0, 0, til...  14.1 us
    concatenate x4, local copies, waits for them, and re-layouts, per_device(): jnp.concatenate([loc_acc, loc_total[..., None], loc_max[..., None]], axis...  8.43 us
    all_to_all x1, waiting for transfers between devices, per_device(): out = jnp.sum(lax.all_to_all(part_out, 'tensor', 0, 0, tiled=True), axis=0)  7.05 us
    ppermute x3, waiting for transfers between devices, butterfly_sum(): x = x + lax.ppermute(x, axis, [(i, i ^ d) for i in range(n)])  5.92 us
  transfers between devices with their start and end apart: 8, of which 8 were waited for; matrix products, arithmetic and copies ran while one was open for 3% of the time, Pallas kernels for 0%

profile of v4, /device:TPU:0, one launch (start us, length us, event | category | flops | bytes accessed | tf_op | source)
XLA Modules:
  0.0 149.5 jit_solution(16052808204274137577)
XLA Ops:
  0.6 0.0 copy-start
  0.6 0.0 copy-start.3
  0.7 1.4 broadcast_in_dim.35
  2.1 7.1 %all-to-all-start = ((bf16[16,2,1024]{2,1,0:T(2,128)(2,1)}), bf16[16,2,1024]{2,1,0:T(2,128)(2,1)S(1)}, u32[]{:S(2)}, u32[]{:S(2)}) async-start(bf16[16,2,1024]{2,1,0:T(2,128)(2,1)} %broadcast_in_dim.35), calls=%async_computation | async-start | bytes 131072 | tf_op jit(solution)/shard_map/all_to_all | solution.py:46
  9.3 7.7 %all-to-all-done = bf16[16,2,1024]{2,1,0:T(2,128)(2,1)S(1)} async-done(((bf16[16,2,1024]{2,1,0:T(2,128)(2,1)}), bf16[16,2,1024]{2,1,0:T(2,128)(2,1)S(1)}, u32[]{:S(2)}, u32[]{:S(2)}) %all-to-all-start) | async-done | bytes 65568 | tf_op jit(solution)/shard_map/all_to_all | solution.py:46
  16.9 1.1 fusion.16
  18.0 0.0 copy-start.2
  18.1 1.5 %fusion.15 = f32[32,512]{1,0:T(8,128)S(1)} fusion(bf16[32,1024]{1,0:T(8,128)(2,1)S(1)} %reshape.164, bf16[1024,512]{1,0:T(8,128)(2,1)} %param.8), kind=kOutput, calls=%fused_computation.53 | convolution fusion | flops 33554432 | bytes 1179648 | tf_op jit(solution)/shard_map/dot_general | solution.py:164
  19.6 0.1 collective-permute-start
  19.7 1.3 collective-permute-done
  21.0 2.0 %collective-permute-start.1 = (f32[32,640]{1,0:T(8,128)S(1)}, f32[32,640]{1,0:T(8,128)S(1)}, u32[]{:S(2)}, u32[]{:S(2)}) collective-permute-start(f32[32,640]{1,0:T(8,128)S(1)} %fusion.13), channel_id=1, source_target_pairs={{0,32},{16,48},{32,0},{48,16},{64,96},{80,112},{96,64},{112,80},{1... | collective-permute-start | bytes 245768 | tf_op jit(solution)/shard_map/ppermute | solution.py:52
  23.0 0.0 copy-done.3
  23.0 0.4 select_reduce_fusion
  23.4 2.3 %collective-permute-done.1 = f32[32,640]{1,0:T(8,128)S(1)} collective-permute-done((f32[32,640]{1,0:T(8,128)S(1)}, f32[32,640]{1,0:T(8,128)S(1)}, u32[]{:S(2)}, u32[]{:S(2)}) %collective-permute-start.1) | collective-permute-done | bytes 81952 | tf_op jit(solution)/shard_map/ppermute | solution.py:52
  25.8 3.8 %collective-permute-start.2 = (f32[32,640]{1,0:T(8,128)S(1)}, f32[32,640]{1,0:T(8,128)S(1)}, u32[]{:S(2)}, u32[]{:S(2)}) collective-permute-start(f32[32,640]{1,0:T(8,128)S(1)} %add.105), channel_id=1, source_target_pairs={{0,64},{16,80},{32,96},{48,112},{64,0},{80,16},{96,32},{112,48},{1... | collective-permute-start | bytes 245768 | tf_op jit(solution)/shard_map/ppermute | solution.py:52
  29.6 0.1 fusion.11
  29.6 2.4 %collective-permute-done.2 = f32[32,640]{1,0:T(8,128)S(1)} collective-permute-done((f32[32,640]{1,0:T(8,128)S(1)}, f32[32,640]{1,0:T(8,128)S(1)}, u32[]{:S(2)}, u32[]{:S(2)}) %collective-permute-start.2) | collective-permute-done | bytes 81952 | tf_op jit(solution)/shard_map/ppermute | solution.py:52
  32.0 0.1 subtract_convert_fusion
  32.1 0.1 pad_maximum_fusion.1
  32.3 0.8 broadcast_in_dim.36
  33.1 3.6 %all-to-all-start.1 = ((bf16[16,32,512]{2,1,0:T(8,128)(2,1)}), bf16[16,32,512]{2,1,0:T(8,128)(2,1)S(1)}, u32[]{:S(2)}, u32[]{:S(2)}) async-start(bf16[16,32,512]{2,1,0:T(8,128)(2,1)} %broadcast_in_dim.36), calls=%async_computation.1 | async-start | bytes 1048576 | tf_op jit(solution)/shard_map/all_to_all | solution.py:46
  36.7 0.0 copy-done.2
  36.7 0.6 gather_fusion
  37.4 0.5 and_select_fusion.1
  37.9 1.3 compare_reduce_fusion
  39.2 0.7 reshape.170.pick_ref
  39.8 7.2 %all-to-all-done.1 = bf16[16,32,512]{2,1,0:T(8,128)(2,1)S(1)} async-done(((bf16[16,32,512]{2,1,0:T(8,128)(2,1)}), bf16[16,32,512]{2,1,0:T(8,128)(2,1)S(1)}, u32[]{:S(2)}, u32[]{:S(2)}) %all-to-all-start.1) | async-done | bytes 524320 | tf_op jit(solution)/shard_map/all_to_all | solution.py:46
  47.0 0.1 reshape.166
  47.1 1.1 copy.29
  48.2 25.0 %shard_map.86 = (f32[32,8,8,128]{3,2,1,0:T(8,128)}, f32[32,8,8,128]{3,2,1,0:T(8,128)}, f32[32,8,8,128]{3,2,1,0:T(8,128)}) custom-call(s32[64]{0:T(128)} %get-tuple-element.16.seq_ref, s32[512]{0:T(512)} %reshape.170.pick_ref, bf16[32,8,8,128]{3,2,1,0:T(8,128)(2,1)} %bitcast.54, bf16[64,64,2048]{2,1,0:T(8,128)(2,1)} %kv_hbm.1), custom_call_target="tpu_custom_call" | custom-call | tf_op jit(solution)/shard_map/pallas_call | solution.py:123
  73.2 0.0 copy-start.1
  73.2 1.7 %slice_reduce_fusion.1 = f32[32,8,8]{2,1,0:T(8,128)S(1)} fusion(f32[32,8,8,128]{3,2,1,0:T(8,128)} %get-tuple-element.6), kind=kLoop, calls=%fused_computation.8 | loop fusion | bytes 16384 | tf_op jit(solution)/shard_map/slice | solution.py:181
  74.9 0.1 reshape.180
  75.0 0.0 copy-done.1
  75.0 0.3 slice_reduce_fusion
  75.3 0.1 reshape.181
  75.4 4.1 %copy.34 = f32[8,4,16,4,1]{4,3,1,2,0:T(4,128)} copy(f32[8,4,16,4,1]{3,2,1,0,4:T(8,128)S(1)} %reshape.181) | data formatting | bytes 16384 | tf_op jit(solution)/shard_map/concatenate | solution.py:184
  79.6 4.1 %copy.33 = f32[8,4,16,4,1]{4,3,1,2,0:T(4,128)} copy(f32[8,4,16,4,1]{3,2,1,0,4:T(8,128)S(1)} %reshape.180) | data formatting | bytes 16384 | tf_op jit(solution)/shard_map/concatenate | solution.py:184
  83.7 2.7 %maximum_bitcast_fusion = f32[8,16,4,4,130]{4,3,2,1,0:T(4,128)S(1)} fusion(f32[8,4,16,4,1]{4,3,1,2,0:T(4,128)} %copy.34, f32[8,4,16,4,1]{4,3,1,2,0:T(4,128)} %copy.33, f32[8,4,16,4,128]{4,3,2,1,0:T(4,128)} %bitcast.55), kind=kLoop, calls=%fused_computation.1 | loop fusion | flops 532480 | bytes 2129920 | tf_op jit(solution)/shard_map/transpose | solution.py:187
  86.4 4.4 %all_to_all.24 = f32[128,1,2080]{2,1,0:T(1,128)} reshape(f32[8,16,4,4,130]{4,3,2,1,0:T(4,128)S(1)} %maximum_bitcast_fusion) | data formatting | bytes 2129920 | tf_op jit(solution)/shard_map/all_to_all | solution.py:188
  90.7 14.4 %all-to-all-start.2 = ((f32[128,1,2080]{2,1,0:T(1,128)}), f32[128,1,2080]{2,1,0:T(1,128)S(1)}, u32[]{:S(2)}, u32[]{:S(2)}) async-start(f32[128,1,2080]{2,1,0:T(1,128)} %all_to_all.24), calls=%async_computation.2 | async-start | bytes 2228224 | tf_op jit(solution)/shard_map/all_to_all | solution.py:188
  105.1 19.7 %all-to-all-done.2 = f32[128,1,2080]{2,1,0:T(1,128)S(1)} async-done(((f32[128,1,2080]{2,1,0:T(1,128)}), f32[128,1,2080]{2,1,0:T(1,128)S(1)}, u32[]{:S(2)}, u32[]{:S(2)}) %all-to-all-start.2) | async-done | bytes 1064992 | tf_op jit(solution)/shard_map/all_to_all | solution.py:188
  124.8 1.5 copy.36
  126.3 0.1 reshape.168
  126.4 0.1 fusion.14
  126.5 0.1 subtract_exponential_fusion
  126.6 0.4 fusion
  126.9 0.2 multiply_reduce_fusion
  127.1 0.1 fusion.4
  127.2 0.6 broadcast_in_dim.37
  127.8 3.3 %all-to-all-start.3 = ((bf16[8,4,512]{2,1,0:T(4,128)(2,1)}), bf16[8,4,512]{2,1,0:T(4,128)(2,1)S(1)}, u32[]{:S(2)}, u32[]{:S(2)}) async-start(bf16[8,4,512]{2,1,0:T(4,128)(2,1)} %broadcast_in_dim.37), calls=%async_computation.3 | async-start | bytes 65536 | tf_op jit(solution)/shard_map/all_to_all | solution.py:46
  131.2 5.4 %all-to-all-done.3 = bf16[8,4,512]{2,1,0:T(4,128)(2,1)S(1)} async-done(((bf16[8,4,512]{2,1,0:T(4,128)(2,1)}), bf16[8,4,512]{2,1,0:T(4,128)(2,1)S(1)}, u32[]{:S(2)}, u32[]{:S(2)}) %all-to-all-start.3) | async-done | bytes 32800 | tf_op jit(solution)/shard_map/all_to_all | solution.py:46
  136.5 0.0 copy-done
  136.5 0.3 fusion.1
  136.8 0.7 copy.38
  137.6 3.5 %all-to-all-start.4 = ((f32[16,2,1024]{2,1,0:T(2,128)}), f32[16,2,1024]{2,1,0:T(2,128)S(1)}, u32[]{:S(2)}, u32[]{:S(2)}) async-start(f32[16,2,1024]{2,1,0:T(2,128)} %copy.38), calls=%async_computation.4 | async-start | bytes 262144 | tf_op jit(solution)/shard_map/all_to_all | solution.py:201
  141.1 0.1 subtract_bitcast_fusion
  141.2 0.6 fusion.8
  141.8 7.0 %all-to-all-done.4 = f32[16,2,1024]{2,1,0:T(2,128)S(1)} async-done(((f32[16,2,1024]{2,1,0:T(2,128)}), f32[16,2,1024]{2,1,0:T(2,128)S(1)}, u32[]{:S(2)}, u32[]{:S(2)}) %all-to-all-start.4) | async-done | bytes 131104 | tf_op jit(solution)/shard_map/all_to_all | solution.py:201
  148.9 0.6 reduce_sum.42
  (16 shorter events, 0.2 us)
Async XLA Ops:
  0.6 135.9 %copy-start = (bf16[512,1024]{1,0:T(8,128)(2,1)S(1)}, bf16[512,1024]{1,0:T(8,128)(2,1)}, u32[]{:S(2)}) copy-start(bf16[512,1024]{1,0:T(8,128)(2,1)} %param.10) | copy-start | bytes 3145732
  0.6 22.4 %copy-start.3 = (s32[8192]{0:T(1024)S(1)}, s32[8192]{0:T(1024)}, u32[]{:S(2)}) copy-start(s32[8192]{0:T(1024)} %param.12) | copy-start | bytes 98308
  2.1 14.8 %all-to-all-start = ((bf16[16,2,1024]{2,1,0:T(2,128)(2,1)}), bf16[16,2,1024]{2,1,0:T(2,128)(2,1)S(1)}, u32[]{:S(2)}, u32[]{:S(2)}) async-start(bf16[16,2,1024]{2,1,0:T(2,128)(2,1)} %broadcast_in_dim.35), calls=%async_computation | async-start | bytes 131072 | tf_op jit(solution)/shard_map/all_to_all | solution.py:46
  18.0 18.7 %copy-start.2 = (s32[1,32,8,32]{3,2,1,0:T(8,128)S(1)}, s32[1,32,8,32]{3,2,1,0:T(8,128)}, u32[]{:S(2)}) copy-start(s32[1,32,8,32]{3,2,1,0:T(8,128)} %param.13) | copy-start | bytes 98308
  19.6 1.4 collective-permute-start
  21.0 4.8 %collective-permute-start.1 = (f32[32,640]{1,0:T(8,128)S(1)}, f32[32,640]{1,0:T(8,128)S(1)}, u32[]{:S(2)}, u32[]{:S(2)}) collective-permute-start(f32[32,640]{1,0:T(8,128)S(1)} %fusion.13), channel_id=1, source_target_pairs={{0,32},{16,48},{32,0},{48,16},{64,96},{80,112},{96,64},{112,80},{1... | collective-permute-start | bytes 245768 | tf_op jit(solution)/shard_map/ppermute | solution.py:52
  25.8 6.2 %collective-permute-start.2 = (f32[32,640]{1,0:T(8,128)S(1)}, f32[32,640]{1,0:T(8,128)S(1)}, u32[]{:S(2)}, u32[]{:S(2)}) collective-permute-start(f32[32,640]{1,0:T(8,128)S(1)} %add.105), channel_id=1, source_target_pairs={{0,64},{16,80},{32,96},{48,112},{64,0},{80,16},{96,32},{112,48},{1... | collective-permute-start | bytes 245768 | tf_op jit(solution)/shard_map/ppermute | solution.py:52
  33.1 13.9 %all-to-all-start.1 = ((bf16[16,32,512]{2,1,0:T(8,128)(2,1)}), bf16[16,32,512]{2,1,0:T(8,128)(2,1)S(1)}, u32[]{:S(2)}, u32[]{:S(2)}) async-start(bf16[16,32,512]{2,1,0:T(8,128)(2,1)} %broadcast_in_dim.36), calls=%async_computation.1 | async-start | bytes 1048576 | tf_op jit(solution)/shard_map/all_to_all | solution.py:46
  73.2 1.8 %copy-start.1 = (f32[32,8,8,128]{3,2,1,0:T(8,128)S(1)}, f32[32,8,8,128]{3,2,1,0:T(8,128)}, u32[]{:S(2)}) copy-start(f32[32,8,8,128]{3,2,1,0:T(8,128)} %get-tuple-element.7) | copy-start | bytes 3145732
  90.7 34.1 %all-to-all-start.2 = ((f32[128,1,2080]{2,1,0:T(1,128)}), f32[128,1,2080]{2,1,0:T(1,128)S(1)}, u32[]{:S(2)}, u32[]{:S(2)}) async-start(f32[128,1,2080]{2,1,0:T(1,128)} %all_to_all.24), calls=%async_computation.2 | async-start | bytes 2228224 | tf_op jit(solution)/shard_map/all_to_all | solution.py:188
  127.8 8.7 %all-to-all-start.3 = ((bf16[8,4,512]{2,1,0:T(4,128)(2,1)}), bf16[8,4,512]{2,1,0:T(4,128)(2,1)S(1)}, u32[]{:S(2)}, u32[]{:S(2)}) async-start(bf16[8,4,512]{2,1,0:T(4,128)(2,1)} %broadcast_in_dim.37), calls=%async_computation.3 | async-start | bytes 65536 | tf_op jit(solution)/shard_map/all_to_all | solution.py:46
  137.6 11.3 %all-to-all-start.4 = ((f32[16,2,1024]{2,1,0:T(2,128)}), f32[16,2,1024]{2,1,0:T(2,128)S(1)}, u32[]{:S(2)}, u32[]{:S(2)}) async-start(f32[16,2,1024]{2,1,0:T(2,128)} %copy.38), calls=%async_computation.4 | async-start | bytes 262144 | tf_op jit(solution)/shard_map/all_to_all | solution.py:201

commit v5 on v4

--- a/solution.py
+++ b/solution.py
@@ -55,6 +55,7 @@
 
 
 DEPTH = 8
+UNROLL = 4
 
 def merge_kernel(seq_ref, pick_ref, q_ref, kv_hbm, acc_ref, tot_ref, max_ref, order_ref, buf, sems):
     pairs = pick_ref.shape[0]
@@ -68,6 +69,13 @@
         return n + pick_ref[i]
 
     count = lax.fori_loop(0, pairs, compact, 0)
+    padded = (count + UNROLL - 1) // UNROLL * UNROLL
+
+    def pad(k, carry):
+        order_ref[k] = 0
+        return carry
+
+    lax.fori_loop(count, padded, pad, 0)
 
     def copy_of(k):
         e = order_ref[k]
@@ -78,40 +86,45 @@
         )
 
     for k in range(DEPTH):
-        @pl.when(k < count)
+        @pl.when(k < padded)
         def _start():
             copy_of(k).start()
 
-    def body(k, carry):
+    def attend(k):
         e = order_ref[k]
-        slot = e // KVH
         g = e % KVH
-        seq = seq_ref[slot]
+        seq = seq_ref[e // KVH]
         copy_of(k).wait()
         page = buf[k % DEPTH]
-        keys = page[:, :HD]
-        vals = page[:, HD:]
-        sc = lax.dot_general(q_ref[seq, g], keys, (((1,), (1,)), ((), ())),
+        sc = lax.dot_general(q_ref[seq, g], page[:, :HD], (((1,), (1,)), ((), ())),
                              preferred_element_type=jnp.float32) * scale
         pm = jnp.max(sc, axis=1, keepdims=True)
         wt = jnp.exp(sc - pm).astype(jnp.bfloat16)
         pt = jnp.sum(wt.astype(jnp.float32), axis=1, keepdims=True)
-        pa = jnp.dot(wt, vals, preferred_element_type=jnp.float32)
-
-        @pl.when(k + DEPTH < count)
-        def _next():
-            copy_of(k + DEPTH).start()
-
+        pa = jnp.dot(wt, page[:, HD:], preferred_element_type=jnp.float32)
+        return seq, g, pm, pt, pa
+
+    def update(seq, g, pm, pt, pa, live):
         m_old = max_ref[seq, g]
-        m_new = jnp.maximum(m_old, pm)
+        m_new = jnp.where(live, jnp.maximum(m_old, pm), m_old)
         alpha = jnp.exp(m_old - m_new)
-        beta = jnp.exp(pm - m_new)
+        beta = jnp.where(live, jnp.exp(pm - m_new), 0.0)
         acc_ref[seq, g] = acc_ref[seq, g] * alpha + pa * beta
         tot_ref[seq, g] = tot_ref[seq, g] * alpha + pt * beta
         max_ref[seq, g] = m_new
+
+    def body(step, carry):
+        ks = [step * UNROLL + u for u in range(UNROLL)]
+        done = [attend(k) for k in ks]
+        for k in ks:
+            @pl.when(k + DEPTH < padded)
+            def _next():
+                copy_of(k + DEPTH).start()
+        for k, res in zip(ks, done):
+            update(*res, k < count)
         return carry
 
-    lax.fori_loop(0, count, body, 0)
+    lax.fori_loop(0, padded // UNROLL, body, 0)
 
 
 def merge_pages(seq_of, picked, q_all, kv):

time: 150 us -> 150 us (level)
  Pallas kernels: 25 us -> 29.3 us
  starting transfers between devices: 37.8 us -> 33.7 us
    pallas_call x1, Pallas kernels: 25 us -> 29.3 us  [merge_pages(): pl.pallas_call(merge_kernel, in_specs=[smem, smem, vmem, pl.BlockSpec(mem...]
    all_to_all x1, starting transfers between devices: 14.4 us -> 10.3 us  [per_device(): got = lax.all_to_all(packed, ('page', 'tensor'), 0, 0, tiled=True)]
where the time goes in v5:
time: 150 us
  waiting for transfers between devices  52.8 us (35%)
  starting transfers between devices  33.7 us (22%)
  Pallas kernels  29.3 us (20%)
  local copies, waits for them, and re-layouts  22.6 us (15%)
  other arithmetic  7.44 us (5%)
  matrix products  2.92 us (2%)
    pallas_call x1, Pallas kernels, merge_pages(): pl.pallas_call(merge_kernel, in_specs=[smem, smem, vmem, pl.BlockSpec(mem...  29.3 us
    all_to_all x3, waiting for transfers between devices, gather_blocks(): lax.all_to_all(jnp.broadcast_to(x[None], (n,) + x.shape), axis, 0, 0, til...  20.2 us
    all_to_all x1, waiting for transfers between devices, per_device(): got = lax.all_to_all(packed, ('page', 'tensor'), 0, 0, tiled=True)  19.7 us
    all_to_all x3, starting transfers between devices, gather_blocks(): lax.all_to_all(jnp.broadcast_to(x[None], (n,) + x.shape), axis, 0, 0, til...  14.1 us
    all_to_all x1, starting transfers between devices, per_device(): got = lax.all_to_all(packed, ('page', 'tensor'), 0, 0, tiled=True)  10.3 us
    concatenate x4, local copies, waits for them, and re-layouts, per_device(): jnp.concatenate([loc_acc, loc_total[..., None], loc_max[..., None]], axis...  8.43 us
    all_to_all x1, waiting for transfers between devices, per_device(): out = jnp.sum(lax.all_to_all(part_out, 'tensor', 0, 0, tiled=True), axis=0)  7.05 us
    ppermute x3, waiting for transfers between devices, butterfly_sum(): x = x + lax.ppermute(x, axis, [(i, i ^ d) for i in range(n)])  5.92 us
  transfers between devices with their start and end apart: 8, of which 8 were waited for; matrix products, arithmetic and copies ran while one was open for 3% of the time, Pallas kernels for 0%

profile of v5, /device:TPU:0, one launch (start us, length us, event | category | flops | bytes accessed | tf_op | source)
XLA Modules:
  0.0 149.8 jit_solution(7647260423633771147)
XLA Ops:
  0.6 0.0 copy-start
  0.6 0.0 copy-start.3
  0.7 1.4 broadcast_in_dim.35
  2.1 7.1 %all-to-all-start = ((bf16[16,2,1024]{2,1,0:T(2,128)(2,1)}), bf16[16,2,1024]{2,1,0:T(2,128)(2,1)S(1)}, u32[]{:S(2)}, u32[]{:S(2)}) async-start(bf16[16,2,1024]{2,1,0:T(2,128)(2,1)} %broadcast_in_dim.35), calls=%async_computation | async-start | bytes 131072 | tf_op jit(solution)/shard_map/all_to_all | solution.py:46
  9.3 7.7 %all-to-all-done = bf16[16,2,1024]{2,1,0:T(2,128)(2,1)S(1)} async-done(((bf16[16,2,1024]{2,1,0:T(2,128)(2,1)}), bf16[16,2,1024]{2,1,0:T(2,128)(2,1)S(1)}, u32[]{:S(2)}, u32[]{:S(2)}) %all-to-all-start) | async-done | bytes 65568 | tf_op jit(solution)/shard_map/all_to_all | solution.py:46
  16.9 1.1 fusion.16
  18.0 0.0 copy-start.2
  18.1 1.5 %fusion.15 = f32[32,512]{1,0:T(8,128)S(1)} fusion(bf16[32,1024]{1,0:T(8,128)(2,1)S(1)} %reshape.164, bf16[1024,512]{1,0:T(8,128)(2,1)} %param.8), kind=kOutput, calls=%fused_computation.53 | convolution fusion | flops 33554432 | bytes 1179648 | tf_op jit(solution)/shard_map/dot_general | solution.py:177
  19.6 0.1 collective-permute-start
  19.7 1.3 collective-permute-done
  21.0 2.0 %collective-permute-start.1 = (f32[32,640]{1,0:T(8,128)S(1)}, f32[32,640]{1,0:T(8,128)S(1)}, u32[]{:S(2)}, u32[]{:S(2)}) collective-permute-start(f32[32,640]{1,0:T(8,128)S(1)} %fusion.13), channel_id=1, source_target_pairs={{0,32},{16,48},{32,0},{48,16},{64,96},{80,112},{96,64},{112,80},{1... | collective-permute-start | bytes 245768 | tf_op jit(solution)/shard_map/ppermute | solution.py:52
  23.0 0.0 copy-done.3
  23.0 0.4 select_reduce_fusion
  23.4 2.3 %collective-permute-done.1 = f32[32,640]{1,0:T(8,128)S(1)} collective-permute-done((f32[32,640]{1,0:T(8,128)S(1)}, f32[32,640]{1,0:T(8,128)S(1)}, u32[]{:S(2)}, u32[]{:S(2)}) %collective-permute-start.1) | collective-permute-done | bytes 81952 | tf_op jit(solution)/shard_map/ppermute | solution.py:52
  25.8 3.8 %collective-permute-start.2 = (f32[32,640]{1,0:T(8,128)S(1)}, f32[32,640]{1,0:T(8,128)S(1)}, u32[]{:S(2)}, u32[]{:S(2)}) collective-permute-start(f32[32,640]{1,0:T(8,128)S(1)} %add.105), channel_id=1, source_target_pairs={{0,64},{16,80},{32,96},{48,112},{64,0},{80,16},{96,32},{112,48},{1... | collective-permute-start | bytes 245768 | tf_op jit(solution)/shard_map/ppermute | solution.py:52
  29.6 0.1 fusion.11
  29.6 2.4 %collective-permute-done.2 = f32[32,640]{1,0:T(8,128)S(1)} collective-permute-done((f32[32,640]{1,0:T(8,128)S(1)}, f32[32,640]{1,0:T(8,128)S(1)}, u32[]{:S(2)}, u32[]{:S(2)}) %collective-permute-start.2) | collective-permute-done | bytes 81952 | tf_op jit(solution)/shard_map/ppermute | solution.py:52
  32.0 0.1 subtract_convert_fusion
  32.1 0.1 pad_maximum_fusion.1
  32.3 0.8 broadcast_in_dim.36
  33.1 3.6 %all-to-all-start.1 = ((bf16[16,32,512]{2,1,0:T(8,128)(2,1)}), bf16[16,32,512]{2,1,0:T(8,128)(2,1)S(1)}, u32[]{:S(2)}, u32[]{:S(2)}) async-start(bf16[16,32,512]{2,1,0:T(8,128)(2,1)} %broadcast_in_dim.36), calls=%async_computation.1 | async-start | bytes 1048576 | tf_op jit(solution)/shard_map/all_to_all | solution.py:46
  36.7 0.0 copy-done.2
  36.7 0.6 gather_fusion
  37.4 0.5 and_select_fusion.1
  37.9 1.3 compare_reduce_fusion
  39.2 0.7 reshape.170.pick_ref
  39.8 7.2 %all-to-all-done.1 = bf16[16,32,512]{2,1,0:T(8,128)(2,1)S(1)} async-done(((bf16[16,32,512]{2,1,0:T(8,128)(2,1)}), bf16[16,32,512]{2,1,0:T(8,128)(2,1)S(1)}, u32[]{:S(2)}, u32[]{:S(2)}) %all-to-all-start.1) | async-done | bytes 524320 | tf_op jit(solution)/shard_map/all_to_all | solution.py:46
  47.0 0.1 reshape.166
  47.1 1.1 copy.29
  48.2 29.3 %shard_map.86 = (f32[32,8,8,128]{3,2,1,0:T(8,128)}, f32[32,8,8,128]{3,2,1,0:T(8,128)}, f32[32,8,8,128]{3,2,1,0:T(8,128)}) custom-call(s32[64]{0:T(128)} %get-tuple-element.16.seq_ref, s32[512]{0:T(512)} %reshape.170.pick_ref, bf16[32,8,8,128]{3,2,1,0:T(8,128)(2,1)} %bitcast.54, bf16[64,64,2048]{2,1,0:T(8,128)(2,1)} %kv_hbm.1), custom_call_target="tpu_custom_call" | custom-call | tf_op jit(solution)/shard_map/pallas_call | solution.py:136
  77.5 0.0 copy-start.1
  77.5 1.7 %slice_reduce_fusion.1 = f32[32,8,8]{2,1,0:T(8,128)S(1)} fusion(f32[32,8,8,128]{3,2,1,0:T(8,128)} %get-tuple-element.6), kind=kLoop, calls=%fused_computation.8 | loop fusion | bytes 16384 | tf_op jit(solution)/shard_map/slice | solution.py:194
  79.2 0.1 reshape.180
  79.3 0.0 copy-done.1
  79.3 0.3 slice_reduce_fusion
  79.7 0.1 reshape.181
  79.8 4.1 %copy.34 = f32[8,4,16,4,1]{4,3,1,2,0:T(4,128)} copy(f32[8,4,16,4,1]{3,2,1,0,4:T(8,128)S(1)} %reshape.181) | data formatting | bytes 16384 | tf_op jit(solution)/shard_map/concatenate | solution.py:197
  83.9 4.1 %copy.33 = f32[8,4,16,4,1]{4,3,1,2,0:T(4,128)} copy(f32[8,4,16,4,1]{3,2,1,0,4:T(8,128)S(1)} %reshape.180) | data formatting | bytes 16384 | tf_op jit(solution)/shard_map/concatenate | solution.py:197
  88.0 2.7 %maximum_bitcast_fusion = f32[8,16,4,4,130]{4,3,2,1,0:T(4,128)S(1)} fusion(f32[8,4,16,4,1]{4,3,1,2,0:T(4,128)} %copy.34, f32[8,4,16,4,1]{4,3,1,2,0:T(4,128)} %copy.33, f32[8,4,16,4,128]{4,3,2,1,0:T(4,128)} %bitcast.55), kind=kLoop, calls=%fused_computation.1 | loop fusion | flops 532480 | bytes 2129920 | tf_op jit(solution)/shard_map/transpose | solution.py:200
  90.7 4.4 %all_to_all.24 = f32[128,1,2080]{2,1,0:T(1,128)} reshape(f32[8,16,4,4,130]{4,3,2,1,0:T(4,128)S(1)} %maximum_bitcast_fusion) | data formatting | bytes 2129920 | tf_op jit(solution)/shard_map/all_to_all | solution.py:201
  95.1 10.3 %all-to-all-start.2 = ((f32[128,1,2080]{2,1,0:T(1,128)}), f32[128,1,2080]{2,1,0:T(1,128)S(1)}, u32[]{:S(2)}, u32[]{:S(2)}) async-start(f32[128,1,2080]{2,1,0:T(1,128)} %all_to_all.24), calls=%async_computation.2 | async-start | bytes 2228224 | tf_op jit(solution)/shard_map/all_to_all | solution.py:201
  105.4 19.7 %all-to-all-done.2 = f32[128,1,2080]{2,1,0:T(1,128)S(1)} async-done(((f32[128,1,2080]{2,1,0:T(1,128)}), f32[128,1,2080]{2,1,0:T(1,128)S(1)}, u32[]{:S(2)}, u32[]{:S(2)}) %all-to-all-start.2) | async-done | bytes 1064992 | tf_op jit(solution)/shard_map/all_to_all | solution.py:201
  125.1 1.5 copy.36
  126.6 0.1 reshape.168
  126.6 0.1 fusion.14
  126.8 0.1 subtract_exponential_fusion
  126.9 0.4 fusion
  127.2 0.2 multiply_reduce_fusion
  127.4 0.1 fusion.4
  127.5 0.6 broadcast_in_dim.37
  128.1 3.3 %all-to-all-start.3 = ((bf16[8,4,512]{2,1,0:T(4,128)(2,1)}), bf16[8,4,512]{2,1,0:T(4,128)(2,1)S(1)}, u32[]{:S(2)}, u32[]{:S(2)}) async-start(bf16[8,4,512]{2,1,0:T(4,128)(2,1)} %broadcast_in_dim.37), calls=%async_computation.3 | async-start | bytes 65536 | tf_op jit(solution)/shard_map/all_to_all | solution.py:46
  131.4 5.4 %all-to-all-done.3 = bf16[8,4,512]{2,1,0:T(4,128)(2,1)S(1)} async-done(((bf16[8,4,512]{2,1,0:T(4,128)(2,1)}), bf16[8,4,512]{2,1,0:T(4,128)(2,1)S(1)}, u32[]{:S(2)}, u32[]{:S(2)}) %all-to-all-start.3) | async-done | bytes 32800 | tf_op jit(solution)/shard_map/all_to_all | solution.py:46
  136.8 0.0 copy-done
  136.8 0.3 fusion.1
  137.1 0.7 copy.38
  137.9 3.5 %all-to-all-start.4 = ((f32[16,2,1024]{2,1,0:T(2,128)}), f32[16,2,1024]{2,1,0:T(2,128)S(1)}, u32[]{:S(2)}, u32[]{:S(2)}) async-start(f32[16,2,1024]{2,1,0:T(2,128)} %copy.38), calls=%async_computation.4 | async-start | bytes 262144 | tf_op jit(solution)/shard_map/all_to_all | solution.py:214
  141.4 0.1 subtract_bitcast_fusion
  141.5 0.6 fusion.8
  142.1 7.0 %all-to-all-done.4 = f32[16,2,1024]{2,1,0:T(2,128)S(1)} async-done(((f32[16,2,1024]{2,1,0:T(2,128)}), f32[16,2,1024]{2,1,0:T(2,128)S(1)}, u32[]{:S(2)}, u32[]{:S(2)}) %all-to-all-start.4) | async-done | bytes 131104 | tf_op jit(solution)/shard_map/all_to_all | solution.py:214
  149.2 0.6 reduce_sum.42
  (16 shorter events, 0.2 us)
Async XLA Ops:
  0.6 136.2 %copy-start = (bf16[512,1024]{1,0:T(8,128)(2,1)S(1)}, bf16[512,1024]{1,0:T(8,128)(2,1)}, u32[]{:S(2)}) copy-start(bf16[512,1024]{1,0:T(8,128)(2,1)} %param.10) | copy-start | bytes 3145732
  0.6 22.4 %copy-start.3 = (s32[8192]{0:T(1024)S(1)}, s32[8192]{0:T(1024)}, u32[]{:S(2)}) copy-start(s32[8192]{0:T(1024)} %param.12) | copy-start | bytes 98308
  2.1 14.8 %all-to-all-start = ((bf16[16,2,1024]{2,1,0:T(2,128)(2,1)}), bf16[16,2,1024]{2,1,0:T(2,128)(2,1)S(1)}, u32[]{:S(2)}, u32[]{:S(2)}) async-start(bf16[16,2,1024]{2,1,0:T(2,128)(2,1)} %broadcast_in_dim.35), calls=%async_computation | async-start | bytes 131072 | tf_op jit(solution)/shard_map/all_to_all | solution.py:46
  18.0 18.7 %copy-start.2 = (s32[1,32,8,32]{3,2,1,0:T(8,128)S(1)}, s32[1,32,8,32]{3,2,1,0:T(8,128)}, u32[]{:S(2)}) copy-start(s32[1,32,8,32]{3,2,1,0:T(8,128)} %param.13) | copy-start | bytes 98308
  19.6 1.4 collective-permute-start
  21.0 4.8 %collective-permute-start.1 = (f32[32,640]{1,0:T(8,128)S(1)}, f32[32,640]{1,0:T(8,128)S(1)}, u32[]{:S(2)}, u32[]{:S(2)}) collective-permute-start(f32[32,640]{1,0:T(8,128)S(1)} %fusion.13), channel_id=1, source_target_pairs={{0,32},{16,48},{32,0},{48,16},{64,96},{80,112},{96,64},{112,80},{1... | collective-permute-start | bytes 245768 | tf_op jit(solution)/shard_map/ppermute | solution.py:52
  25.8 6.2 %collective-permute-start.2 = (f32[32,640]{1,0:T(8,128)S(1)}, f32[32,640]{1,0:T(8,128)S(1)}, u32[]{:S(2)}, u32[]{:S(2)}) collective-permute-start(f32[32,640]{1,0:T(8,128)S(1)} %add.105), channel_id=1, source_target_pairs={{0,64},{16,80},{32,96},{48,112},{64,0},{80,16},{96,32},{112,48},{1... | collective-permute-start | bytes 245768 | tf_op jit(solution)/shard_map/ppermute | solution.py:52
  33.1 13.9 %all-to-all-start.1 = ((bf16[16,32,512]{2,1,0:T(8,128)(2,1)}), bf16[16,32,512]{2,1,0:T(8,128)(2,1)S(1)}, u32[]{:S(2)}, u32[]{:S(2)}) async-start(bf16[16,32,512]{2,1,0:T(8,128)(2,1)} %broadcast_in_dim.36), calls=%async_computation.1 | async-start | bytes 1048576 | tf_op jit(solution)/shard_map/all_to_all | solution.py:46
  77.5 1.8 %copy-start.1 = (f32[32,8,8,128]{3,2,1,0:T(8,128)S(1)}, f32[32,8,8,128]{3,2,1,0:T(8,128)}, u32[]{:S(2)}) copy-start(f32[32,8,8,128]{3,2,1,0:T(8,128)} %get-tuple-element.7) | copy-start | bytes 3145732
  95.1 30.0 %all-to-all-start.2 = ((f32[128,1,2080]{2,1,0:T(1,128)}), f32[128,1,2080]{2,1,0:T(1,128)S(1)}, u32[]{:S(2)}, u32[]{:S(2)}) async-start(f32[128,1,2080]{2,1,0:T(1,128)} %all_to_all.24), calls=%async_computation.2 | async-start | bytes 2228224 | tf_op jit(solution)/shard_map/all_to_all | solution.py:201
  128.1 8.7 %all-to-all-start.3 = ((bf16[8,4,512]{2,1,0:T(4,128)(2,1)}), bf16[8,4,512]{2,1,0:T(4,128)(2,1)S(1)}, u32[]{:S(2)}, u32[]{:S(2)}) async-start(bf16[8,4,512]{2,1,0:T(4,128)(2,1)} %broadcast_in_dim.37), calls=%async_computation.3 | async-start | bytes 65536 | tf_op jit(solution)/shard_map/all_to_all | solution.py:46
  137.9 11.3 %all-to-all-start.4 = ((f32[16,2,1024]{2,1,0:T(2,128)}), f32[16,2,1024]{2,1,0:T(2,128)S(1)}, u32[]{:S(2)}, u32[]{:S(2)}) async-start(f32[16,2,1024]{2,1,0:T(2,128)} %copy.38), calls=%async_computation.4 | async-start | bytes 262144 | tf_op jit(solution)/shard_map/all_to_all | solution.py:214

commit v6 on v5

--- a/solution.py
+++ b/solution.py
@@ -57,25 +57,14 @@
 DEPTH = 8
 UNROLL = 4
 
-def merge_kernel(seq_ref, pick_ref, q_ref, kv_hbm, acc_ref, tot_ref, max_ref, order_ref, buf, sems):
-    pairs = pick_ref.shape[0]
+def merge_kernel(seq_ref, order_ref, count_ref, q_ref, kv_hbm, acc_ref, tot_ref, max_ref, buf, sems):
     scale = 1.0 / math.sqrt(HD)
     acc_ref[...] = jnp.zeros(acc_ref.shape, jnp.float32)
     tot_ref[...] = jnp.zeros(tot_ref.shape, jnp.float32)
     max_ref[...] = jnp.full(max_ref.shape, NEG_BIG, jnp.float32)
 
-    def compact(i, n):
-        order_ref[n] = i
-        return n + pick_ref[i]
-
-    count = lax.fori_loop(0, pairs, compact, 0)
+    count = count_ref[0]
     padded = (count + UNROLL - 1) // UNROLL * UNROLL
-
-    def pad(k, carry):
-        order_ref[k] = 0
-        return carry
-
-    lax.fori_loop(count, padded, pad, 0)
 
     def copy_of(k):
         e = order_ref[k]
@@ -94,7 +83,6 @@
         e = order_ref[k]
         g = e % KVH
         seq = seq_ref[e // KVH]
-        copy_of(k).wait()
         page = buf[k % DEPTH]
         sc = lax.dot_general(q_ref[seq, g], page[:, :HD], (((1,), (1,)), ((), ())),
                              preferred_element_type=jnp.float32) * scale
@@ -115,13 +103,15 @@
 
     def body(step, carry):
         ks = [step * UNROLL + u for u in range(UNROLL)]
+        for k in ks:
+            copy_of(k).wait()
         done = [attend(k) for k in ks]
+        for k, res in zip(ks, done):
+            update(*res, k < count)
         for k in ks:
             @pl.when(k + DEPTH < padded)
             def _next():
                 copy_of(k + DEPTH).start()
-        for k, res in zip(ks, done):
-            update(*res, k < count)
         return carry
 
     lax.fori_loop(0, padded // UNROLL, body, 0)
@@ -131,19 +121,24 @@
     slots, tok, width = kv.shape
     seqs = q_all.shape[0]
     full = (seqs, KVH, H // KVH, HD)
+    flags = picked.reshape(-1).astype(jnp.int32)
+    pairs = flags.shape[0]
+    place = jnp.cumsum(flags) - 1
+    hit = (place[None, :] == jnp.arange(pairs, dtype=jnp.int32)[:, None]) & (flags[None, :] == 1)
+    order = jnp.sum(jnp.where(hit, jnp.arange(pairs, dtype=jnp.int32)[None, :], 0), axis=1)
+    count = jnp.sum(flags, keepdims=True)
     vmem = pl.BlockSpec(memory_space=pltpu.VMEM)
     smem = pl.BlockSpec(memory_space=pltpu.SMEM)
     return pl.pallas_call(
         merge_kernel,
-        in_specs=[smem, smem, vmem, pl.BlockSpec(memory_space=pl.ANY)],
+        in_specs=[smem, smem, smem, vmem, pl.BlockSpec(memory_space=pl.ANY)],
         out_specs=[vmem] * 3,
         out_shape=[jax.ShapeDtypeStruct(full, jnp.float32)] * 3,
         scratch_shapes=[
-            pltpu.SMEM((slots * KVH,), jnp.int32),
             pltpu.VMEM((DEPTH, tok, 2 * HD), kv.dtype),
             pltpu.SemaphoreType.DMA((DEPTH,)),
         ],
-    )(seq_of, picked.reshape(-1).astype(jnp.int32), q_all, kv)
+    )(seq_of, order, count, q_all, kv)
 
 
 def per_device(hidden_in, w_query, w_keyval, w_output, kv_pool, page_table, selected):
@@ -194,17 +189,20 @@
     loc_total = loc_total[..., 0].reshape(seqs, H)
     loc_max = loc_max[..., 0].reshape(seqs, H)
 
-    packed = jnp.concatenate([loc_acc, loc_total[..., None], loc_max[..., None]], axis=-1)
-    width = HD + 2
-    packed = packed.reshape(n_page, seq_share, n_tensor, local_heads, width)
-    packed = packed.transpose(0, 2, 1, 3, 4).reshape(n_page * n_tensor, -1)
+    blocks = n_page * n_tensor
+    def by_owner(x):
+        x = x.reshape((n_page, seq_share, n_tensor, local_heads) + x.shape[2:])
+        return x.transpose((0, 2, 1, 3) + tuple(range(4, x.ndim))).reshape(blocks, -1)
+    rows = seq_share * local_heads
+    packed = jnp.concatenate([by_owner(loc_acc), by_owner(loc_total), by_owner(loc_max)], axis=1)
     got = lax.all_to_all(packed, ("page", "tensor"), 0, 0, tiled=True)
-    got = got.reshape(n_page * n_tensor, seq_share, local_heads, width)
-    src_max = got[..., HD + 1]
+    src_acc = got[:, :rows * HD].reshape(blocks, rows, HD)
+    src_total = got[:, rows * HD:rows * HD + rows]
+    src_max = got[:, rows * HD + rows:]
     top_max = jnp.max(src_max, axis=0)
     rescale = jnp.exp(src_max - top_max[None])
-    full_total = jnp.sum(got[..., HD] * rescale, axis=0)
-    full_acc = jnp.sum(got[..., :HD] * rescale[..., None], axis=0)
+    full_total = jnp.sum(src_total * rescale, axis=0)
+    full_acc = jnp.sum(src_acc * rescale[..., None], axis=0)
     heads = (full_acc / full_total[..., None]).astype(jnp.bfloat16)
 
     heads_all = gather_blocks(heads.reshape(seq_share, local_heads * HD), "page", n_page)

time: 150 us -> 132 us (0.88)
  Pallas kernels: 29.3 us -> 18.1 us
  local copies, waits for them, and re-layouts: 22.6 us -> 16.5 us
  starting transfers between devices: 33.7 us -> 36.2 us
  waiting for transfers between devices: 52.8 us -> 50.3 us
    pallas_call x1, Pallas kernels: 29.3 us -> 18.1 us  [merge_pages(): pl.pallas_call(merge_kernel, in_specs=[smem, smem, smem, vmem, pl.BlockSp...]
    concatenate x4 -> x1, local copies, waits for them, and re-layouts: 8.43 us -> 0.27 us  [per_device(): jnp.concatenate([by_owner(loc_acc), by_owner(loc_total), by_owner(loc_max...]
    transpose x1 -> x0, other arithmetic: 2.69 us -> none  [per_device(): packed = packed.transpose(0, 2, 1, 3, 4).reshape(n_page * n_tensor, -1)]
    all_to_all x1, starting transfers between devices: 10.3 us -> 12.7 us  [per_device(): got = lax.all_to_all(packed, ('page', 'tensor'), 0, 0, tiled=True)]
    all_to_all x2, local copies, waits for them, and re-layouts: 5.83 us -> 3.59 us  [per_device(): got = lax.all_to_all(packed, ('page', 'tensor'), 0, 0, tiled=True)]
    another operation x0 -> x4, local copies, waits for them, and re-layouts: none -> 1.78 us  [the longest x3 1.66 us: by_owner(): x = x.reshape((n_page, seq_share, n_tensor, local_heads) + x.shape[2:])]
    reduce_sum x2 -> x4, other arithmetic: 0.52 us -> 2.13 us  [the longest x1 0.87 us: merge_pages(): jnp.sum(jnp.where(hit, jnp.arange(pairs, dtype=jnp.int32)[None, :], 0), a...]
    all_to_all x3, waiting for transfers between devices: 20.2 us -> 18.6 us  [gather_blocks(): lax.all_to_all(jnp.broadcast_to(x[None], (n,) + x.shape), axis, 0, 0, til...]
  transfers between devices with their start and end apart: 8 -> 8, of which waited for: 8 -> 7; matrix products, arithmetic and copies ran while one was open for 3% -> 6% of each run, Pallas kernels for 0% -> 0%
where the time goes in v6:
time: 132 us; the launch traced here: 131 us
  waiting for transfers between devices  50.3 us (38%)
  starting transfers between devices  36.2 us (27%)
  Pallas kernels  18.1 us (14%)
  local copies, waits for them, and re-layouts  16.5 us (12%)
  other arithmetic  7.3 us (6%)
  matrix products  1.66 us (1%)
    all_to_all x1, waiting for transfers between devices, per_device(): got = lax.all_to_all(packed, ('page', 'tensor'), 0, 0, tiled=True)  19.7 us
    all_to_all x3, waiting for transfers between devices, gather_blocks(): lax.all_to_all(jnp.broadcast_to(x[None], (n,) + x.shape), axis, 0, 0, til...  18.6 us
    pallas_call x1, Pallas kernels, merge_pages(): pl.pallas_call(merge_kernel, in_specs=[smem, smem, smem, vmem, pl.BlockSp...  18.1 us
    all_to_all x3, starting transfers between devices, gather_blocks(): lax.all_to_all(jnp.broadcast_to(x[None], (n,) + x.shape), axis, 0, 0, til...  14.1 us
    all_to_all x1, starting transfers between devices, per_device(): got = lax.all_to_all(packed, ('page', 'tensor'), 0, 0, tiled=True)  12.7 us
    all_to_all x1, waiting for transfers between devices, per_device(): out = jnp.sum(lax.all_to_all(part_out, 'tensor', 0, 0, tiled=True), axis=0)  7.05 us
    ppermute x3, starting transfers between devices, butterfly_sum(): x = x + lax.ppermute(x, axis, [(i, i ^ d) for i in range(n)])  5.86 us
    ppermute x3, waiting for transfers between devices, butterfly_sum(): x = x + lax.ppermute(x, axis, [(i, i ^ d) for i in range(n)])  4.94 us
  transfers between devices with their start and end apart: 8, of which 7 were waited for; matrix products, arithmetic and copies ran while one was open for 6% of the time, Pallas kernels for 0%

profile of v6, /device:TPU:0, one launch (start us, length us, event | category | flops | bytes accessed | tf_op | source)
XLA Modules:
  0.0 130.9 jit_solution(10426077988326994473)
XLA Ops:
  0.7 1.5 %broadcast_in_dim.52 = bf16[16,2,1024]{2,1,0:T(2,128)(2,1)} broadcast(bf16[2,1024]{1,0:T(2,128)(2,1)} %bitcast.92), dimensions={1,2} | broadcast | bytes 69632 | tf_op jit(solution)/shard_map/broadcast_in_dim | solution.py:46
  2.1 7.1 %all-to-all-start = ((bf16[16,2,1024]{2,1,0:T(2,128)(2,1)}), bf16[16,2,1024]{2,1,0:T(2,128)(2,1)S(1)}, u32[]{:S(2)}, u32[]{:S(2)}) async-start(bf16[16,2,1024]{2,1,0:T(2,128)(2,1)} %broadcast_in_dim.52), calls=%async_computation | async-start | bytes 131072 | tf_op jit(solution)/shard_map/all_to_all | solution.py:46
  9.3 1.1 select_reduce_fusion
  10.5 0.5 and_select_fusion.1
  11.0 1.5 %gather_fusion = s32[64,8,32]{2,1,0:T(8,128)S(1)} fusion(s32[32,8,32]{2,1,0:T(8,128)} %bitcast.89, s32[1024]{0:T(1024)S(1)} %pad_clamp_fusion), kind=kCustom, calls=%fused_computation | custom fusion | bytes 131328 | tf_op jit(solution)/shard_map/gather | solution.py:168
  12.5 4.5 %all-to-all-done = bf16[16,2,1024]{2,1,0:T(2,128)(2,1)S(1)} async-done(((bf16[16,2,1024]{2,1,0:T(2,128)(2,1)}), bf16[16,2,1024]{2,1,0:T(2,128)(2,1)S(1)}, u32[]{:S(2)}, u32[]{:S(2)}) %all-to-all-start) | async-done | bytes 65568 | tf_op jit(solution)/shard_map/all_to_all | solution.py:46
  17.0 1.1 fusion.17
  18.1 0.0 copy-done.1
  18.1 0.3 fusion.16
  18.4 0.1 collective-permute-start
  18.5 1.3 compare_reduce_fusion
  19.8 2.0 %collective-permute-start.1 = (f32[32,640]{1,0:T(8,128)S(1)}, f32[32,640]{1,0:T(8,128)S(1)}, u32[]{:S(2)}, u32[]{:S(2)}) collective-permute-start(f32[32,640]{1,0:T(8,128)S(1)} %fusion.15), channel_id=1, source_target_pairs={{0,32},{16,48},{32,0},{48,16},{64,96},{80,112},{96,64},{112,80},{1... | collective-permute-start | bytes 245768 | tf_op jit(solution)/shard_map/ppermute | solution.py:52
  21.8 0.1 reshape.209
  21.9 0.3 reduce-window.9
  22.2 0.1 slice.40
  22.3 2.6 %collective-permute-done.1 = f32[32,640]{1,0:T(8,128)S(1)} collective-permute-done((f32[32,640]{1,0:T(8,128)S(1)}, f32[32,640]{1,0:T(8,128)S(1)}, u32[]{:S(2)}, u32[]{:S(2)}) %collective-permute-start.1) | collective-permute-done | bytes 81952 | tf_op jit(solution)/shard_map/ppermute | solution.py:52
  24.9 3.8 %collective-permute-start.2 = (f32[32,640]{1,0:T(8,128)S(1)}, f32[32,640]{1,0:T(8,128)S(1)}, u32[]{:S(2)}, u32[]{:S(2)}) collective-permute-start(f32[32,640]{1,0:T(8,128)S(1)} %add.111), channel_id=1, source_target_pairs={{0,64},{16,80},{32,96},{48,112},{64,0},{80,16},{96,32},{112,48},{1... | collective-permute-start | bytes 245768 | tf_op jit(solution)/shard_map/ppermute | solution.py:52
  28.7 0.1 fusion.13
  28.8 2.4 %collective-permute-done.2 = f32[32,640]{1,0:T(8,128)S(1)} collective-permute-done((f32[32,640]{1,0:T(8,128)S(1)}, f32[32,640]{1,0:T(8,128)S(1)}, u32[]{:S(2)}, u32[]{:S(2)}) %collective-permute-start.2) | collective-permute-done | bytes 81952 | tf_op jit(solution)/shard_map/ppermute | solution.py:52
  31.2 0.1 subtract_convert_fusion
  31.3 0.1 pad_maximum_fusion.1
  31.4 0.8 broadcast_in_dim.53
  32.2 3.6 %all-to-all-start.1 = ((bf16[16,32,512]{2,1,0:T(8,128)(2,1)}), bf16[16,32,512]{2,1,0:T(8,128)(2,1)S(1)}, u32[]{:S(2)}, u32[]{:S(2)}) async-start(bf16[16,32,512]{2,1,0:T(8,128)(2,1)} %broadcast_in_dim.53), calls=%async_computation.1 | async-start | bytes 1048576 | tf_op jit(solution)/shard_map/all_to_all | solution.py:46
  35.8 0.1 slice_reduce_fusion.1
  35.9 0.1 eq.66
  36.0 0.7 convert_reduce_fusion
  36.8 0.1 add_bitcast_fusion.1
  36.8 0.9 select_reduce_fusion.1.order_ref
  37.7 8.8 %all-to-all-done.1 = bf16[16,32,512]{2,1,0:T(8,128)(2,1)S(1)} async-done(((bf16[16,32,512]{2,1,0:T(8,128)(2,1)}), bf16[16,32,512]{2,1,0:T(8,128)(2,1)S(1)}, u32[]{:S(2)}, u32[]{:S(2)}) %all-to-all-start.1) | async-done | bytes 524320 | tf_op jit(solution)/shard_map/all_to_all | solution.py:46
  46.5 0.1 reshape.203
  46.6 1.1 copy.40
  47.7 18.1 %shard_map.86 = (f32[32,8,8,128]{3,2,1,0:T(8,128)}, f32[32,8,8,128]{3,2,1,0:T(8,128)}, f32[32,8,8,128]{3,2,1,0:T(8,128)}) custom-call(s32[64]{0:T(128)} %get-tuple-element.17.seq_ref, s32[512]{0:T(512)} %select_reduce_fusion.1.order_ref, s32[1]{0:T(128)} %bitcast.4.count_ref, bf16[32,8,8,128]{3,2,1,0:T(8,128)(2,1)} %bitcast.83, bf16[64,64,2048]{2,1,0:T(8,128)(2,1)} %kv_hbm.1), custom_call_target="tpu_custom_call" | custom-call | tf_op jit(solution)/shard_map/pallas_call | solution.py:132
  65.8 1.4 %copy.61 = f32[8,4,16,4,128]{4,3,1,2,0:T(4,128)S(1)} copy(f32[8,4,16,4,128]{4,3,2,1,0:T(4,128)} %bitcast.88) | data formatting | bytes 2097152 | tf_op jit(solution)/shard_map/reshape;reshape | solution.py:194
  67.2 0.4 reshape.205
  67.6 1.9 %copy.42 = f32[32,8,8,1]{0,2,1,3:T(8,128)S(1)} copy(f32[32,8,8,1]{3,2,1,0:T(8,128)} %bitcast.87) | data formatting | bytes 16384 | tf_op jit(solution)/shard_map/slice | solution.py:189
  69.5 0.6 copy.44
  70.1 0.1 reshape_reshape_squeeze.7
  70.2 0.3 copy.45
  70.5 0.1 reshape.207
  70.6 0.1 copy.47
  70.7 0.1 reshape_reshape_squeeze.6
  70.9 0.3 copy.43
  71.2 0.1 reshape.206
  71.3 0.1 copy.46
  71.4 0.3 concatenate.20
  71.6 2.1 %copy.48 = f32[128,1,2080]{2,1,0:T(1,128)} copy(f32[128,1,2080]{2,0,1:T(8,128)S(1)} %bitcast.78) | data formatting | bytes 2129920 | tf_op jit(solution)/shard_map/all_to_all | solution.py:198
  73.8 12.7 %all-to-all-start.2 = ((f32[128,1,2080]{2,1,0:T(1,128)}), f32[128,1,2080]{2,1,0:T(1,128)S(1)}, u32[]{:S(2)}, u32[]{:S(2)}) async-start(f32[128,1,2080]{2,1,0:T(1,128)} %copy.48), calls=%async_computation.2 | async-start | bytes 2228224 | tf_op jit(solution)/shard_map/all_to_all | solution.py:198
  86.5 19.7 %all-to-all-done.2 = f32[128,1,2080]{2,1,0:T(1,128)S(1)} async-done(((f32[128,1,2080]{2,1,0:T(1,128)}), f32[128,1,2080]{2,1,0:T(1,128)S(1)}, u32[]{:S(2)}, u32[]{:S(2)}) %all-to-all-start.2) | async-done | bytes 1064992 | tf_op jit(solution)/shard_map/all_to_all | solution.py:198
  106.2 1.5 %copy.49 = f32[128,1,2080]{0,2,1:T(8,128)S(1)} copy(f32[128,1,2080]{2,1,0:T(1,128)S(1)} %all-to-all-done.2) | data formatting | bytes 2129920 | tf_op jit(solution)/shard_map/all_to_all | solution.py:198
  107.7 0.1 slice_reduce_fusion
  107.8 0.2 fusion.5
  108.0 0.4 fusion
  108.4 0.1 div.165
  108.4 0.1 broadcast_bitcast_fusion
  108.5 0.6 broadcast_in_dim.54
  109.2 3.3 %all-to-all-start.3 = ((bf16[8,4,512]{2,1,0:T(4,128)(2,1)}), bf16[8,4,512]{2,1,0:T(4,128)(2,1)S(1)}, u32[]{:S(2)}, u32[]{:S(2)}) async-start(bf16[8,4,512]{2,1,0:T(4,128)(2,1)} %broadcast_in_dim.54), calls=%async_computation.3 | async-start | bytes 65536 | tf_op jit(solution)/shard_map/all_to_all | solution.py:46
  112.5 5.4 %all-to-all-done.3 = bf16[8,4,512]{2,1,0:T(4,128)(2,1)S(1)} async-done(((bf16[8,4,512]{2,1,0:T(4,128)(2,1)}), bf16[8,4,512]{2,1,0:T(4,128)(2,1)S(1)}, u32[]{:S(2)}, u32[]{:S(2)}) %all-to-all-start.3) | async-done | bytes 32800 | tf_op jit(solution)/shard_map/all_to_all | solution.py:46
  117.9 0.3 fusion.1
  118.2 0.7 copy.51
  118.9 3.5 %all-to-all-start.4 = ((f32[16,2,1024]{2,1,0:T(2,128)}), f32[16,2,1024]{2,1,0:T(2,128)S(1)}, u32[]{:S(2)}, u32[]{:S(2)}) async-start(f32[16,2,1024]{2,1,0:T(2,128)} %copy.51), calls=%async_computation.4 | async-start | bytes 262144 | tf_op jit(solution)/shard_map/all_to_all | solution.py:212
  122.4 0.1 subtract_bitcast_fusion
  122.5 0.6 fusion.10
  123.2 7.0 %all-to-all-done.4 = f32[16,2,1024]{2,1,0:T(2,128)S(1)} async-done(((f32[16,2,1024]{2,1,0:T(2,128)}), f32[16,2,1024]{2,1,0:T(2,128)S(1)}, u32[]{:S(2)}, u32[]{:S(2)}) %all-to-all-start.4) | async-done | bytes 131104 | tf_op jit(solution)/shard_map/all_to_all | solution.py:212
  130.2 0.6 reduce_sum.65
  (24 shorter events, 0.2 us)
Async XLA Ops:
  0.6 117.3 %copy-start = (bf16[512,1024]{1,0:T(8,128)(2,1)S(1)}, bf16[512,1024]{1,0:T(8,128)(2,1)}, u32[]{:S(2)}) copy-start(bf16[512,1024]{1,0:T(8,128)(2,1)} %param.10) | copy-start | bytes 3145732
  0.6 17.5 %copy-start.1 = (bf16[1024,512]{1,0:T(8,128)(2,1)S(1)}, bf16[1024,512]{1,0:T(8,128)(2,1)}, u32[]{:S(2)}) copy-start(bf16[1024,512]{1,0:T(8,128)(2,1)} %param.8) | copy-start | bytes 3145732
  2.1 14.8 %all-to-all-start = ((bf16[16,2,1024]{2,1,0:T(2,128)(2,1)}), bf16[16,2,1024]{2,1,0:T(2,128)(2,1)S(1)}, u32[]{:S(2)}, u32[]{:S(2)}) async-start(bf16[16,2,1024]{2,1,0:T(2,128)(2,1)} %broadcast_in_dim.52), calls=%async_computation | async-start | bytes 131072 | tf_op jit(solution)/shard_map/all_to_all | solution.py:46
  18.4 1.4 %collective-permute-start = (f32[32,640]{1,0:T(8,128)S(1)}, f32[32,640]{1,0:T(8,128)S(1)}, u32[]{:S(2)}, u32[]{:S(2)}) collective-permute-start(f32[32,640]{1,0:T(8,128)S(1)} %pad_maximum_fusion), channel_id=1, source_target_pairs={{0,16},{16,0},{32,48},{48,32},{64,80},{80,64},{96,112},{112,96},{1... | collective-permute-start | bytes 245768 | tf_op jit(solution)/shard_map/ppermute | solution.py:52
  19.8 5.1 %collective-permute-start.1 = (f32[32,640]{1,0:T(8,128)S(1)}, f32[32,640]{1,0:T(8,128)S(1)}, u32[]{:S(2)}, u32[]{:S(2)}) collective-permute-start(f32[32,640]{1,0:T(8,128)S(1)} %fusion.15), channel_id=1, source_target_pairs={{0,32},{16,48},{32,0},{48,16},{64,96},{80,112},{96,64},{112,80},{1... | collective-permute-start | bytes 245768 | tf_op jit(solution)/shard_map/ppermute | solution.py:52
  24.9 6.2 %collective-permute-start.2 = (f32[32,640]{1,0:T(8,128)S(1)}, f32[32,640]{1,0:T(8,128)S(1)}, u32[]{:S(2)}, u32[]{:S(2)}) collective-permute-start(f32[32,640]{1,0:T(8,128)S(1)} %add.111), channel_id=1, source_target_pairs={{0,64},{16,80},{32,96},{48,112},{64,0},{80,16},{96,32},{112,48},{1... | collective-permute-start | bytes 245768 | tf_op jit(solution)/shard_map/ppermute | solution.py:52
  32.2 14.2 %all-to-all-start.1 = ((bf16[16,32,512]{2,1,0:T(8,128)(2,1)}), bf16[16,32,512]{2,1,0:T(8,128)(2,1)S(1)}, u32[]{:S(2)}, u32[]{:S(2)}) async-start(bf16[16,32,512]{2,1,0:T(8,128)(2,1)} %broadcast_in_dim.53), calls=%async_computation.1 | async-start | bytes 1048576 | tf_op jit(solution)/shard_map/all_to_all | solution.py:46
  67.6 1.9 %copy-start.2 = (f32[32,8,8,128]{3,2,1,0:T(8,128)S(1)}, f32[32,8,8,128]{3,2,1,0:T(8,128)}, u32[]{:S(2)}) copy-start(f32[32,8,8,128]{3,2,1,0:T(8,128)} %get-tuple-element.7) | copy-start | bytes 3145732
  73.8 32.5 %all-to-all-start.2 = ((f32[128,1,2080]{2,1,0:T(1,128)}), f32[128,1,2080]{2,1,0:T(1,128)S(1)}, u32[]{:S(2)}, u32[]{:S(2)}) async-start(f32[128,1,2080]{2,1,0:T(1,128)} %copy.48), calls=%async_computation.2 | async-start | bytes 2228224 | tf_op jit(solution)/shard_map/all_to_all | solution.py:198
  109.2 8.7 %all-to-all-start.3 = ((bf16[8,4,512]{2,1,0:T(4,128)(2,1)}), bf16[8,4,512]{2,1,0:T(4,128)(2,1)S(1)}, u32[]{:S(2)}, u32[]{:S(2)}) async-start(bf16[8,4,512]{2,1,0:T(4,128)(2,1)} %broadcast_in_dim.54), calls=%async_computation.3 | async-start | bytes 65536 | tf_op jit(solution)/shard_map/all_to_all | solution.py:46
  118.9 11.3 %all-to-all-start.4 = ((f32[16,2,1024]{2,1,0:T(2,128)}), f32[16,2,1024]{2,1,0:T(2,128)S(1)}, u32[]{:S(2)}, u32[]{:S(2)}) async-start(f32[16,2,1024]{2,1,0:T(2,128)} %copy.51), calls=%async_computation.4 | async-start | bytes 262144 | tf_op jit(solution)/shard_map/all_to_all | solution.py:212

commit v7 on v6

--- a/solution.py
+++ b/solution.py
@@ -54,8 +54,8 @@
     return x
 
 
-DEPTH = 8
-UNROLL = 4
+DEPTH = 32
+UNROLL = 16
 
 def merge_kernel(seq_ref, order_ref, count_ref, q_ref, kv_hbm, acc_ref, tot_ref, max_ref, buf, sems):
     scale = 1.0 / math.sqrt(HD)
@@ -79,18 +79,31 @@
         def _start():
             copy_of(k).start()
 
-    def attend(k):
-        e = order_ref[k]
-        g = e % KVH
-        seq = seq_ref[e // KVH]
-        page = buf[k % DEPTH]
-        sc = lax.dot_general(q_ref[seq, g], page[:, :HD], (((1,), (1,)), ((), ())),
-                             preferred_element_type=jnp.float32) * scale
+    rows = lax.broadcasted_iota(jnp.int32, (UNROLL * 8, UNROLL * 64), 0) // 8
+    cols = lax.broadcasted_iota(jnp.int32, (UNROLL * 8, UNROLL * 64), 1) // 64
+    own_page = rows == cols
+
+    def attend_all(ks):
+        where = []
+        qs, keys, vals = [], [], []
+        for k in ks:
+            e = order_ref[k]
+            g = e % KVH
+            seq = seq_ref[e // KVH]
+            page = buf[k % DEPTH]
+            where.append((seq, g))
+            qs.append(q_ref[seq, g])
+            keys.append(page[:, :HD])
+            vals.append(page[:, HD:])
+        sc = lax.dot_general(jnp.concatenate(qs, axis=0), jnp.concatenate(keys, axis=0),
+                             (((1,), (1,)), ((), ())), preferred_element_type=jnp.float32) * scale
+        sc = jnp.where(own_page, sc, -jnp.inf)
         pm = jnp.max(sc, axis=1, keepdims=True)
         wt = jnp.exp(sc - pm).astype(jnp.bfloat16)
         pt = jnp.sum(wt.astype(jnp.float32), axis=1, keepdims=True)
-        pa = jnp.dot(wt, page[:, HD:], preferred_element_type=jnp.float32)
-        return seq, g, pm, pt, pa
+        pa = jnp.dot(wt, jnp.concatenate(vals, axis=0), preferred_element_type=jnp.float32)
+        rows8 = [slice(8 * u, 8 * u + 8) for u in range(len(ks))]
+        return [(seq, g, pm[r], pt[r], pa[r]) for (seq, g), r in zip(where, rows8)]
 
     def update(seq, g, pm, pt, pa, live):
         m_old = max_ref[seq, g]
@@ -105,7 +118,7 @@
         ks = [step * UNROLL + u for u in range(UNROLL)]
         for k in ks:
             copy_of(k).wait()
-        done = [attend(k) for k in ks]
+        done = attend_all(ks)
         for k, res in zip(ks, done):
             update(*res, k < count)
         for k in ks:

time: 132 us -> 117 us (0.89)
  Pallas kernels: 18.1 us -> 9.51 us
  starting transfers between devices: 36.2 us -> 30 us
    pallas_call x1, Pallas kernels: 18.1 us -> 9.51 us  [merge_pages(): pl.pallas_call(merge_kernel, in_specs=[smem, smem, smem, vmem, pl.BlockSp...]
    all_to_all x1, starting transfers between devices: 12.7 us -> 6.57 us  [per_device(): got = lax.all_to_all(packed, ('page', 'tensor'), 0, 0, tiled=True)]
  transfers between devices with their start and end apart: 8 -> 8, of which waited for: 7 -> 7; matrix products, arithmetic and copies ran while one was open for 6% -> 7% of each run, Pallas kernels for 0% -> 0%
where the time goes in v7:
time: 117 us; the launch traced here: 116 us
  waiting for transfers between devices  50.3 us (43%)
  starting transfers between devices  30 us (26%)
  local copies, waits for them, and re-layouts  16.5 us (14%)
  Pallas kernels  9.51 us (8%)
  other arithmetic  7.3 us (6%)
  matrix products  1.66 us (1%)
    all_to_all x1, waiting for transfers between devices, per_device(): got = lax.all_to_all(packed, ('page', 'tensor'), 0, 0, tiled=True)  19.7 us
    all_to_all x3, waiting for transfers between devices, gather_blocks(): lax.all_to_all(jnp.broadcast_to(x[None], (n,) + x.shape), axis, 0, 0, til...  18.6 us
    all_to_all x3, starting transfers between devices, gather_blocks(): lax.all_to_all(jnp.broadcast_to(x[None], (n,) + x.shape), axis, 0, 0, til...  14.1 us
    pallas_call x1, Pallas kernels, merge_pages(): pl.pallas_call(merge_kernel, in_specs=[smem, smem, smem, vmem, pl.BlockSp...  9.51 us
    all_to_all x1, waiting for transfers between devices, per_device(): out = jnp.sum(lax.all_to_all(part_out, 'tensor', 0, 0, tiled=True), axis=0)  7.05 us
    all_to_all x1, starting transfers between devices, per_device(): got = lax.all_to_all(packed, ('page', 'tensor'), 0, 0, tiled=True)  6.57 us
    ppermute x3, starting transfers between devices, butterfly_sum(): x = x + lax.ppermute(x, axis, [(i, i ^ d) for i in range(n)])  5.86 us
    ppermute x3, waiting for transfers between devices, butterfly_sum(): x = x + lax.ppermute(x, axis, [(i, i ^ d) for i in range(n)])  4.94 us
  transfers between devices with their start and end apart: 8, of which 7 were waited for; matrix products, arithmetic and copies ran while one was open for 7% of the time, Pallas kernels for 0%

profile of v7, /device:TPU:0, one launch (start us, length us, event | category | flops | bytes accessed | tf_op | source)
XLA Modules:
  0.0 116.1 jit_solution(15376865994142492779)
XLA Ops:
  0.7 1.5 %broadcast_in_dim.52 = bf16[16,2,1024]{2,1,0:T(2,128)(2,1)} broadcast(bf16[2,1024]{1,0:T(2,128)(2,1)} %bitcast.92), dimensions={1,2} | broadcast | bytes 69632 | tf_op jit(solution)/shard_map/broadcast_in_dim | solution.py:46
  2.1 7.1 %all-to-all-start = ((bf16[16,2,1024]{2,1,0:T(2,128)(2,1)}), bf16[16,2,1024]{2,1,0:T(2,128)(2,1)S(1)}, u32[]{:S(2)}, u32[]{:S(2)}) async-start(bf16[16,2,1024]{2,1,0:T(2,128)(2,1)} %broadcast_in_dim.52), calls=%async_computation | async-start | bytes 131072 | tf_op jit(solution)/shard_map/all_to_all | solution.py:46
  9.3 1.1 select_reduce_fusion
  10.5 0.5 and_select_fusion.1
  11.0 1.5 %gather_fusion = s32[64,8,32]{2,1,0:T(8,128)S(1)} fusion(s32[32,8,32]{2,1,0:T(8,128)} %bitcast.89, s32[1024]{0:T(1024)S(1)} %pad_clamp_fusion), kind=kCustom, calls=%fused_computation | custom fusion | bytes 131328 | tf_op jit(solution)/shard_map/gather | solution.py:181
  12.5 4.5 %all-to-all-done = bf16[16,2,1024]{2,1,0:T(2,128)(2,1)S(1)} async-done(((bf16[16,2,1024]{2,1,0:T(2,128)(2,1)}), bf16[16,2,1024]{2,1,0:T(2,128)(2,1)S(1)}, u32[]{:S(2)}, u32[]{:S(2)}) %all-to-all-start) | async-done | bytes 65568 | tf_op jit(solution)/shard_map/all_to_all | solution.py:46
  17.0 1.1 fusion.17
  18.1 0.0 copy-done.1
  18.1 0.3 fusion.16
  18.4 0.1 collective-permute-start
  18.5 1.3 %compare_reduce_fusion = pred[64,8]{1,0:T(8,128)(4,1)S(1)} fusion(s32[64,8,32]{2,1,0:T(8,128)S(1)} %gather_fusion, s32[64]{0:T(128)S(1)} %get-tuple-element.16), kind=kLoop, calls=%fused_computation.10 | loop fusion | flops 32256 | bytes 66304 | tf_op jit(solution)/shard_map/reduce_or | solution.py:182
  19.8 2.0 %collective-permute-start.1 = (f32[32,640]{1,0:T(8,128)S(1)}, f32[32,640]{1,0:T(8,128)S(1)}, u32[]{:S(2)}, u32[]{:S(2)}) collective-permute-start(f32[32,640]{1,0:T(8,128)S(1)} %fusion.15), channel_id=1, source_target_pairs={{0,32},{16,48},{32,0},{48,16},{64,96},{80,112},{96,64},{112,80},{1... | collective-permute-start | bytes 245768 | tf_op jit(solution)/shard_map/ppermute | solution.py:52
  21.8 0.1 reshape.209
  21.9 0.3 reduce-window.9
  22.2 0.1 slice.40
  22.3 2.6 %collective-permute-done.1 = f32[32,640]{1,0:T(8,128)S(1)} collective-permute-done((f32[32,640]{1,0:T(8,128)S(1)}, f32[32,640]{1,0:T(8,128)S(1)}, u32[]{:S(2)}, u32[]{:S(2)}) %collective-permute-start.1) | collective-permute-done | bytes 81952 | tf_op jit(solution)/shard_map/ppermute | solution.py:52
  24.9 3.8 %collective-permute-start.2 = (f32[32,640]{1,0:T(8,128)S(1)}, f32[32,640]{1,0:T(8,128)S(1)}, u32[]{:S(2)}, u32[]{:S(2)}) collective-permute-start(f32[32,640]{1,0:T(8,128)S(1)} %add.111), channel_id=1, source_target_pairs={{0,64},{16,80},{32,96},{48,112},{64,0},{80,16},{96,32},{112,48},{1... | collective-permute-start | bytes 245768 | tf_op jit(solution)/shard_map/ppermute | solution.py:52
  28.7 0.1 fusion.13
  28.8 2.4 %collective-permute-done.2 = f32[32,640]{1,0:T(8,128)S(1)} collective-permute-done((f32[32,640]{1,0:T(8,128)S(1)}, f32[32,640]{1,0:T(8,128)S(1)}, u32[]{:S(2)}, u32[]{:S(2)}) %collective-permute-start.2) | collective-permute-done | bytes 81952 | tf_op jit(solution)/shard_map/ppermute | solution.py:52
  31.2 0.1 subtract_convert_fusion
  31.3 0.1 pad_maximum_fusion.1
  31.4 0.8 broadcast_in_dim.53
  32.2 3.6 %all-to-all-start.1 = ((bf16[16,32,512]{2,1,0:T(8,128)(2,1)}), bf16[16,32,512]{2,1,0:T(8,128)(2,1)S(1)}, u32[]{:S(2)}, u32[]{:S(2)}) async-start(bf16[16,32,512]{2,1,0:T(8,128)(2,1)} %broadcast_in_dim.53), calls=%async_computation.1 | async-start | bytes 1048576 | tf_op jit(solution)/shard_map/all_to_all | solution.py:46
  35.8 0.1 slice_reduce_fusion.1
  35.9 0.1 eq.66
  36.0 0.7 convert_reduce_fusion
  36.8 0.1 add_bitcast_fusion.1
  36.8 0.9 select_reduce_fusion.1.order_ref
  37.7 8.8 %all-to-all-done.1 = bf16[16,32,512]{2,1,0:T(8,128)(2,1)S(1)} async-done(((bf16[16,32,512]{2,1,0:T(8,128)(2,1)}), bf16[16,32,512]{2,1,0:T(8,128)(2,1)S(1)}, u32[]{:S(2)}, u32[]{:S(2)}) %all-to-all-start.1) | async-done | bytes 524320 | tf_op jit(solution)/shard_map/all_to_all | solution.py:46
  46.5 0.1 reshape.203
  46.6 1.1 copy.40
  47.7 9.5 %shard_map.86 = (f32[32,8,8,128]{3,2,1,0:T(8,128)}, f32[32,8,8,128]{3,2,1,0:T(8,128)}, f32[32,8,8,128]{3,2,1,0:T(8,128)}) custom-call(s32[64]{0:T(128)} %get-tuple-element.17.seq_ref, s32[512]{0:T(512)} %select_reduce_fusion.1.order_ref, s32[1]{0:T(128)} %bitcast.4.count_ref, bf16[32,8,8,128]{3,2,1,0:T(8,128)(2,1)} %bitcast.83, bf16[64,64,2048]{2,1,0:T(8,128)(2,1)} %kv_hbm.1), custom_call_target="tpu_custom_call" | custom-call | tf_op jit(solution)/shard_map/pallas_call | solution.py:145
  57.2 1.4 %copy.61 = f32[8,4,16,4,128]{4,3,1,2,0:T(4,128)S(1)} copy(f32[8,4,16,4,128]{4,3,2,1,0:T(4,128)} %bitcast.88) | data formatting | bytes 2097152 | tf_op jit(solution)/shard_map/reshape;reshape | solution.py:207
  58.6 0.4 reshape.205
  59.1 1.9 %copy.42 = f32[32,8,8,1]{0,2,1,3:T(8,128)S(1)} copy(f32[32,8,8,1]{3,2,1,0:T(8,128)} %bitcast.87) | data formatting | bytes 16384 | tf_op jit(solution)/shard_map/slice | solution.py:202
  60.9 0.6 copy.44
  61.5 0.1 reshape_reshape_squeeze.7
  61.7 0.3 copy.45
  62.0 0.1 reshape.207
  62.1 0.1 copy.47
  62.2 0.1 reshape_reshape_squeeze.6
  62.3 0.3 copy.43
  62.6 0.1 reshape.206
  62.7 0.1 copy.46
  62.8 0.3 concatenate.20
  63.1 2.1 %copy.48 = f32[128,1,2080]{2,1,0:T(1,128)} copy(f32[128,1,2080]{2,0,1:T(8,128)S(1)} %bitcast.78) | data formatting | bytes 2129920 | tf_op jit(solution)/shard_map/all_to_all | solution.py:211
  65.2 6.6 %all-to-all-start.2 = ((f32[128,1,2080]{2,1,0:T(1,128)}), f32[128,1,2080]{2,1,0:T(1,128)S(1)}, u32[]{:S(2)}, u32[]{:S(2)}) async-start(f32[128,1,2080]{2,1,0:T(1,128)} %copy.48), calls=%async_computation.2 | async-start | bytes 2228224 | tf_op jit(solution)/shard_map/all_to_all | solution.py:211
  71.8 19.7 %all-to-all-done.2 = f32[128,1,2080]{2,1,0:T(1,128)S(1)} async-done(((f32[128,1,2080]{2,1,0:T(1,128)}), f32[128,1,2080]{2,1,0:T(1,128)S(1)}, u32[]{:S(2)}, u32[]{:S(2)}) %all-to-all-start.2) | async-done | bytes 1064992 | tf_op jit(solution)/shard_map/all_to_all | solution.py:211
  91.5 1.5 %copy.49 = f32[128,1,2080]{0,2,1:T(8,128)S(1)} copy(f32[128,1,2080]{2,1,0:T(1,128)S(1)} %all-to-all-done.2) | data formatting | bytes 2129920 | tf_op jit(solution)/shard_map/all_to_all | solution.py:211
  93.0 0.1 slice_reduce_fusion
  93.1 0.2 fusion.5
  93.3 0.4 fusion
  93.6 0.1 div.165
  93.7 0.1 broadcast_bitcast_fusion
  93.8 0.6 broadcast_in_dim.54
  94.4 3.3 %all-to-all-start.3 = ((bf16[8,4,512]{2,1,0:T(4,128)(2,1)}), bf16[8,4,512]{2,1,0:T(4,128)(2,1)S(1)}, u32[]{:S(2)}, u32[]{:S(2)}) async-start(bf16[8,4,512]{2,1,0:T(4,128)(2,1)} %broadcast_in_dim.54), calls=%async_computation.3 | async-start | bytes 65536 | tf_op jit(solution)/shard_map/all_to_all | solution.py:46
  97.8 5.4 %all-to-all-done.3 = bf16[8,4,512]{2,1,0:T(4,128)(2,1)S(1)} async-done(((bf16[8,4,512]{2,1,0:T(4,128)(2,1)}), bf16[8,4,512]{2,1,0:T(4,128)(2,1)S(1)}, u32[]{:S(2)}, u32[]{:S(2)}) %all-to-all-start.3) | async-done | bytes 32800 | tf_op jit(solution)/shard_map/all_to_all | solution.py:46
  103.2 0.3 fusion.1
  103.4 0.7 copy.51
  104.2 3.5 %all-to-all-start.4 = ((f32[16,2,1024]{2,1,0:T(2,128)}), f32[16,2,1024]{2,1,0:T(2,128)S(1)}, u32[]{:S(2)}, u32[]{:S(2)}) async-start(f32[16,2,1024]{2,1,0:T(2,128)} %copy.51), calls=%async_computation.4 | async-start | bytes 262144 | tf_op jit(solution)/shard_map/all_to_all | solution.py:225
  107.7 0.1 subtract_bitcast_fusion
  107.8 0.6 fusion.10
  108.4 7.0 %all-to-all-done.4 = f32[16,2,1024]{2,1,0:T(2,128)S(1)} async-done(((f32[16,2,1024]{2,1,0:T(2,128)}), f32[16,2,1024]{2,1,0:T(2,128)S(1)}, u32[]{:S(2)}, u32[]{:S(2)}) %all-to-all-start.4) | async-done | bytes 131104 | tf_op jit(solution)/shard_map/all_to_all | solution.py:225
  115.5 0.6 reduce_sum.65
  (24 shorter events, 0.2 us)
Async XLA Ops:
  0.6 102.5 %copy-start = (bf16[512,1024]{1,0:T(8,128)(2,1)S(1)}, bf16[512,1024]{1,0:T(8,128)(2,1)}, u32[]{:S(2)}) copy-start(bf16[512,1024]{1,0:T(8,128)(2,1)} %param.10) | copy-start | bytes 3145732
  0.6 17.5 %copy-start.1 = (bf16[1024,512]{1,0:T(8,128)(2,1)S(1)}, bf16[1024,512]{1,0:T(8,128)(2,1)}, u32[]{:S(2)}) copy-start(bf16[1024,512]{1,0:T(8,128)(2,1)} %param.8) | copy-start | bytes 3145732
  2.1 14.8 %all-to-all-start = ((bf16[16,2,1024]{2,1,0:T(2,128)(2,1)}), bf16[16,2,1024]{2,1,0:T(2,128)(2,1)S(1)}, u32[]{:S(2)}, u32[]{:S(2)}) async-start(bf16[16,2,1024]{2,1,0:T(2,128)(2,1)} %broadcast_in_dim.52), calls=%async_computation | async-start | bytes 131072 | tf_op jit(solution)/shard_map/all_to_all | solution.py:46
  18.4 1.4 %collective-permute-start = (f32[32,640]{1,0:T(8,128)S(1)}, f32[32,640]{1,0:T(8,128)S(1)}, u32[]{:S(2)}, u32[]{:S(2)}) collective-permute-start(f32[32,640]{1,0:T(8,128)S(1)} %pad_maximum_fusion), channel_id=1, source_target_pairs={{0,16},{16,0},{32,48},{48,32},{64,80},{80,64},{96,112},{112,96},{1... | collective-permute-start | bytes 245768 | tf_op jit(solution)/shard_map/ppermute | solution.py:52
  19.8 5.1 %collective-permute-start.1 = (f32[32,640]{1,0:T(8,128)S(1)}, f32[32,640]{1,0:T(8,128)S(1)}, u32[]{:S(2)}, u32[]{:S(2)}) collective-permute-start(f32[32,640]{1,0:T(8,128)S(1)} %fusion.15), channel_id=1, source_target_pairs={{0,32},{16,48},{32,0},{48,16},{64,96},{80,112},{96,64},{112,80},{1... | collective-permute-start | bytes 245768 | tf_op jit(solution)/shard_map/ppermute | solution.py:52
  24.9 6.2 %collective-permute-start.2 = (f32[32,640]{1,0:T(8,128)S(1)}, f32[32,640]{1,0:T(8,128)S(1)}, u32[]{:S(2)}, u32[]{:S(2)}) collective-permute-start(f32[32,640]{1,0:T(8,128)S(1)} %add.111), channel_id=1, source_target_pairs={{0,64},{16,80},{32,96},{48,112},{64,0},{80,16},{96,32},{112,48},{1... | collective-permute-start | bytes 245768 | tf_op jit(solution)/shard_map/ppermute | solution.py:52
  32.2 14.2 %all-to-all-start.1 = ((bf16[16,32,512]{2,1,0:T(8,128)(2,1)}), bf16[16,32,512]{2,1,0:T(8,128)(2,1)S(1)}, u32[]{:S(2)}, u32[]{:S(2)}) async-start(bf16[16,32,512]{2,1,0:T(8,128)(2,1)} %broadcast_in_dim.53), calls=%async_computation.1 | async-start | bytes 1048576 | tf_op jit(solution)/shard_map/all_to_all | solution.py:46
  59.0 1.9 %copy-start.2 = (f32[32,8,8,128]{3,2,1,0:T(8,128)S(1)}, f32[32,8,8,128]{3,2,1,0:T(8,128)}, u32[]{:S(2)}) copy-start(f32[32,8,8,128]{3,2,1,0:T(8,128)} %get-tuple-element.7) | copy-start | bytes 3145732
  65.2 26.3 %all-to-all-start.2 = ((f32[128,1,2080]{2,1,0:T(1,128)}), f32[128,1,2080]{2,1,0:T(1,128)S(1)}, u32[]{:S(2)}, u32[]{:S(2)}) async-start(f32[128,1,2080]{2,1,0:T(1,128)} %copy.48), calls=%async_computation.2 | async-start | bytes 2228224 | tf_op jit(solution)/shard_map/all_to_all | solution.py:211
  94.4 8.7 %all-to-all-start.3 = ((bf16[8,4,512]{2,1,0:T(4,128)(2,1)}), bf16[8,4,512]{2,1,0:T(4,128)(2,1)S(1)}, u32[]{:S(2)}, u32[]{:S(2)}) async-start(bf16[8,4,512]{2,1,0:T(4,128)(2,1)} %broadcast_in_dim.54), calls=%async_computation.3 | async-start | bytes 65536 | tf_op jit(solution)/shard_map/all_to_all | solution.py:46
  104.2 11.3 %all-to-all-start.4 = ((f32[16,2,1024]{2,1,0:T(2,128)}), f32[16,2,1024]{2,1,0:T(2,128)S(1)}, u32[]{:S(2)}, u32[]{:S(2)}) async-start(f32[16,2,1024]{2,1,0:T(2,128)} %copy.51), calls=%async_computation.4 | async-start | bytes 262144 | tf_op jit(solution)/shard_map/all_to_all | solution.py:225

commit v8 on v7

--- a/solution.py
+++ b/solution.py
@@ -57,7 +57,7 @@
 DEPTH = 32
 UNROLL = 16
 
-def merge_kernel(seq_ref, order_ref, count_ref, q_ref, kv_hbm, acc_ref, tot_ref, max_ref, buf, sems):
+def merge_kernel(seq_ref, order_ref, count_ref, q_ref, kv_hbm, acc_ref, stats_ref, tot_ref, max_ref, buf, sems):
     scale = 1.0 / math.sqrt(HD)
     acc_ref[...] = jnp.zeros(acc_ref.shape, jnp.float32)
     tot_ref[...] = jnp.zeros(tot_ref.shape, jnp.float32)
@@ -129,6 +129,18 @@
 
     lax.fori_loop(0, padded // UNROLL, body, 0)
 
+    heads = KVH * (H // KVH)
+    diag = (lax.broadcasted_iota(jnp.int32, (heads, 128), 0)
+            == lax.broadcasted_iota(jnp.int32, (heads, 128), 1))
+
+    def emit(s, carry):
+        for i, ref in enumerate((tot_ref, max_ref)):
+            col = ref[s].reshape(heads, 128)
+            stats_ref[i, s] = jnp.sum(jnp.where(diag, col, 0.0), axis=0, keepdims=True)[:, :heads]
+        return carry
+
+    lax.fori_loop(0, stats_ref.shape[1], emit, 0)
+
 
 def merge_pages(seq_of, picked, q_all, kv):
     slots, tok, width = kv.shape
@@ -145,9 +157,12 @@
     return pl.pallas_call(
         merge_kernel,
         in_specs=[smem, smem, smem, vmem, pl.BlockSpec(memory_space=pl.ANY)],
-        out_specs=[vmem] * 3,
-        out_shape=[jax.ShapeDtypeStruct(full, jnp.float32)] * 3,
+        out_specs=[vmem] * 2,
+        out_shape=[jax.ShapeDtypeStruct(full, jnp.float32),
+                   jax.ShapeDtypeStruct((2, seqs, 1, H), jnp.float32)],
         scratch_shapes=[
+            pltpu.VMEM(full, jnp.float32),
+            pltpu.VMEM(full, jnp.float32),
             pltpu.VMEM((DEPTH, tok, 2 * HD), kv.dtype),
             pltpu.SemaphoreType.DMA((DEPTH,)),
         ],
@@ -197,10 +212,10 @@
     q_all = q_all.reshape(KVH, n_tensor // KVH, seqs, local_heads, HD)
     q_all = q_all.transpose(2, 0, 1, 3, 4).reshape(seqs, KVH, groups, HD)
 
-    loc_acc, loc_total, loc_max = merge_pages(seq_of, picked, q_all, kv_pool)
+    loc_acc, stats = merge_pages(seq_of, picked, q_all, kv_pool)
     loc_acc = loc_acc.reshape(seqs, H, HD)
-    loc_total = loc_total[..., 0].reshape(seqs, H)
-    loc_max = loc_max[..., 0].reshape(seqs, H)
+    loc_total = stats[0].reshape(seqs, H)
+    loc_max = stats[1].reshape(seqs, H)
 
     blocks = n_page * n_tensor
     def by_owner(x):

time: 117 us -> 114 us (0.974)
  local copies, waits for them, and re-layouts: 16.5 us -> 14.4 us
    slice x3 -> x2, local copies, waits for them, and re-layouts: 2.56 us -> 0.16 us  [the longest x1 0.09 us: per_device(): loc_max = stats[1].reshape(seqs, H)]
where the time goes in v8:
time: 114 us; the launch traced here: 113 us
  waiting for transfers between devices  50.3 us (44%)
  starting transfers between devices  29.7 us (26%)
  local copies, waits for them, and re-layouts  14.4 us (13%)
  Pallas kernels  8.98 us (8%)
  other arithmetic  7.31 us (6%)
  matrix products  1.66 us (1%)
    all_to_all x1, waiting for transfers between devices, per_device(): got = lax.all_to_all(packed, ('page', 'tensor'), 0, 0, tiled=True)  19.7 us
    all_to_all x3, waiting for transfers between devices, gather_blocks(): lax.all_to_all(jnp.broadcast_to(x[None], (n,) + x.shape), axis, 0, 0, til...  18.6 us
    all_to_all x3, starting transfers between devices, gather_blocks(): lax.all_to_all(jnp.broadcast_to(x[None], (n,) + x.shape), axis, 0, 0, til...  14.1 us
    pallas_call x1, Pallas kernels, merge_pages(): pl.pallas_call(merge_kernel, in_specs=[smem, smem, smem, vmem, pl.BlockSp...  8.98 us
    all_to_all x1, waiting for transfers between devices, per_device(): out = jnp.sum(lax.all_to_all(part_out, 'tensor', 0, 0, tiled=True), axis=0)  7.05 us
    all_to_all x1, starting transfers between devices, per_device(): got = lax.all_to_all(packed, ('page', 'tensor'), 0, 0, tiled=True)  6.28 us
    ppermute x3, starting transfers between devices, butterfly_sum(): x = x + lax.ppermute(x, axis, [(i, i ^ d) for i in range(n)])  5.86 us
    ppermute x3, waiting for transfers between devices, butterfly_sum(): x = x + lax.ppermute(x, axis, [(i, i ^ d) for i in range(n)])  4.94 us
  transfers between devices with their start and end apart: 8, of which 7 were waited for; matrix products, arithmetic and copies ran while one was open for 7% of the time, Pallas kernels for 0%

profile of v8, /device:TPU:0, one launch (start us, length us, event | category | flops | bytes accessed | tf_op | source)
XLA Modules:
  0.0 113.3 jit_solution(4720849577462996094)
XLA Ops:
  0.7 1.5 %broadcast_in_dim.52 = bf16[16,2,1024]{2,1,0:T(2,128)(2,1)} broadcast(bf16[2,1024]{1,0:T(2,128)(2,1)} %bitcast.80), dimensions={1,2} | broadcast | bytes 69632 | tf_op jit(solution)/shard_map/broadcast_in_dim | solution.py:46
  2.1 7.1 %all-to-all-start = ((bf16[16,2,1024]{2,1,0:T(2,128)(2,1)}), bf16[16,2,1024]{2,1,0:T(2,128)(2,1)S(1)}, u32[]{:S(2)}, u32[]{:S(2)}) async-start(bf16[16,2,1024]{2,1,0:T(2,128)(2,1)} %broadcast_in_dim.52), calls=%async_computation | async-start | bytes 131072 | tf_op jit(solution)/shard_map/all_to_all | solution.py:46
  9.3 1.1 %select_reduce_fusion = s32[64]{0:T(128)S(1)} fusion(s32[8192]{0:T(1024)} %param.12, s32[64]{0:T(128)S(1)} %iota_add_fusion), kind=kLoop, calls=%fused_computation.1 | loop fusion | flops 1572800 | bytes 33280 | tf_op jit(solution)/shard_map/reduce_sum | solution.py:191
  10.5 0.5 and_select_fusion.1
  11.0 1.5 %gather_fusion = s32[64,8,32]{2,1,0:T(8,128)S(1)} fusion(s32[32,8,32]{2,1,0:T(8,128)} %bitcast.77, s32[1024]{0:T(1024)S(1)} %pad_clamp_fusion), kind=kCustom, calls=%fused_computation | custom fusion | bytes 131328 | tf_op jit(solution)/shard_map/gather | solution.py:196
  12.5 4.4 %all-to-all-done = bf16[16,2,1024]{2,1,0:T(2,128)(2,1)S(1)} async-done(((bf16[16,2,1024]{2,1,0:T(2,128)(2,1)}), bf16[16,2,1024]{2,1,0:T(2,128)(2,1)S(1)}, u32[]{:S(2)}, u32[]{:S(2)}) %all-to-all-start) | async-done | bytes 65568 | tf_op jit(solution)/shard_map/all_to_all | solution.py:46
  17.0 1.1 fusion.17
  18.1 0.0 copy-done.1
  18.1 0.3 fusion.16
  18.4 0.1 collective-permute-start
  18.5 1.3 %compare_reduce_fusion = pred[64,8]{1,0:T(8,128)(4,1)S(1)} fusion(s32[64,8,32]{2,1,0:T(8,128)S(1)} %gather_fusion, s32[64]{0:T(128)S(1)} %get-tuple-element.16), kind=kLoop, calls=%fused_computation.10 | loop fusion | flops 32256 | bytes 66304 | tf_op jit(solution)/shard_map/reduce_or | solution.py:197
  19.8 2.0 %collective-permute-start.1 = (f32[32,640]{1,0:T(8,128)S(1)}, f32[32,640]{1,0:T(8,128)S(1)}, u32[]{:S(2)}, u32[]{:S(2)}) collective-permute-start(f32[32,640]{1,0:T(8,128)S(1)} %fusion.15), channel_id=1, source_target_pairs={{0,32},{16,48},{32,0},{48,16},{64,96},{80,112},{96,64},{112,80},{1... | collective-permute-start | bytes 245768 | tf_op jit(solution)/shard_map/ppermute | solution.py:52
  21.8 0.1 reshape.209
  21.9 0.3 reduce-window.9
  22.2 0.1 slice.40
  22.3 2.6 %collective-permute-done.1 = f32[32,640]{1,0:T(8,128)S(1)} collective-permute-done((f32[32,640]{1,0:T(8,128)S(1)}, f32[32,640]{1,0:T(8,128)S(1)}, u32[]{:S(2)}, u32[]{:S(2)}) %collective-permute-start.1) | collective-permute-done | bytes 81952 | tf_op jit(solution)/shard_map/ppermute | solution.py:52
  24.9 3.8 %collective-permute-start.2 = (f32[32,640]{1,0:T(8,128)S(1)}, f32[32,640]{1,0:T(8,128)S(1)}, u32[]{:S(2)}, u32[]{:S(2)}) collective-permute-start(f32[32,640]{1,0:T(8,128)S(1)} %add.111), channel_id=1, source_target_pairs={{0,64},{16,80},{32,96},{48,112},{64,0},{80,16},{96,32},{112,48},{1... | collective-permute-start | bytes 245768 | tf_op jit(solution)/shard_map/ppermute | solution.py:52
  28.7 0.1 fusion.13
  28.8 2.4 %collective-permute-done.2 = f32[32,640]{1,0:T(8,128)S(1)} collective-permute-done((f32[32,640]{1,0:T(8,128)S(1)}, f32[32,640]{1,0:T(8,128)S(1)}, u32[]{:S(2)}, u32[]{:S(2)}) %collective-permute-start.2) | collective-permute-done | bytes 81952 | tf_op jit(solution)/shard_map/ppermute | solution.py:52
  31.2 0.1 subtract_convert_fusion
  31.3 0.1 pad_maximum_fusion.1
  31.4 0.8 broadcast_in_dim.53
  32.2 3.6 %all-to-all-start.1 = ((bf16[16,32,512]{2,1,0:T(8,128)(2,1)}), bf16[16,32,512]{2,1,0:T(8,128)(2,1)S(1)}, u32[]{:S(2)}, u32[]{:S(2)}) async-start(bf16[16,32,512]{2,1,0:T(8,128)(2,1)} %broadcast_in_dim.53), calls=%async_computation.1 | async-start | bytes 1048576 | tf_op jit(solution)/shard_map/all_to_all | solution.py:46
  35.8 0.1 slice_reduce_fusion.3
  35.9 0.1 eq.66
  36.0 0.7 convert_reduce_fusion
  36.7 0.1 add_bitcast_fusion.1
  36.8 0.9 select_reduce_fusion.1.order_ref
  37.7 8.8 %all-to-all-done.1 = bf16[16,32,512]{2,1,0:T(8,128)(2,1)S(1)} async-done(((bf16[16,32,512]{2,1,0:T(8,128)(2,1)}), bf16[16,32,512]{2,1,0:T(8,128)(2,1)S(1)}, u32[]{:S(2)}, u32[]{:S(2)}) %all-to-all-start.1) | async-done | bytes 524320 | tf_op jit(solution)/shard_map/all_to_all | solution.py:46
  46.5 0.1 reshape.203
  46.6 1.1 copy.34
  47.7 9.0 %shard_map.86 = (f32[32,8,8,128]{3,2,1,0:T(8,128)}, f32[2,32,1,64]{3,2,1,0:T(1,128)}) custom-call(s32[64]{0:T(128)} %get-tuple-element.17.seq_ref, s32[512]{0:T(512)} %select_reduce_fusion.1.order_ref, s32[1]{0:T(128)} %bitcast.4.count_ref, bf16[32,8,8,128]{3,2,1,0:T(8,128)(2,1)} %bitcast.73, bf16[64,64,2048]{2,1,0:T(8,128)(2,1)} %kv_hbm.1), custom_call_target="tpu_custom_call" | custom-call | tf_op jit(solution)/shard_map/pallas_call | solution.py:157
  56.7 1.4 %copy.53 = f32[8,4,16,4,128]{4,3,1,2,0:T(4,128)S(1)} copy(f32[8,4,16,4,128]{4,3,2,1,0:T(4,128)} %bitcast.76) | data formatting | bytes 2097152 | tf_op jit(solution)/shard_map/reshape;reshape | solution.py:222
  58.1 0.4 reshape.205
  58.6 0.3 copy-done.2
  58.9 0.1 slice_reduce_fusion
  59.0 0.2 reshape_reshape_squeeze.7
  59.1 0.3 copy.37
  59.4 0.1 reshape.207
  59.5 0.1 copy.39
  59.6 0.2 reshape_reshape_squeeze.6
  59.8 0.3 copy.36
  60.0 0.1 reshape.206
  60.1 0.1 copy.38
  60.2 0.3 concatenate.20
  60.5 2.1 %copy.40 = f32[128,1,2080]{2,1,0:T(1,128)} copy(f32[128,1,2080]{2,0,1:T(8,128)S(1)} %bitcast.68) | data formatting | bytes 2129920 | tf_op jit(solution)/shard_map/all_to_all | solution.py:226
  62.6 6.3 %all-to-all-start.2 = ((f32[128,1,2080]{2,1,0:T(1,128)}), f32[128,1,2080]{2,1,0:T(1,128)S(1)}, u32[]{:S(2)}, u32[]{:S(2)}) async-start(f32[128,1,2080]{2,1,0:T(1,128)} %copy.40), calls=%async_computation.2 | async-start | bytes 2228224 | tf_op jit(solution)/shard_map/all_to_all | solution.py:226
  68.9 19.7 %all-to-all-done.2 = f32[128,1,2080]{2,1,0:T(1,128)S(1)} async-done(((f32[128,1,2080]{2,1,0:T(1,128)}), f32[128,1,2080]{2,1,0:T(1,128)S(1)}, u32[]{:S(2)}, u32[]{:S(2)}) %all-to-all-start.2) | async-done | bytes 1064992 | tf_op jit(solution)/shard_map/all_to_all | solution.py:226
  88.6 1.5 %copy.41 = f32[128,1,2080]{0,2,1:T(8,128)S(1)} copy(f32[128,1,2080]{2,1,0:T(1,128)S(1)} %all-to-all-done.2) | data formatting | bytes 2129920 | tf_op jit(solution)/shard_map/all_to_all | solution.py:226
  90.1 0.1 slice_reduce_fusion.2
  90.2 0.2 fusion.5
  90.4 0.4 fusion
  90.8 0.1 div.165
  90.8 0.1 broadcast_bitcast_fusion
  90.9 0.6 broadcast_in_dim.54
  91.5 3.3 %all-to-all-start.3 = ((bf16[8,4,512]{2,1,0:T(4,128)(2,1)}), bf16[8,4,512]{2,1,0:T(4,128)(2,1)S(1)}, u32[]{:S(2)}, u32[]{:S(2)}) async-start(bf16[8,4,512]{2,1,0:T(4,128)(2,1)} %broadcast_in_dim.54), calls=%async_computation.3 | async-start | bytes 65536 | tf_op jit(solution)/shard_map/all_to_all | solution.py:46
  94.9 5.4 %all-to-all-done.3 = bf16[8,4,512]{2,1,0:T(4,128)(2,1)S(1)} async-done(((bf16[8,4,512]{2,1,0:T(4,128)(2,1)}), bf16[8,4,512]{2,1,0:T(4,128)(2,1)S(1)}, u32[]{:S(2)}, u32[]{:S(2)}) %all-to-all-start.3) | async-done | bytes 32800 | tf_op jit(solution)/shard_map/all_to_all | solution.py:46
  100.3 0.3 fusion.1
  100.6 0.8 copy.43
  101.3 3.5 %all-to-all-start.4 = ((f32[16,2,1024]{2,1,0:T(2,128)}), f32[16,2,1024]{2,1,0:T(2,128)S(1)}, u32[]{:S(2)}, u32[]{:S(2)}) async-start(f32[16,2,1024]{2,1,0:T(2,128)} %copy.43), calls=%async_computation.4 | async-start | bytes 262144 | tf_op jit(solution)/shard_map/all_to_all | solution.py:240
  104.8 0.1 subtract_bitcast_fusion
  104.9 0.6 fusion.10
  105.6 7.0 %all-to-all-done.4 = f32[16,2,1024]{2,1,0:T(2,128)S(1)} async-done(((f32[16,2,1024]{2,1,0:T(2,128)}), f32[16,2,1024]{2,1,0:T(2,128)S(1)}, u32[]{:S(2)}, u32[]{:S(2)}) %all-to-all-start.4) | async-done | bytes 131104 | tf_op jit(solution)/shard_map/all_to_all | solution.py:240
  112.6 0.6 reduce_sum.65
  (23 shorter events, 0.2 us)
Async XLA Ops:
  0.6 99.6 %copy-start = (bf16[512,1024]{1,0:T(8,128)(2,1)S(1)}, bf16[512,1024]{1,0:T(8,128)(2,1)}, u32[]{:S(2)}) copy-start(bf16[512,1024]{1,0:T(8,128)(2,1)} %param.10) | copy-start | bytes 3145732
  0.6 17.5 %copy-start.1 = (bf16[1024,512]{1,0:T(8,128)(2,1)S(1)}, bf16[1024,512]{1,0:T(8,128)(2,1)}, u32[]{:S(2)}) copy-start(bf16[1024,512]{1,0:T(8,128)(2,1)} %param.8) | copy-start | bytes 3145732
  2.1 14.8 %all-to-all-start = ((bf16[16,2,1024]{2,1,0:T(2,128)(2,1)}), bf16[16,2,1024]{2,1,0:T(2,128)(2,1)S(1)}, u32[]{:S(2)}, u32[]{:S(2)}) async-start(bf16[16,2,1024]{2,1,0:T(2,128)(2,1)} %broadcast_in_dim.52), calls=%async_computation | async-start | bytes 131072 | tf_op jit(solution)/shard_map/all_to_all | solution.py:46
  18.4 1.4 %collective-permute-start = (f32[32,640]{1,0:T(8,128)S(1)}, f32[32,640]{1,0:T(8,128)S(1)}, u32[]{:S(2)}, u32[]{:S(2)}) collective-permute-start(f32[32,640]{1,0:T(8,128)S(1)} %pad_maximum_fusion), channel_id=1, source_target_pairs={{0,16},{16,0},{32,48},{48,32},{64,80},{80,64},{96,112},{112,96},{1... | collective-permute-start | bytes 245768 | tf_op jit(solution)/shard_map/ppermute | solution.py:52
  19.8 5.1 %collective-permute-start.1 = (f32[32,640]{1,0:T(8,128)S(1)}, f32[32,640]{1,0:T(8,128)S(1)}, u32[]{:S(2)}, u32[]{:S(2)}) collective-permute-start(f32[32,640]{1,0:T(8,128)S(1)} %fusion.15), channel_id=1, source_target_pairs={{0,32},{16,48},{32,0},{48,16},{64,96},{80,112},{96,64},{112,80},{1... | collective-permute-start | bytes 245768 | tf_op jit(solution)/shard_map/ppermute | solution.py:52
  24.9 6.2 %collective-permute-start.2 = (f32[32,640]{1,0:T(8,128)S(1)}, f32[32,640]{1,0:T(8,128)S(1)}, u32[]{:S(2)}, u32[]{:S(2)}) collective-permute-start(f32[32,640]{1,0:T(8,128)S(1)} %add.111), channel_id=1, source_target_pairs={{0,64},{16,80},{32,96},{48,112},{64,0},{80,16},{96,32},{112,48},{1... | collective-permute-start | bytes 245768 | tf_op jit(solution)/shard_map/ppermute | solution.py:52
  32.2 14.2 %all-to-all-start.1 = ((bf16[16,32,512]{2,1,0:T(8,128)(2,1)}), bf16[16,32,512]{2,1,0:T(8,128)(2,1)S(1)}, u32[]{:S(2)}, u32[]{:S(2)}) async-start(bf16[16,32,512]{2,1,0:T(8,128)(2,1)} %broadcast_in_dim.53), calls=%async_computation.1 | async-start | bytes 1048576 | tf_op jit(solution)/shard_map/all_to_all | solution.py:46
  58.1 0.8 copy-start.2
  62.6 26.0 %all-to-all-start.2 = ((f32[128,1,2080]{2,1,0:T(1,128)}), f32[128,1,2080]{2,1,0:T(1,128)S(1)}, u32[]{:S(2)}, u32[]{:S(2)}) async-start(f32[128,1,2080]{2,1,0:T(1,128)} %copy.40), calls=%async_computation.2 | async-start | bytes 2228224 | tf_op jit(solution)/shard_map/all_to_all | solution.py:226
  91.5 8.7 %all-to-all-start.3 = ((bf16[8,4,512]{2,1,0:T(4,128)(2,1)}), bf16[8,4,512]{2,1,0:T(4,128)(2,1)S(1)}, u32[]{:S(2)}, u32[]{:S(2)}) async-start(bf16[8,4,512]{2,1,0:T(4,128)(2,1)} %broadcast_in_dim.54), calls=%async_computation.3 | async-start | bytes 65536 | tf_op jit(solution)/shard_map/all_to_all | solution.py:46
  101.3 11.3 %all-to-all-start.4 = ((f32[16,2,1024]{2,1,0:T(2,128)}), f32[16,2,1024]{2,1,0:T(2,128)S(1)}, u32[]{:S(2)}, u32[]{:S(2)}) async-start(f32[16,2,1024]{2,1,0:T(2,128)} %copy.43), calls=%async_computation.4 | async-start | bytes 262144 | tf_op jit(solution)/shard_map/all_to_all | solution.py:240

commit v9 on v8

--- a/solution.py
+++ b/solution.py
@@ -222,11 +222,28 @@
         x = x.reshape((n_page, seq_share, n_tensor, local_heads) + x.shape[2:])
         return x.transpose((0, 2, 1, 3) + tuple(range(4, x.ndim))).reshape(blocks, -1)
     rows = seq_share * local_heads
-    packed = jnp.concatenate([by_owner(loc_acc), by_owner(loc_total), by_owner(loc_max)], axis=1)
-    got = lax.all_to_all(packed, ("page", "tensor"), 0, 0, tiled=True)
-    src_acc = got[:, :rows * HD].reshape(blocks, rows, HD)
-    src_total = got[:, rows * HD:rows * HD + rows]
-    src_max = got[:, rows * HD + rows:]
+    to_bf16 = lambda x: lax.reduce_precision(x, exponent_bits=8, mantissa_bits=7)
+    hi = to_bf16(loc_max)
+    rest = loc_max - hi
+    mid = to_bf16(rest)
+    max_hi = hi.astype(jnp.bfloat16)
+    max_mid = mid.astype(jnp.bfloat16)
+    max_lo = to_bf16(rest - mid).astype(jnp.bfloat16)
+    packed = jnp.concatenate(
+        [
+            by_owner(loc_acc.astype(jnp.bfloat16)),
+            by_owner(loc_total.astype(jnp.bfloat16)),
+            by_owner(max_hi),
+            by_owner(max_mid),
+            by_owner(max_lo),
+        ],
+        axis=1,
+    )
+    got = lax.all_to_all(packed, ("page", "tensor"), 0, 0, tiled=True).astype(jnp.float32)
+    base = rows * HD
+    src_acc = got[:, :base].reshape(blocks, rows, HD)
+    src_total = got[:, base:base + rows]
+    src_max = (got[:, base + rows:base + 2 * rows] + got[:, base + 2 * rows:base + 3 * rows]) + got[:, base + 3 * rows:]
     top_max = jnp.max(src_max, axis=0)
     rescale = jnp.exp(src_max - top_max[None])
     full_total = jnp.sum(src_total * rescale, axis=0)

time: 114 us -> 115 us (level)
  waiting for transfers between devices: 50.3 us -> 44.8 us
  other arithmetic: 7.31 us -> 9.75 us
  local copies, waits for them, and re-layouts: 14.4 us -> 15.8 us
  matrix products: 1.66 us -> 2.9 us
    all_to_all x1, waiting for transfers between devices: 19.7 us -> 14.2 us  [per_device(): lax.all_to_all(packed, ('page', 'tensor'), 0, 0, tiled=True)]
    unnamed x8 -> x6, local copies, waits for them, and re-layouts: 0.43 us -> 2.12 us
    all_to_all x2, local copies, waits for them, and re-layouts: 3.59 us -> 2.01 us  [per_device(): lax.all_to_all(packed, ('page', 'tensor'), 0, 0, tiled=True)]
    another operation x4 -> x2, local copies, waits for them, and re-layouts: 1.84 us -> 0.28 us  [the longest x1 0.17 us: per_device(): loc_max = stats[1].reshape(seqs, H)]
    convert_element_type x0 -> x2, other arithmetic: none -> 1.38 us  [the longest x1 1.3 us: per_device(): loc_acc.astype(jnp.bfloat16)]
    dot_general x1, matrix products: 0.27 us -> 1.51 us  [per_device(): part_q = jnp.dot(tok_all, w_query, preferred_element_type=jnp.float32)]
where the time goes in v9:
time: 115 us; the launch traced here: 113 us
  waiting for transfers between devices  44.8 us (39%)
  starting transfers between devices  29.6 us (26%)
  local copies, waits for them, and re-layouts  15.8 us (14%)
  other arithmetic  9.75 us (8%)
  Pallas kernels  9.26 us (8%)
  matrix products  2.9 us (3%)
    all_to_all x3, waiting for transfers between devices, gather_blocks(): lax.all_to_all(jnp.broadcast_to(x[None], (n,) + x.shape), axis, 0, 0, til...  18.6 us
    all_to_all x1, waiting for transfers between devices, per_device(): lax.all_to_all(packed, ('page', 'tensor'), 0, 0, tiled=True)  14.2 us
    all_to_all x3, starting transfers between devices, gather_blocks(): lax.all_to_all(jnp.broadcast_to(x[None], (n,) + x.shape), axis, 0, 0, til...  14.1 us
    pallas_call x1, Pallas kernels, merge_pages(): pl.pallas_call(merge_kernel, in_specs=[smem, smem, smem, vmem, pl.BlockSp...  9.26 us
    all_to_all x1, waiting for transfers between devices, per_device(): out = jnp.sum(lax.all_to_all(part_out, 'tensor', 0, 0, tiled=True), axis=0)  7.05 us
    all_to_all x1, starting transfers between devices, per_device(): lax.all_to_all(packed, ('page', 'tensor'), 0, 0, tiled=True)  6.2 us
    ppermute x3, starting transfers between devices, butterfly_sum(): x = x + lax.ppermute(x, axis, [(i, i ^ d) for i in range(n)])  5.86 us
    ppermute x3, waiting for transfers between devices, butterfly_sum(): x = x + lax.ppermute(x, axis, [(i, i ^ d) for i in range(n)])  4.94 us
  transfers between devices with their start and end apart: 8, of which 7 were waited for; matrix products, arithmetic and copies ran while one was open for 7% of the time, Pallas kernels for 0%

profile of v9, /device:TPU:0, one launch (start us, length us, event | category | flops | bytes accessed | tf_op | source)
XLA Modules:
  0.0 113.2 jit_solution(4755903544427815561)
XLA Ops:
  0.6 1.4 %broadcast_in_dim.52 = bf16[16,2,1024]{2,1,0:T(2,128)(2,1)} broadcast(bf16[2,1024]{1,0:T(2,128)(2,1)} %bitcast.91), dimensions={1,2} | broadcast | bytes 69632 | tf_op jit(solution)/shard_map/broadcast_in_dim | solution.py:46
  2.1 7.1 %all-to-all-start = ((bf16[16,2,1024]{2,1,0:T(2,128)(2,1)}), bf16[16,2,1024]{2,1,0:T(2,128)(2,1)S(1)}, u32[]{:S(2)}, u32[]{:S(2)}) async-start(bf16[16,2,1024]{2,1,0:T(2,128)(2,1)} %broadcast_in_dim.52), calls=%async_computation | async-start | bytes 131072 | tf_op jit(solution)/shard_map/all_to_all | solution.py:46
  9.2 1.1 %select_reduce_fusion = s32[64]{0:T(128)S(1)} fusion(s32[8192]{0:T(1024)} %param.12, s32[64]{0:T(128)S(1)} %iota_add_fusion), kind=kLoop, calls=%fused_computation.1 | loop fusion | flops 1572800 | bytes 33280 | tf_op jit(solution)/shard_map/reduce_sum | solution.py:191
  10.4 0.5 and_select_fusion.1
  11.0 1.5 %gather_fusion = s32[64,8,32]{2,1,0:T(8,128)S(1)} fusion(s32[32,8,32]{2,1,0:T(8,128)} %bitcast.87, s32[1024]{0:T(1024)S(1)} %pad_clamp_fusion), kind=kCustom, calls=%fused_computation | custom fusion | bytes 131328 | tf_op jit(solution)/shard_map/gather | solution.py:196
  12.5 4.4 %all-to-all-done = bf16[16,2,1024]{2,1,0:T(2,128)(2,1)S(1)} async-done(((bf16[16,2,1024]{2,1,0:T(2,128)(2,1)}), bf16[16,2,1024]{2,1,0:T(2,128)(2,1)S(1)}, u32[]{:S(2)}, u32[]{:S(2)}) %all-to-all-start) | async-done | bytes 65568 | tf_op jit(solution)/shard_map/all_to_all | solution.py:46
  16.9 1.1 fusion.24
  18.0 1.5 %fusion.23 = f32[32,512]{1,0:T(8,128)S(1)} fusion(bf16[32,1024]{1,0:T(8,128)(2,1)S(1)} %reshape.222, bf16[1024,512]{1,0:T(8,128)(2,1)} %param.8), kind=kOutput, calls=%fused_computation.73 | convolution fusion | flops 33554432 | bytes 1179648 | tf_op jit(solution)/shard_map/dot_general | solution.py:200
  19.7 1.3 %compare_reduce_fusion = pred[64,8]{1,0:T(8,128)(4,1)S(1)} fusion(s32[64,8,32]{2,1,0:T(8,128)S(1)} %gather_fusion, s32[64]{0:T(128)S(1)} %get-tuple-element.17), kind=kLoop, calls=%fused_computation.17 | loop fusion | flops 32256 | bytes 66304 | tf_op jit(solution)/shard_map/reduce_or | solution.py:197
  20.9 2.0 %collective-permute-start.1 = (f32[32,640]{1,0:T(8,128)S(1)}, f32[32,640]{1,0:T(8,128)S(1)}, u32[]{:S(2)}, u32[]{:S(2)}) collective-permute-start(f32[32,640]{1,0:T(8,128)S(1)} %fusion.22), channel_id=1, source_target_pairs={{0,32},{16,48},{32,0},{48,16},{64,96},{80,112},{96,64},{112,80},{1... | collective-permute-start | bytes 245768 | tf_op jit(solution)/shard_map/ppermute | solution.py:52
  23.0 0.3 reduce-window.9
  23.5 2.6 %collective-permute-done.1 = f32[32,640]{1,0:T(8,128)S(1)} collective-permute-done((f32[32,640]{1,0:T(8,128)S(1)}, f32[32,640]{1,0:T(8,128)S(1)}, u32[]{:S(2)}, u32[]{:S(2)}) %collective-permute-start.1) | collective-permute-done | bytes 81952 | tf_op jit(solution)/shard_map/ppermute | solution.py:52
  26.1 3.8 %collective-permute-start.2 = (f32[32,640]{1,0:T(8,128)S(1)}, f32[32,640]{1,0:T(8,128)S(1)}, u32[]{:S(2)}, u32[]{:S(2)}) collective-permute-start(f32[32,640]{1,0:T(8,128)S(1)} %add.117), channel_id=1, source_target_pairs={{0,64},{16,80},{32,96},{48,112},{64,0},{80,16},{96,32},{112,48},{1... | collective-permute-start | bytes 245768 | tf_op jit(solution)/shard_map/ppermute | solution.py:52
  29.9 2.4 %collective-permute-done.2 = f32[32,640]{1,0:T(8,128)S(1)} collective-permute-done((f32[32,640]{1,0:T(8,128)S(1)}, f32[32,640]{1,0:T(8,128)S(1)}, u32[]{:S(2)}, u32[]{:S(2)}) %collective-permute-start.2) | collective-permute-done | bytes 81952 | tf_op jit(solution)/shard_map/ppermute | solution.py:52
  32.3 0.1 subtract_convert_fusion
  32.6 0.8 broadcast_in_dim.53
  33.4 3.6 %all-to-all-start.1 = ((bf16[16,32,512]{2,1,0:T(8,128)(2,1)}), bf16[16,32,512]{2,1,0:T(8,128)(2,1)S(1)}, u32[]{:S(2)}, u32[]{:S(2)}) async-start(bf16[16,32,512]{2,1,0:T(8,128)(2,1)} %broadcast_in_dim.53), calls=%async_computation.1 | async-start | bytes 1048576 | tf_op jit(solution)/shard_map/all_to_all | solution.py:46
  37.0 0.1 slice_reduce_fusion.1
  37.1 0.1 eq.66
  37.2 0.7 convert_reduce_fusion
  38.0 0.9 select_reduce_fusion.1.order_ref
  38.8 8.8 %all-to-all-done.1 = bf16[16,32,512]{2,1,0:T(8,128)(2,1)S(1)} async-done(((bf16[16,32,512]{2,1,0:T(8,128)(2,1)}), bf16[16,32,512]{2,1,0:T(8,128)(2,1)S(1)}, u32[]{:S(2)}, u32[]{:S(2)}) %all-to-all-start.1) | async-done | bytes 524320 | tf_op jit(solution)/shard_map/all_to_all | solution.py:46
  47.6 0.1 reshape.224
  47.8 1.1 copy.46
  48.9 9.3 %shard_map.86 = (f32[32,8,8,128]{3,2,1,0:T(8,128)}, f32[2,32,1,64]{3,2,1,0:T(1,128)}) custom-call(s32[64]{0:T(128)} %get-tuple-element.18.seq_ref, s32[512]{0:T(512)} %select_reduce_fusion.1.order_ref, s32[1]{0:T(128)} %bitcast.4.count_ref, bf16[32,8,8,128]{3,2,1,0:T(8,128)(2,1)} %bitcast.84, bf16[64,64,2048]{2,1,0:T(8,128)(2,1)} %kv_hbm.1), custom_call_target="tpu_custom_call" | custom-call | tf_op jit(solution)/shard_map/pallas_call | solution.py:157
  58.1 0.8 fusion.10
  58.9 0.8 slice_reduce_fusion
  59.7 1.3 %convert_element_type.80 = bf16[32,8,8,128]{3,2,1,0:T(8,128)(2,1)S(1)} convert(f32[32,8,8,128]{3,2,1,0:T(8,128)} %get-tuple-element.4) | non-fusion elementwise | flops 262144 | bytes 1572864 | tf_op jit(solution)/shard_map/convert_element_type | solution.py:234
  61.0 0.2 copy.69
  61.2 0.4 reshape.226
  61.6 0.2 convert_element_type.82
  61.8 0.3 copy.48
  62.0 0.1 reshape.227
  62.1 0.1 copy.52
  62.3 0.2 reshape_squeeze.4
  62.5 0.3 copy.51
  62.8 0.1 reshape.230
  62.9 0.1 copy.55
  63.1 0.3 copy.50
  63.3 0.1 reshape.229
  63.4 0.1 copy.54
  63.6 0.3 copy.49
  63.8 0.1 reshape.228
  64.0 0.1 copy.53
  64.1 0.3 concatenate.20
  64.4 0.5 broadcast.321
  64.9 1.0 reduce.10
  65.9 1.4 %reshape.252 = bf16[128,2,1056]{2,1,0:T(2,128)(2,1)} reshape(bf16[128,2112]{1,0:T(8,128)(2,1)S(1)} %reduce.10) | data formatting | bytes 1081344
  67.3 6.2 %all-to-all-start.2 = ((bf16[128,2,1056]{2,1,0:T(2,128)(2,1)}), bf16[128,2,1056]{2,1,0:T(2,128)(2,1)S(1)}, u32[]{:S(2)}, u32[]{:S(2)}) async-start(bf16[128,2,1056]{2,1,0:T(2,128)(2,1)} %reshape.252), calls=%async_computation.2 | async-start | bytes 1179648 | tf_op jit(solution)/shard_map/all_to_all | solution.py:242
  73.5 14.2 %all-to-all-done.2 = bf16[128,2,1056]{2,1,0:T(2,128)(2,1)S(1)} async-done(((bf16[128,2,1056]{2,1,0:T(2,128)(2,1)}), bf16[128,2,1056]{2,1,0:T(2,128)(2,1)S(1)}, u32[]{:S(2)}, u32[]{:S(2)}) %all-to-all-start.2) | async-done | bytes 540704 | tf_op jit(solution)/shard_map/all_to_all | solution.py:242
  87.7 0.6 reshape.253
  88.4 1.5 %copy.57 = bf16[128,1,2112]{0,2,1:T(8,128)(2,1)S(1)} copy(bf16[128,1,2112]{2,1,0:T(2,128)(2,1)S(1)} %reshape.253) | data formatting | bytes 1081344 | tf_op jit(solution)/shard_map/all_to_all | solution.py:242
  90.0 0.1 fusion.21
  90.1 0.2 fusion.11
  90.3 0.4 fusion
  90.8 0.6 broadcast_in_dim.54
  91.4 3.3 %all-to-all-start.3 = ((bf16[8,4,512]{2,1,0:T(4,128)(2,1)}), bf16[8,4,512]{2,1,0:T(4,128)(2,1)S(1)}, u32[]{:S(2)}, u32[]{:S(2)}) async-start(bf16[8,4,512]{2,1,0:T(4,128)(2,1)} %broadcast_in_dim.54), calls=%async_computation.3 | async-start | bytes 65536 | tf_op jit(solution)/shard_map/all_to_all | solution.py:46
  94.8 5.4 %all-to-all-done.3 = bf16[8,4,512]{2,1,0:T(4,128)(2,1)S(1)} async-done(((bf16[8,4,512]{2,1,0:T(4,128)(2,1)}), bf16[8,4,512]{2,1,0:T(4,128)(2,1)S(1)}, u32[]{:S(2)}, u32[]{:S(2)}) %all-to-all-start.3) | async-done | bytes 32800 | tf_op jit(solution)/shard_map/all_to_all | solution.py:46
  100.2 0.3 fusion.1
  100.5 0.7 copy.59
  101.2 3.5 %all-to-all-start.4 = ((f32[16,2,1024]{2,1,0:T(2,128)}), f32[16,2,1024]{2,1,0:T(2,128)S(1)}, u32[]{:S(2)}, u32[]{:S(2)}) async-start(f32[16,2,1024]{2,1,0:T(2,128)} %copy.59), calls=%async_computation.4 | async-start | bytes 262144 | tf_op jit(solution)/shard_map/all_to_all | solution.py:257
  104.8 0.6 fusion.16
  105.5 7.0 %all-to-all-done.4 = f32[16,2,1024]{2,1,0:T(2,128)S(1)} async-done(((f32[16,2,1024]{2,1,0:T(2,128)}), f32[16,2,1024]{2,1,0:T(2,128)S(1)}, u32[]{:S(2)}, u32[]{:S(2)}) %all-to-all-start.4) | async-done | bytes 131104 | tf_op jit(solution)/shard_map/all_to_all | solution.py:257
  112.5 0.6 reduce_sum.65
  (32 shorter events, 1.1 us)
Async XLA Ops:
  0.6 99.5 %copy-start = (bf16[512,1024]{1,0:T(8,128)(2,1)S(1)}, bf16[512,1024]{1,0:T(8,128)(2,1)}, u32[]{:S(2)}) copy-start(bf16[512,1024]{1,0:T(8,128)(2,1)} %param.10) | copy-start | bytes 3145732
  2.1 14.8 %all-to-all-start = ((bf16[16,2,1024]{2,1,0:T(2,128)(2,1)}), bf16[16,2,1024]{2,1,0:T(2,128)(2,1)S(1)}, u32[]{:S(2)}, u32[]{:S(2)}) async-start(bf16[16,2,1024]{2,1,0:T(2,128)(2,1)} %broadcast_in_dim.52), calls=%async_computation | async-start | bytes 131072 | tf_op jit(solution)/shard_map/all_to_all | solution.py:46
  19.6 1.4 %collective-permute-start = (f32[32,640]{1,0:T(8,128)S(1)}, f32[32,640]{1,0:T(8,128)S(1)}, u32[]{:S(2)}, u32[]{:S(2)}) collective-permute-start(f32[32,640]{1,0:T(8,128)S(1)} %pad_maximum_fusion), channel_id=1, source_target_pairs={{0,16},{16,0},{32,48},{48,32},{64,80},{80,64},{96,112},{112,96},{1... | collective-permute-start | bytes 245768 | tf_op jit(solution)/shard_map/ppermute | solution.py:52
  20.9 5.1 %collective-permute-start.1 = (f32[32,640]{1,0:T(8,128)S(1)}, f32[32,640]{1,0:T(8,128)S(1)}, u32[]{:S(2)}, u32[]{:S(2)}) collective-permute-start(f32[32,640]{1,0:T(8,128)S(1)} %fusion.22), channel_id=1, source_target_pairs={{0,32},{16,48},{32,0},{48,16},{64,96},{80,112},{96,64},{112,80},{1... | collective-permute-start | bytes 245768 | tf_op jit(solution)/shard_map/ppermute | solution.py:52
  26.1 6.2 %collective-permute-start.2 = (f32[32,640]{1,0:T(8,128)S(1)}, f32[32,640]{1,0:T(8,128)S(1)}, u32[]{:S(2)}, u32[]{:S(2)}) collective-permute-start(f32[32,640]{1,0:T(8,128)S(1)} %add.117), channel_id=1, source_target_pairs={{0,64},{16,80},{32,96},{48,112},{64,0},{80,16},{96,32},{112,48},{1... | collective-permute-start | bytes 245768 | tf_op jit(solution)/shard_map/ppermute | solution.py:52
  33.4 14.2 %all-to-all-start.1 = ((bf16[16,32,512]{2,1,0:T(8,128)(2,1)}), bf16[16,32,512]{2,1,0:T(8,128)(2,1)S(1)}, u32[]{:S(2)}, u32[]{:S(2)}) async-start(bf16[16,32,512]{2,1,0:T(8,128)(2,1)} %broadcast_in_dim.53), calls=%async_computation.1 | async-start | bytes 1048576 | tf_op jit(solution)/shard_map/all_to_all | solution.py:46
  67.3 20.5 %all-to-all-start.2 = ((bf16[128,2,1056]{2,1,0:T(2,128)(2,1)}), bf16[128,2,1056]{2,1,0:T(2,128)(2,1)S(1)}, u32[]{:S(2)}, u32[]{:S(2)}) async-start(bf16[128,2,1056]{2,1,0:T(2,128)(2,1)} %reshape.252), calls=%async_computation.2 | async-start | bytes 1179648 | tf_op jit(solution)/shard_map/all_to_all | solution.py:242
  91.4 8.7 %all-to-all-start.3 = ((bf16[8,4,512]{2,1,0:T(4,128)(2,1)}), bf16[8,4,512]{2,1,0:T(4,128)(2,1)S(1)}, u32[]{:S(2)}, u32[]{:S(2)}) async-start(bf16[8,4,512]{2,1,0:T(4,128)(2,1)} %broadcast_in_dim.54), calls=%async_computation.3 | async-start | bytes 65536 | tf_op jit(solution)/shard_map/all_to_all | solution.py:46
  101.2 11.3 %all-to-all-start.4 = ((f32[16,2,1024]{2,1,0:T(2,128)}), f32[16,2,1024]{2,1,0:T(2,128)S(1)}, u32[]{:S(2)}, u32[]{:S(2)}) async-start(f32[16,2,1024]{2,1,0:T(2,128)} %copy.59), calls=%async_computation.4 | async-start | bytes 262144 | tf_op jit(solution)/shard_map/all_to_all | solution.py:257
